TPU v7x, 128 devices: a whole 4x4x4 slice. The times are simulated.
128 devices in a mesh: seq: 64 (over x, y, z_lo, core), row: 2 (over z_hi).
Axes of the slice: x: 4, y: 4, z: 4 (z_hi: 2, z_lo: 2; z = z_hi * 2 + z_lo), core: 2. Of those that a mesh axis runs over, the one named last changes fastest.
Arguments:
- queries: bfloat16 [2, 64, 128, 3072], P(None, 'seq', 'row'), may hold values from -9 to 9
- keys: bfloat16 [2, 64, 128, 512], P(None, 'seq', 'row'), may hold values from -9 to 9
- values: bfloat16 [2, 64, 128, 512], P(None, 'seq', 'row'), may hold values from -6 to 6
- gain: float32 [128], replicated, may hold values from 0.1 to 1.9
Outputs:
- attended: bfloat16 [2, 64, 128, 3072], P(None, 'seq', 'row')
All inputs are finite; a program needn't handle non-finite values.
Results may differ from a plain program's by a relative error of at most 0.017.
Values may be sent and summed in bfloat16 or wider, within the bound.
No kernel may reach another device: no remote copies, remote signals or barrier semaphores. Data moves between devices by JAX's collectives and lax.ppermute only.
A program may use at most 128 MiB of HBM per device.

v0:
```python
import math

import jax
import jax.numpy as jnp
from jax import lax
from jax.sharding import PartitionSpec as P

KV_HEADS = 4
GROUP = 6
HEAD_DIM = 128


lowest_score = -1e30


def attend_block(state, query_group, key_block, value_block, visible):
    running_max, running_sum, running_acc = state
    scores = jnp.einsum(
        "qgjd,kgd->qgjk", query_group, key_block, preferred_element_type=jnp.float32
    )
    scores = scores * (1.0 / math.sqrt(HEAD_DIM))
    scores = jnp.where(visible, scores, -jnp.inf)
    new_max = jnp.maximum(running_max, jnp.max(scores, axis=-1))
    raw_weights = jnp.exp(scores - new_max[..., None])
    factor = jnp.exp(running_max - new_max)
    new_sum = running_sum * factor + jnp.sum(raw_weights, axis=-1)
    weights = raw_weights.astype(jnp.bfloat16)
    new_acc = running_acc * factor[..., None] + jnp.einsum(
        "qgjk,kgd->qgjd", weights, value_block, preferred_element_type=jnp.float32
    )
    return (new_max, new_sum, new_acc)


def fold_history(queries_here, query_blocks, keys_here, values_here):
    query_count = queries_here.shape[2]
    key_rows = keys_here.shape[2]
    block_count = 2 * lax.axis_size("seq")
    grouped = queries_here.reshape(2, query_count, KV_HEADS, GROUP, HEAD_DIM)
    stat_shape = (2, query_count, KV_HEADS, GROUP)
    initial = (
        jnp.full(stat_shape, lowest_score, jnp.float32),
        jnp.zeros(stat_shape, jnp.float32),
        jnp.zeros(stat_shape + (HEAD_DIM,), jnp.float32),
    )
    key_piece = lax.all_gather(keys_here, "seq", axis=1, tiled=True)
    value_piece = lax.all_gather(values_here, "seq", axis=1, tiled=True)
    shard_count = key_piece.shape[1]
    per_step = math.gcd(shard_count, max(1, 1024 // key_rows))
    step_count = shard_count // per_step
    span_rows = per_step * key_rows
    key_blocks = key_piece.reshape(2 * step_count, span_rows, KV_HEADS, HEAD_DIM)
    value_blocks = value_piece.reshape(2 * step_count, span_rows, KV_HEADS, HEAD_DIM)
    step_ids = jnp.arange(2 * step_count, dtype=jnp.int32)
    shard_of_row = jnp.arange(span_rows, dtype=jnp.int32) // key_rows

    def visit(state, operands):
        key_block, value_block, step_id = operands
        which_half = step_id // step_count
        device_ids = step_id % step_count * per_step + shard_of_row
        key_ids = jnp.where(which_half == 0, device_ids, block_count - 1 - device_ids)
        updated = []
        for query_half in range(2):
            current = (state[0][query_half], state[1][query_half], state[2][query_half])
            visible = key_ids <= query_blocks[query_half]
            current = attend_block(current, grouped[query_half], key_block, value_block, visible)
            updated.append(current)
        new_state = (
            jnp.stack([updated[0][0], updated[1][0]]),
            jnp.stack([updated[0][1], updated[1][1]]),
            jnp.stack([updated[0][2], updated[1][2]]),
        )
        return (new_state, None)

    result_state, _ = lax.scan(visit, initial, (key_blocks, value_blocks, step_ids))
    return result_state


def per_device(queries, keys, values, gain):
    seq_index = lax.axis_index("seq")
    block_count = 2 * lax.axis_size("seq")
    query_blocks = jnp.stack([seq_index, block_count - 1 - seq_index])
    own_rows = queries.shape[2]
    keys_here, values_here = (
        lax.all_gather(keys, "row", axis=2, tiled=True),
        lax.all_gather(values, "row", axis=2, tiled=True),
    )
    running_max, running_sum, running_acc = fold_history(
        queries, query_blocks, keys_here, values_here
    )
    mixed = running_acc / running_sum[..., None]
    spread = jnp.sqrt(jnp.mean(mixed * mixed, axis=-1, keepdims=True) + 1e-06)
    normed = (mixed / spread * gain).astype(jnp.bfloat16)
    return normed.reshape(2, 1, own_rows, KV_HEADS * GROUP * HEAD_DIM)


def solution(mesh):
    return jax.shard_map(
        per_device,
        mesh=mesh,
        in_specs=(
            P(None, "seq", "row", None),
            P(None, "seq", "row", None),
            P(None, "seq", "row", None),
            P(),
        ),
        out_specs=P(None, "seq", "row", None),
        check_vma=False,
    )
```

profile of v0, /device:TPU:0, one launch (start us, length us, event | category | flops | bytes accessed | tf_op | source)
XLA Modules:
  0.0 533.7 jit_solution(8361810853024658721)
XLA Ops:
  6.5 10.0 %all_gather.12 = bf16[2,1,128,512]{3,2,1,0:T(8,128)(2,1)} all-gather(bf16[2,1,64,512]{3,2,1,0:T(8,128)(2,1)} %param.7), channel_id=1, replica_groups=mesh['seq'=64,'row'=2] {'row'}, dimensions={2}, use_global_device_ids=true | all-gather | bytes 393216 | tf_op jit(solution)/shard_map/all_gather | solution.py:84
  16.6 7.5 %all_gather.14 = bf16[2,1,128,512]{3,2,1,0:T(8,128)(2,1)} all-gather(bf16[2,1,64,512]{3,2,1,0:T(8,128)(2,1)} %param.8), channel_id=1, replica_groups=mesh['seq'=64,'row'=2] {'row'}, dimensions={2}, use_global_device_ids=true | all-gather | bytes 393216 | tf_op jit(solution)/shard_map/all_gather | solution.py:85
  24.1 2.1 reshape.97
  26.5 112.5 %all-gather.3.cloned.1.call-done = bf16[2,64,128,512]{3,2,1,0:T(8,128)(2,1)} async-done(((bf16[2,1,128,512]{3,2,1,0:T(8,128)(2,1)}), bf16[2,64,128,512]{3,2,1,0:T(8,128)(2,1)}) %all-gather.3.cloned.1.call-update) | async-done | bytes 16777232 | tf_op jit(solution)/shard_map/all_gather | solution.py:45
  138.9 23.9 %reshape.102 = bf16[16,1024,4,128]{3,2,1,0:T(4,128)(2,1)} reshape(bf16[2,64,128,512]{3,2,1,0:T(8,128)(2,1)} %all-gather.3.cloned.1.call-done) | data formatting | bytes 33554432 | tf_op jit(solution)/shard_map/reshape | solution.py:51
  162.9 98.4 %all-gather.5.cloned.1.call-done = bf16[2,64,128,512]{3,2,1,0:T(8,128)(2,1)} async-done(((bf16[2,1,128,512]{3,2,1,0:T(8,128)(2,1)}), bf16[2,64,128,512]{3,2,1,0:T(8,128)(2,1)}) %all-gather.5.cloned.1.call-update) | async-done | bytes 16777232 | tf_op jit(solution)/shard_map/all_gather | solution.py:46
  261.3 23.7 %reshape.103 = bf16[16,1024,4,128]{3,2,1,0:T(4,128)(2,1)} reshape(bf16[2,64,128,512]{3,2,1,0:T(8,128)(2,1)} %all-gather.5.cloned.1.call-done) | data formatting | bytes 33554432 | tf_op jit(solution)/shard_map/reshape | solution.py:52
  285.1 238.0 %while.17 = (s32[]{:T(128)}, f32[2,64,4,6]{1,3,2,0:T(8,128)S(1)}, f32[2,64,4,6]{1,3,2,0:T(8,128)S(1)}, f32[2,64,4,6,128]{4,1,3,2,0:T(8,128)S(1)}, s32[16]{0:T(12...) while((s32[]{:T(128)}, f32[2,64,4,6]{1,3,2,0:T(8,128)S(1)}, ...), condition=%wide.region_5.6_spmd.clone, body=%wide.region_0.5_spmd.clone.sunk | while | flops 1646427136 | bytes 53457288 | solution.py:74
  288.5 2.3 constant_dynamic-slice_fusion.3
  293.0 1.6 fusion.62
  294.6 1.8 fusion.65
  296.4 1.8 fusion.64
  298.2 1.6 fusion.63
  303.4 2.3 constant_dynamic-slice_fusion.3
  307.9 1.6 fusion.62
  309.4 1.8 fusion.65
  311.2 1.8 fusion.64
  313.1 1.6 fusion.63
  318.3 2.3 constant_dynamic-slice_fusion.3
  322.7 1.6 fusion.62
  324.3 1.8 fusion.65
  326.1 1.8 fusion.64
  327.9 1.6 fusion.63
  333.1 2.3 constant_dynamic-slice_fusion.3
  337.6 1.6 fusion.62
  339.1 1.8 fusion.65
  341.0 1.8 fusion.64
  348.0 2.3 constant_dynamic-slice_fusion.3
  354.0 1.8 fusion.65
  355.8 1.8 fusion.64
  362.8 2.3 constant_dynamic-slice_fusion.3
  368.8 1.8 fusion.65
  370.7 1.8 fusion.64
  377.7 2.3 constant_dynamic-slice_fusion.3
  383.7 1.8 fusion.65
  385.5 1.8 fusion.64
  392.5 2.3 constant_dynamic-slice_fusion.3
  398.5 1.8 fusion.65
  400.4 1.8 fusion.64
  407.4 2.4 constant_dynamic-slice_fusion.3
  413.5 1.8 fusion.65
  415.3 1.8 fusion.64
  422.3 2.3 constant_dynamic-slice_fusion.3
  428.3 1.8 fusion.65
  430.2 1.8 fusion.64
  437.2 2.3 constant_dynamic-slice_fusion.3
  443.2 1.8 fusion.65
  445.0 1.8 fusion.64
  452.0 2.3 constant_dynamic-slice_fusion.3
  458.1 1.8 fusion.65
  459.9 1.8 fusion.64
  466.9 2.3 constant_dynamic-slice_fusion.3
  473.0 1.8 fusion.65
  474.8 1.8 fusion.64
  481.8 2.3 constant_dynamic-slice_fusion.3
  487.8 1.8 fusion.65
  489.6 1.8 fusion.64
  496.6 2.3 constant_dynamic-slice_fusion.3
  502.7 1.8 fusion.65
  504.5 1.8 fusion.64
  511.5 2.3 constant_dynamic-slice_fusion.3
  517.5 1.8 fusion.65
  519.3 1.8 fusion.64
  525.1 1.7 reshape.99
  (184 shorter events, 89.9 us)
Async XLA Ops:
  6.5 132.4 %all-gather.3.cloned.1.call-start = ((), (), s32[]{:S(2)}) async-start(), calls=%async_computation | async-start | bytes 17039360 | tf_op jit(solution)/shard_map/all_gather | solution.py:45
  16.6 244.7 %all-gather.5.cloned.1.call-start = ((), (), s32[]{:S(2)}) async-start(), calls=%async_computation.1 | async-start | bytes 17039360 | tf_op jit(solution)/shard_map/all_gather | solution.py:46
  285.1 238.9 %copy-start = (f32[128]{0:T(128)S(1)}, f32[128]{0:T(128)}, u32[]{:S(2)}) copy-start(f32[128]{0:T(128)} %param.9) | copy-start | bytes 1540
Sparse Core Ops, SparseCore 0:
  16.7 122.2 all-gather.2
  140.7 120.5 all-gather.4
where the time goes:
time: 537 us; the launch traced here: 534 us
  waiting for transfers between devices  211 us (39%)
  local copies, waits for them, and re-layouts  99.3 us (18%)
  matrix products  92.8 us (17%)
  other arithmetic  54.7 us (10%)
  loops' own time  45.1 us (8%)
  blocking collectives  17.5 us (3%)
  between operations  13.5 us (3%)
    all_gather x1, waiting for transfers between devices, fold_history(): key_piece = lax.all_gather(keys_here, 'seq', axis=1, tiled=True)  112 us
    all_gather x1, waiting for transfers between devices, fold_history(): value_piece = lax.all_gather(values_here, 'seq', axis=1, tiled=True)  98.4 us
    dot_general x32, matrix products, attend_block(): jnp.einsum('qgjk,kgd->qgjd', weights, value_block, preferred_element_type...  58.2 us
    reduce_sum x32, other arithmetic, attend_block(): new_sum = running_sum * factor + jnp.sum(raw_weights, axis=-1)  49.6 us
    dynamic_slice x32, local copies, waits for them, and re-layouts, fold_history(): lax.scan(visit, initial, (key_blocks, value_blocks, step_ids))  46.8 us
    another operation x1, loops' own time, fold_history(): lax.scan(visit, initial, (key_blocks, value_blocks, step_ids))  45.1 us
    dot_general x32, matrix products, attend_block(): jnp.einsum('qgjd,kgd->qgjk', query_group, key_block, preferred_element_ty...  34.5 us
    reshape x1, local copies, waits for them, and re-layouts, fold_history(): key_piece.reshape(2 * step_count, span_rows, KV_HEADS, HEAD_DIM)  23.9 us
  transfers between devices with their start and end apart: 2, of which 2 were waited for; matrix products, arithmetic and copies ran while one was open for 5% of the time, Pallas kernels for 0%

commit v1 on v0

v1 whole, which is shorter than its diff:
```python
import functools
import math

import jax
import jax.numpy as jnp
from jax import lax
from jax.experimental import pallas as pl
from jax.experimental.pallas import tpu as pltpu
from jax.sharding import PartitionSpec as P

KV_HEADS = 4
GROUP = 6
HEAD_DIM = 128
TILE_BLOCKS = 8

lowest_score = -1e30


def attend_kernel(bounds_ref, q_ref, k_ref, v_ref, gain_ref, *rest, rows, finalize, carry_in):
    if carry_in:
        m_in, l_in, acc_in = rest[:3]
        rest = rest[3:]
    if finalize:
        o_ref = rest[0]
        rest = rest[1:]
    else:
        m_out, l_out, acc_out = rest[:3]
        rest = rest[3:]
    q_sc, m_sc, l_sc, acc_sc = rest

    t = pl.program_id(1)
    last = pl.num_programs(1) - 1
    lo = bounds_ref[0]
    hi = bounds_ref[1]
    tile = lo // TILE_BLOCKS + t
    block_rows = k_ref.shape[1]

    @pl.when(t == 0)
    def _init():
        q_sc[...] = jnp.concatenate(
            [q_ref[:, j * HEAD_DIM:(j + 1) * HEAD_DIM] for j in range(GROUP)], axis=0
        )
        if carry_in:
            m_sc[...] = m_in[0]
            l_sc[...] = l_in[0]
            acc_sc[...] = acc_in[0]
        else:
            m_sc[...] = jnp.full(m_sc.shape, lowest_score, jnp.float32)
            l_sc[...] = jnp.zeros(l_sc.shape, jnp.float32)
            acc_sc[...] = jnp.zeros(acc_sc.shape, jnp.float32)

    @pl.when(tile <= hi // TILE_BLOCKS)
    def _step():
        keys = k_ref[...].reshape(TILE_BLOCKS * block_rows, HEAD_DIM)
        vals = v_ref[...].reshape(TILE_BLOCKS * block_rows, HEAD_DIM)
        scores = lax.dot_general(
            q_sc[...], keys, (((1,), (1,)), ((), ())), preferred_element_type=jnp.float32
        )
        scores = scores * (1.0 / math.sqrt(HEAD_DIM))
        key_block = tile * TILE_BLOCKS + lax.broadcasted_iota(jnp.int32, scores.shape, 1) // block_rows
        visible = (key_block >= lo) & (key_block <= hi)
        scores = jnp.where(visible, scores, -jnp.inf)
        running_max = m_sc[...]
        new_max = jnp.maximum(running_max, jnp.max(scores, axis=1, keepdims=True))
        raw_weights = jnp.exp(scores - new_max)
        factor = jnp.exp(running_max - new_max)
        l_sc[...] = l_sc[...] * factor + jnp.sum(raw_weights, axis=1, keepdims=True)
        acc_sc[...] = acc_sc[...] * factor + jnp.dot(
            raw_weights.astype(jnp.bfloat16), vals, preferred_element_type=jnp.float32
        )
        m_sc[...] = new_max

    @pl.when(t == last)
    def _done():
        if finalize:
            mixed = acc_sc[...] / l_sc[...]
            spread = jnp.sqrt(jnp.mean(mixed * mixed, axis=1, keepdims=True) + 1e-06)
            normed = (mixed / spread * gain_ref[...]).astype(o_ref.dtype)
            for j in range(GROUP):
                o_ref[:, j * HEAD_DIM:(j + 1) * HEAD_DIM] = normed[j * rows:(j + 1) * rows]
        else:
            m_out[0] = m_sc[...]
            l_out[0] = l_sc[...]
            acc_out[0] = acc_sc[...]


def attend(bounds, q, kv, gain, state=None, finalize=True):
    rows = q.shape[0]
    n_blocks, block_rows, _ = kv.shape
    n_tiles = n_blocks // TILE_BLOCKS
    qrows = rows * GROUP

    def tile_of(t, b):
        return jnp.minimum(b[0] // TILE_BLOCKS + t, b[1] // TILE_BLOCKS)

    in_specs = [
        pl.BlockSpec((rows, GROUP * HEAD_DIM), lambda g, t, b: (0, g)),
        pl.BlockSpec((TILE_BLOCKS, block_rows, HEAD_DIM), lambda g, t, b: (tile_of(t, b), 0, g)),
        pl.BlockSpec(
            (TILE_BLOCKS, block_rows, HEAD_DIM), lambda g, t, b: (tile_of(t, b), 0, KV_HEADS + g)
        ),
        pl.BlockSpec((1, HEAD_DIM), lambda g, t, b: (0, 0)),
    ]
    operands = [q, kv, kv, gain.reshape(1, HEAD_DIM)]
    state_specs = [
        pl.BlockSpec((1, qrows, 1), lambda g, t, b: (g, 0, 0)),
        pl.BlockSpec((1, qrows, 1), lambda g, t, b: (g, 0, 0)),
        pl.BlockSpec((1, qrows, HEAD_DIM), lambda g, t, b: (g, 0, 0)),
    ]
    state_shapes = [
        jax.ShapeDtypeStruct((KV_HEADS, qrows, 1), jnp.float32),
        jax.ShapeDtypeStruct((KV_HEADS, qrows, 1), jnp.float32),
        jax.ShapeDtypeStruct((KV_HEADS, qrows, HEAD_DIM), jnp.float32),
    ]
    if state is not None:
        in_specs += state_specs
        operands += list(state)
    if finalize:
        out_specs = pl.BlockSpec((rows, GROUP * HEAD_DIM), lambda g, t, b: (0, g))
        out_shape = jax.ShapeDtypeStruct((rows, KV_HEADS * GROUP * HEAD_DIM), jnp.bfloat16)
    else:
        out_specs = state_specs
        out_shape = state_shapes
    kernel = functools.partial(
        attend_kernel, rows=rows, finalize=finalize, carry_in=state is not None
    )
    tile_flops = 4 * qrows * TILE_BLOCKS * block_rows * HEAD_DIM
    cost = pl.CostEstimate(
        flops=KV_HEADS * n_tiles * tile_flops,
        transcendentals=KV_HEADS * n_tiles * qrows * TILE_BLOCKS * block_rows,
        bytes_accessed=kv.size * 2 + q.size * 4,
    )
    return pl.pallas_call(
        kernel,
        grid_spec=pltpu.PrefetchScalarGridSpec(
            num_scalar_prefetch=1,
            grid=(KV_HEADS, n_tiles),
            in_specs=in_specs,
            out_specs=out_specs,
            scratch_shapes=[
                pltpu.VMEM((qrows, HEAD_DIM), jnp.bfloat16),
                pltpu.VMEM((qrows, 1), jnp.float32),
                pltpu.VMEM((qrows, 1), jnp.float32),
                pltpu.VMEM((qrows, HEAD_DIM), jnp.float32),
            ],
        ),
        out_shape=out_shape,
        compiler_params=pltpu.CompilerParams(
            dimension_semantics=("arbitrary", "arbitrary"),
        ),
        cost_estimate=cost,
    )(bounds, *operands)


def per_device(queries, keys, values, gain):
    seq_index = lax.axis_index("seq")
    last_index = lax.axis_size("seq") - 1
    own_rows = queries.shape[2]
    pair = jnp.concatenate([keys, values], axis=-1)
    pair = lax.all_gather(pair, "row", axis=2, tiled=True)
    low_blocks = lax.all_gather(pair[0, 0], "seq", axis=0, tiled=True)
    low_blocks = low_blocks.reshape(-1, pair.shape[2], pair.shape[3])
    high_blocks = lax.all_gather(pair[1, 0], "seq", axis=0, tiled=True)
    high_blocks = high_blocks.reshape(-1, pair.shape[2], pair.shape[3])
    zero = jnp.int32(0)
    top = jnp.int32(last_index)
    early = attend(jnp.stack([zero, seq_index]), queries[0, 0], low_blocks, gain)
    state = attend(
        jnp.stack([zero, top]), queries[1, 0], low_blocks, gain, finalize=False
    )
    late = attend(jnp.stack([seq_index, top]), queries[1, 0], high_blocks, gain, state=state)
    return jnp.stack([early, late]).reshape(2, 1, own_rows, KV_HEADS * GROUP * HEAD_DIM)


def solution(mesh):
    return jax.shard_map(
        per_device,
        mesh=mesh,
        in_specs=(
            P(None, "seq", "row", None),
            P(None, "seq", "row", None),
            P(None, "seq", "row", None),
            P(),
        ),
        out_specs=P(None, "seq", "row", None),
        check_vma=False,
    )
```

time: 537 us -> 317 us (0.59)
  local copies, waits for them, and re-layouts: 99.3 us -> 2.91 us
  Pallas kernels: 0 us -> 92.9 us
  matrix products: 92.8 us -> 0 us
  other arithmetic: 54.7 us -> 4.77 us
  loops' own time: 45.1 us -> 0 us
  waiting for transfers between devices: 211 us -> 190 us
  blocking collectives: 17.5 us -> 11 us
    pallas_call x0 -> x3, Pallas kernels: none -> 92.9 us  [attend(): pl.pallas_call(kernel, grid_spec=pltpu.PrefetchScalarGridSpec(num_scalar_...]
    dot_general x64 -> x0, matrix products: 92.8 us -> none  [the longest x32 58.2 us: attend_block(): jnp.einsum('qgjk,kgd->qgjd', weights, value_block, preferred_element_type...]
    reshape x4 -> x0, local copies, waits for them, and re-layouts: 51.4 us -> none  [the longest x1 23.9 us: fold_history(): key_piece.reshape(2 * step_count, span_rows, KV_HEADS, HEAD_DIM)]
    reduce_sum x33 -> x0, other arithmetic: 50.5 us -> none  [the longest x32 49.6 us: attend_block(): new_sum = running_sum * factor + jnp.sum(raw_weights, axis=-1)]
    dynamic_slice x32 -> x0, local copies, waits for them, and re-layouts: 46.8 us -> none  [fold_history(): lax.scan(visit, initial, (key_blocks, value_blocks, step_ids))]
    another operation x1 -> x0, loops' own time: 45.1 us -> none  [fold_history(): lax.scan(visit, initial, (key_blocks, value_blocks, step_ids))]
    all_gather x2, waiting for transfers between devices: 211 us -> 190 us  [the longest x1 119 us: per_device(): low_blocks = lax.all_gather(pair[0, 0], 'seq', axis=0, tiled=True)]
    all_gather x2 -> x1, blocking collectives: 17.5 us -> 11 us  [per_device(): pair = lax.all_gather(pair, 'row', axis=2, tiled=True)]
  transfers between devices with their start and end apart: 2 -> 2, of which waited for: 2 -> 2; matrix products, arithmetic and copies ran while one was open for 5% -> 1% of each run, Pallas kernels for 0% -> 17%
where the time goes in v1:
time: 317 us; the launch traced here: 315 us
  waiting for transfers between devices  190 us (60%)
  Pallas kernels  92.9 us (29%)
  between operations  13.4 us (4%)
  blocking collectives  11 us (3%)
  other arithmetic  4.77 us (2%)
    all_gather x1, waiting for transfers between devices, per_device(): low_blocks = lax.all_gather(pair[0, 0], 'seq', axis=0, tiled=True)  119 us
    pallas_call x3, Pallas kernels, attend(): pl.pallas_call(kernel, grid_spec=pltpu.PrefetchScalarGridSpec(num_scalar_...  92.9 us
    all_gather x1, waiting for transfers between devices, per_device(): high_blocks = lax.all_gather(pair[1, 0], 'seq', axis=0, tiled=True)  70.5 us
    all_gather x1, blocking collectives, per_device(): pair = lax.all_gather(pair, 'row', axis=2, tiled=True)  11 us
  transfers between devices with their start and end apart: 2, of which 2 were waited for; matrix products, arithmetic and copies ran while one was open for 1% of the time, Pallas kernels for 17%

profile of v1, /device:TPU:0, one launch (start us, length us, event | category | flops | bytes accessed | tf_op | source)
XLA Modules:
  0.0 315.2 jit_solution(5896997612974553499)
XLA Ops:
  6.5 0.0 all-gather.5.cloned.1.call-start
  6.5 1.0 pad_maximum_fusion
  7.5 11.0 %all_gather.9 = bf16[2,1,128,1024]{3,2,1,0:T(8,128)(2,1)S(1)} all-gather(bf16[2,1,64,1024]{3,2,1,0:T(8,128)(2,1)S(1)} %pad_maximum_fusion), channel_id=1, replica_groups=mesh['seq'=64,'row'=2] {'row'}, dimensions={2}, use_global_device_ids=true | all-gather | bytes 786432 | tf_op jit(solution)/shard_map/all_gather | solution.py:160
  18.5 0.8 fusion
  19.3 0.0 all-gather.5.cloned.1.call-update
  19.4 0.0 all-gather.7.cloned.1.call-start
  19.4 0.7 all-gather.7.cloned.1.call-update
  20.1 0.6 iota_multiply_fusion.bounds_ref
  20.7 0.6 pad_add_fusion.bounds_ref
  21.3 0.7 pad_add_fusion.1.bounds_ref
  22.0 2.1 slice_bitcast_fusion.1
  24.0 119.1 %all-gather.5.cloned.1.call-done = bf16[1,1,8192,1024]{3,2,1,0:T(8,128)(2,1)} async-done(((bf16[1,1,128,1024]{3,2,1,0:T(8,128)(2,1)}), bf16[1,1,8192,1024]{3,2,1,0:T(8,128)(2,1)}) %all-gather.5.cloned.1.call-update) | async-done | bytes 16777232 | tf_op jit(solution)/shard_map/all_gather | solution.py:161
  143.1 13.1 %shard_map.46 = bf16[64,3072]{1,0:T(8,128)(2,1)} custom-call(s32[2]{0:T(128)} %pad_add_fusion.bounds_ref, bf16[64,3072]{1,0:T(8,128)(2,1)} %get-tuple-element.11.q_ref, bf16[64,128,1024]{2,1,0:T(8,128)(2,1)} %bitcast.14, bf16[64,128,1024]{2,1,0:T(8,128)(2,1)} %bitcast.15, f32[1,128]{1,0:T(1,128)} %bitcast.22), custom_call_target="tpu_custom_call" | custom-call | flops 6442450944 | bytes 17563648 | tf_op jit(solution)/shard_map/pallas_call | solution.py:133
  156.2 39.0 %shard_map.47 = (f32[4,384,1]{2,1,0:T(8,128)}, f32[4,384,1]{2,1,0:T(8,128)}, f32[4,384,128]{2,1,0:T(8,128)}) custom-call(s32[2]{0:T(128)} %iota_multiply_fusion.bounds_ref, bf16[64,3072]{1,0:T(8,128)(2,1)} %get-tuple-element.12.q_ref, bf16[64,128,1024]{2,1,0:T(8,128)(2,1)} %bitcast.16, bf16[64,128,1024]{2,1,0:T(8,128)(2,1)} %bitcast.17, f32[1,128]{1,0:T(1,128)} %bitcast.23), custom_call_target="tpu_custom_call" | custom-call | flops 6442450944 | bytes 17563648 | tf_op jit(solution)/shard_map/pallas_call | solution.py:133
  195.2 70.5 %all-gather.7.cloned.1.call-done = bf16[1,1,8192,1024]{3,2,1,0:T(8,128)(2,1)} async-done(((bf16[1,1,128,1024]{3,2,1,0:T(8,128)(2,1)}), bf16[1,1,8192,1024]{3,2,1,0:T(8,128)(2,1)}) %all-gather.7.cloned.1.call-update) | async-done | bytes 16777232 | tf_op jit(solution)/shard_map/all_gather | solution.py:163
  265.7 0.0 copy-start
  265.7 40.8 %shard_map.48 = bf16[64,3072]{1,0:T(8,128)(2,1)} custom-call(s32[2]{0:T(128)} %pad_add_fusion.1.bounds_ref, bf16[64,3072]{1,0:T(8,128)(2,1)} %get-tuple-element.12.q_ref, bf16[64,128,1024]{2,1,0:T(8,128)(2,1)} %bitcast.18, bf16[64,128,1024]{2,1,0:T(8,128)(2,1)} %bitcast.19, f32[1,128]{1,0:T(1,128)} %bitcast.24, f32[4,384,1]{2,1,0:T(8,128)} %get-tuple-element.8.rest_0_, ...), custom_call_target="tpu_custom_call" | custom-call | flops 6442450944 | bytes 17563648 | tf_op jit(solution)/shard_map/pallas_call | solution.py:133
  306.5 0.0 copy-done
  306.5 1.9 maximum_bitcast_fusion
Async XLA Ops:
  6.5 136.6 %all-gather.5.cloned.1.call-start = ((), (), s32[]{:S(2)}) async-start(), calls=%async_computation | async-start | bytes 17039360 | tf_op jit(solution)/shard_map/all_gather | solution.py:161
  19.4 246.3 %all-gather.7.cloned.1.call-start = ((), (), s32[]{:S(2)}) async-start(), calls=%async_computation.1 | async-start | bytes 17039360 | tf_op jit(solution)/shard_map/all_gather | solution.py:163
  265.7 40.8 %copy-start = (bf16[64,3072]{1,0:T(8,128)(2,1)S(1)}, bf16[64,3072]{1,0:T(8,128)(2,1)}, u32[]{:S(2)}) copy-start(bf16[64,3072]{1,0:T(8,128)(2,1)} %shard_map.46) | copy-start | bytes 1179652
Sparse Core Ops, SparseCore 0:
  19.5 123.5 all-gather.4
  144.8 120.8 all-gather.6

commit v2 on v1

v2 whole, which is shorter than its diff:
```python
import functools
import math

import jax
import jax.numpy as jnp
from jax import lax
from jax.experimental import pallas as pl
from jax.experimental.pallas import tpu as pltpu
from jax.sharding import PartitionSpec as P

KV_HEADS = 4
GROUP = 6
HEAD_DIM = 128
TILE_KEYS = 1024

lowest_score = -1e30


def attend_kernel(bounds_ref, q_ref, k_ref, v_ref, *rest, carry_in):
    if carry_in:
        m_in, l_in, acc_in = rest[:3]
        rest = rest[3:]
    m_out, l_out, acc_out = rest[:3]
    q_sc, m_sc, l_sc, acc_sc = rest[3:]

    t = pl.program_id(1)
    last = pl.num_programs(1) - 1
    tile_blocks, block_rows, _ = k_ref.shape
    lo = bounds_ref[0]
    hi = bounds_ref[1]
    tile = lo // tile_blocks + t
    first_block = tile * tile_blocks

    @pl.when(t == 0)
    def _init():
        q_sc[...] = jnp.concatenate(
            [q_ref[:, j * HEAD_DIM:(j + 1) * HEAD_DIM] for j in range(GROUP)], axis=0
        )
        if carry_in:
            m_sc[...] = m_in[0]
            l_sc[...] = l_in[0]
            acc_sc[...] = acc_in[0]
        else:
            m_sc[...] = jnp.full(m_sc.shape, lowest_score, jnp.float32)
            l_sc[...] = jnp.zeros(l_sc.shape, jnp.float32)
            acc_sc[...] = jnp.zeros(acc_sc.shape, jnp.float32)

    def step(masked):
        keys = k_ref[...].reshape(tile_blocks * block_rows, HEAD_DIM)
        vals = v_ref[...].reshape(tile_blocks * block_rows, HEAD_DIM)
        scores = lax.dot_general(
            q_sc[...], keys, (((1,), (1,)), ((), ())), preferred_element_type=jnp.float32
        )
        scores = scores * (1.0 / math.sqrt(HEAD_DIM))
        if masked:
            key_block = first_block + lax.broadcasted_iota(jnp.int32, scores.shape, 1) // block_rows
            visible = (key_block >= lo) & (key_block <= hi)
            scores = jnp.where(visible, scores, -jnp.inf)
        running_max = m_sc[...]
        new_max = jnp.maximum(running_max, jnp.max(scores, axis=1, keepdims=True))
        raw_weights = jnp.exp(scores - new_max)
        factor = jnp.exp(running_max - new_max)
        l_sc[...] = l_sc[...] * factor + jnp.sum(raw_weights, axis=1, keepdims=True)
        acc_sc[...] = acc_sc[...] * factor + jnp.dot(
            raw_weights.astype(jnp.bfloat16), vals, preferred_element_type=jnp.float32
        )
        m_sc[...] = new_max

    active = tile <= hi // tile_blocks
    edge = (first_block < lo) | (first_block + tile_blocks - 1 > hi)

    @pl.when(active & edge)
    def _edge_step():
        step(True)

    @pl.when(active & jnp.logical_not(edge))
    def _inner_step():
        step(False)

    @pl.when(t == last)
    def _done():
        m_out[0] = m_sc[...]
        l_out[0] = l_sc[...]
        acc_out[0] = acc_sc[...]


def attend(bounds, q, kv, state=None):
    rows = q.shape[0]
    n_blocks, block_rows, _ = kv.shape
    tile_blocks = TILE_KEYS // block_rows
    n_tiles = n_blocks // tile_blocks
    qrows = rows * GROUP

    def tile_of(t, b):
        return jnp.minimum(b[0] // tile_blocks + t, b[1] // tile_blocks)

    in_specs = [
        pl.BlockSpec((rows, GROUP * HEAD_DIM), lambda g, t, b: (0, g)),
        pl.BlockSpec((tile_blocks, block_rows, HEAD_DIM), lambda g, t, b: (tile_of(t, b), 0, g)),
        pl.BlockSpec(
            (tile_blocks, block_rows, HEAD_DIM), lambda g, t, b: (tile_of(t, b), 0, KV_HEADS + g)
        ),
    ]
    operands = [q, kv, kv]
    state_specs = [
        pl.BlockSpec((1, qrows, 1), lambda g, t, b: (g, 0, 0)),
        pl.BlockSpec((1, qrows, 1), lambda g, t, b: (g, 0, 0)),
        pl.BlockSpec((1, qrows, HEAD_DIM), lambda g, t, b: (g, 0, 0)),
    ]
    state_shapes = [
        jax.ShapeDtypeStruct((KV_HEADS, qrows, 1), jnp.float32),
        jax.ShapeDtypeStruct((KV_HEADS, qrows, 1), jnp.float32),
        jax.ShapeDtypeStruct((KV_HEADS, qrows, HEAD_DIM), jnp.float32),
    ]
    if state is not None:
        in_specs += state_specs
        operands += list(state)
    kernel = functools.partial(attend_kernel, carry_in=state is not None)
    tile_flops = 4 * qrows * TILE_KEYS * HEAD_DIM
    cost = pl.CostEstimate(
        flops=KV_HEADS * n_tiles * tile_flops,
        transcendentals=KV_HEADS * n_tiles * qrows * TILE_KEYS,
        bytes_accessed=kv.size * 2 + q.size * 2 + KV_HEADS * qrows * HEAD_DIM * 8,
    )
    return pl.pallas_call(
        kernel,
        grid_spec=pltpu.PrefetchScalarGridSpec(
            num_scalar_prefetch=1,
            grid=(KV_HEADS, n_tiles),
            in_specs=in_specs,
            out_specs=state_specs,
            scratch_shapes=[
                pltpu.VMEM((qrows, HEAD_DIM), jnp.bfloat16),
                pltpu.VMEM((qrows, 1), jnp.float32),
                pltpu.VMEM((qrows, 1), jnp.float32),
                pltpu.VMEM((qrows, HEAD_DIM), jnp.float32),
            ],
        ),
        out_shape=state_shapes,
        compiler_params=pltpu.CompilerParams(
            dimension_semantics=("arbitrary", "arbitrary"),
        ),
        cost_estimate=cost,
    )(bounds, *operands)


def split_halves(state, own_rows):
    mine, theirs = [], []
    for part in state:
        shaped = part.reshape(KV_HEADS, GROUP, 2, own_rows, part.shape[-1])
        mine.append(shaped[:, :, 0])
        theirs.append(shaped[:, :, 1])
    return mine, theirs


def finish(mine, theirs, gain):
    own_max, own_sum, own_acc = mine
    far_max, far_sum, far_acc = theirs
    top = jnp.maximum(own_max, far_max)
    own_factor = jnp.exp(own_max - top)
    far_factor = jnp.exp(far_max - top)
    total = own_sum * own_factor + far_sum * far_factor
    acc = own_acc * own_factor + far_acc * far_factor
    mixed = acc / total
    spread = jnp.sqrt(jnp.mean(mixed * mixed, axis=-1, keepdims=True) + 1e-06)
    normed = (mixed / spread * gain).astype(jnp.bfloat16)
    rows = normed.shape[2]
    return normed.transpose(2, 0, 1, 3).reshape(rows, KV_HEADS * GROUP * HEAD_DIM)


def per_device(queries, keys, values, gain):
    seq_index = lax.axis_index("seq")
    last_index = lax.axis_size("seq") - 1
    own_rows = queries.shape[2]
    swap = [(0, 1), (1, 0)]
    partner_queries = lax.ppermute(queries, "row", swap)
    both_queries = jnp.concatenate([queries, partner_queries], axis=2)
    pair = jnp.concatenate([keys, values], axis=-1)
    low_blocks = lax.all_gather(pair[0, 0], "seq", axis=0, tiled=True)
    low_blocks = low_blocks.reshape(-1, own_rows, pair.shape[3])
    high_blocks = lax.all_gather(pair[1, 0], "seq", axis=0, tiled=True)
    high_blocks = high_blocks.reshape(-1, own_rows, pair.shape[3])
    zero = jnp.int32(0)
    top = jnp.int32(last_index)

    early = attend(jnp.stack([zero, seq_index]), both_queries[0, 0], low_blocks)
    early_mine, early_theirs = split_halves(early, own_rows)
    early_back = [lax.ppermute(x, "row", swap) for x in early_theirs]

    state = attend(jnp.stack([zero, top]), both_queries[1, 0], low_blocks)
    late = attend(jnp.stack([seq_index, top]), both_queries[1, 0], high_blocks, state=state)
    late_mine, late_theirs = split_halves(late, own_rows)
    late_back = [lax.ppermute(x, "row", swap) for x in late_theirs]

    early_out = finish(early_mine, early_back, gain)
    late_out = finish(late_mine, late_back, gain)
    return jnp.stack([early_out, late_out]).reshape(2, 1, own_rows, KV_HEADS * GROUP * HEAD_DIM)


def solution(mesh):
    return jax.shard_map(
        per_device,
        mesh=mesh,
        in_specs=(
            P(None, "seq", "row", None),
            P(None, "seq", "row", None),
            P(None, "seq", "row", None),
            P(),
        ),
        out_specs=P(None, "seq", "row", None),
        check_vma=False,
    )
```

time: 317 us -> 325 us (1.025)
  waiting for transfers between devices: 190 us -> 158 us
  Pallas kernels: 92.9 us -> 113 us
  starting transfers between devices: 0.04 us -> 17.4 us
  blocking collectives: 11 us -> 0 us
  other arithmetic: 4.77 us -> 15.4 us
  local copies, waits for them, and re-layouts: 2.91 us -> 6.95 us
    ppermute x0 -> x7, waiting for transfers between devices: none -> 38.9 us  [the longest x1 23.4 us: per_device(): partner_queries = lax.ppermute(queries, 'row', swap)]
    all_gather x1, waiting for transfers between devices: 119 us -> 81.7 us  [per_device(): low_blocks = lax.all_gather(pair[0, 0], 'seq', axis=0, tiled=True)]
    all_gather x1, waiting for transfers between devices: 70.5 us -> 36.8 us  [per_device(): high_blocks = lax.all_gather(pair[1, 0], 'seq', axis=0, tiled=True)]
    pallas_call x3, Pallas kernels: 92.9 us -> 113 us  [attend(): pl.pallas_call(kernel, grid_spec=pltpu.PrefetchScalarGridSpec(num_scalar_...]
    ppermute x0 -> x7, starting transfers between devices: none -> 17.3 us  [the longest x3 6.97 us: per_device(): late_back = [lax.ppermute(x, 'row', swap) for x in late_theirs]]
    all_gather x1 -> x0, blocking collectives: 11 us -> none  [per_device(): pair = lax.all_gather(pair, 'row', axis=2, tiled=True)]
    pallas_call x0 -> x4, other arithmetic: none -> 6.43 us  [attend(): pl.pallas_call(kernel, grid_spec=pltpu.PrefetchScalarGridSpec(num_scalar_...]
  transfers between devices with their start and end apart: 2 -> 9, of which waited for: 2 -> 5; matrix products, arithmetic and copies ran while one was open for 1% -> 4% of each run, Pallas kernels for 17% -> 35%
where the time goes in v2:
time: 325 us; the launch traced here: 324 us
  waiting for transfers between devices  158 us (49%)
  Pallas kernels  113 us (35%)
  starting transfers between devices  17.4 us (5%)
  other arithmetic  15.4 us (5%)
  between operations  13.7 us (4%)
  local copies, waits for them, and re-layouts  6.95 us (2%)
    pallas_call x3, Pallas kernels, attend(): pl.pallas_call(kernel, grid_spec=pltpu.PrefetchScalarGridSpec(num_scalar_...  113 us
    all_gather x1, waiting for transfers between devices, per_device(): low_blocks = lax.all_gather(pair[0, 0], 'seq', axis=0, tiled=True)  81.7 us
    all_gather x1, waiting for transfers between devices, per_device(): high_blocks = lax.all_gather(pair[1, 0], 'seq', axis=0, tiled=True)  36.8 us
    ppermute x1, waiting for transfers between devices, per_device(): partner_queries = lax.ppermute(queries, 'row', swap)  23.4 us
    ppermute x3, waiting for transfers between devices, per_device(): late_back = [lax.ppermute(x, 'row', swap) for x in late_theirs]  15.5 us
    ppermute x3, starting transfers between devices, per_device(): late_back = [lax.ppermute(x, 'row', swap) for x in late_theirs]  6.97 us
  transfers between devices with their start and end apart: 9, of which 5 were waited for; matrix products, arithmetic and copies ran while one was open for 4% of the time, Pallas kernels for 35%

profile of v2, /device:TPU:0, one launch (start us, length us, event | category | flops | bytes accessed | tf_op | source)
XLA Modules:
  0.0 324.3 jit_solution(9960372035124909734)
XLA Ops:
  6.5 0.0 copy-start.3
  6.5 0.0 all-gather.5.cloned.1.call-start
  6.5 1.0 constant_dynamic-update-slice_fusion.3
  7.5 0.9 constant_dynamic-update-slice_fusion.2
  8.4 0.7 fusion.24
  9.2 0.0 all-gather.5.cloned.1.call-update
  9.2 0.0 all-gather.7.cloned.1.call-start
  9.3 0.7 all-gather.7.cloned.1.call-update
  10.0 4.1 %collective-permute-start = (bf16[2,1,64,3072]{3,2,1,0:T(8,128)(2,1)}, bf16[2,1,64,3072]{3,2,1,0:T(8,128)(2,1)S(1)}, u32[]{:S(2)}, u32[]{:S(2)}) collective-permute-start(bf16[2,1,64,3072]{3,2,1,0:T(8,128)(2,1)} %param.4), channel_id=1, source_target_pairs={{0,1},{1,0},{2,3},{3,2},{4,5},{5,4},{6,7},{7,6},{8,9},{9,8},{10,11... | collective-permute-start | bytes 2359304 | tf_op jit(solution)/shard_map/ppermute | solution.py:176
  14.0 0.6 iota_multiply_fusion.bounds_ref
  14.6 0.6 pad_add_fusion.bounds_ref
  15.2 0.6 pad_add_fusion.1.bounds_ref
  15.8 0.0 copy-done.3
  15.8 0.1 constant_dynamic-update-slice_fusion.1
  15.9 23.4 %collective-permute-done = bf16[2,1,64,3072]{3,2,1,0:T(8,128)(2,1)S(1)} collective-permute-done((bf16[2,1,64,3072]{3,2,1,0:T(8,128)(2,1)}, bf16[2,1,64,3072]{3,2,1,0:T(8,128)(2,1)S(1)}, u32[]{:S(2)}, u32[]{:S(2)}) %collective-permute-start) | collective-permute-done | bytes 786464 | tf_op jit(solution)/shard_map/ppermute | solution.py:176
  39.2 0.1 constant_dynamic-update-slice_fusion
  39.3 1.3 slice_bitcast_fusion.5
  40.5 81.7 %all-gather.5.cloned.1.call-done = bf16[1,1,4096,1024]{3,2,1,0:T(8,128)(2,1)} async-done(((bf16[1,1,64,1024]{3,2,1,0:T(8,128)(2,1)}), bf16[1,1,4096,1024]{3,2,1,0:T(8,128)(2,1)}) %all-gather.5.cloned.1.call-update) | async-done | bytes 8388624 | tf_op jit(solution)/shard_map/all_gather | solution.py:179
  122.3 19.3 %shard_map.46 = (f32[4,768,1]{2,1,0:T(8,128)}, f32[4,768,1]{2,1,0:T(8,128)}, f32[4,768,128]{2,1,0:T(8,128)}) custom-call(s32[2]{0:T(128)} %pad_add_fusion.bounds_ref, bf16[128,3072]{1,0:T(8,128)(2,1)} %get-tuple-element.29.q_ref, bf16[64,64,1024]{2,1,0:T(8,128)(2,1)} %bitcast.121, bf16[64,64,1024]{2,1,0:T(8,128)(2,1)} %bitcast.122), custom_call_target="tpu_custom_call" | custom-call | flops 6442450944 | bytes 12320768 | tf_op jit(solution)/shard_map/pallas_call | solution.py:125
  141.6 0.0 copy-start.2
  141.6 0.0 copy-start
  141.6 2.1 reduce.1
  143.7 0.1 reshape.47
  143.8 2.7 collective-permute-start.3
  146.5 0.0 copy-done.2
  146.5 0.5 reduce
  147.0 0.1 reshape.46
  147.1 1.0 collective-permute-start.1
  148.1 0.0 copy-done
  148.1 1.0 slice_bitcast_fusion.3
  149.1 2.6 collective-permute-start.2
  151.7 46.3 %shard_map.47 = (f32[4,768,1]{2,1,0:T(8,128)}, f32[4,768,1]{2,1,0:T(8,128)}, f32[4,768,128]{2,1,0:T(8,128)}) custom-call(s32[2]{0:T(128)} %iota_multiply_fusion.bounds_ref, bf16[128,3072]{1,0:T(8,128)(2,1)} %get-tuple-element.30.q_ref, bf16[64,64,1024]{2,1,0:T(8,128)(2,1)} %bitcast.123, bf16[64,64,1024]{2,1,0:T(8,128)(2,1)} %bitcast.124), custom_call_target="tpu_custom_call" | custom-call | flops 6442450944 | bytes 12320768 | tf_op jit(solution)/shard_map/pallas_call | solution.py:125
  198.0 36.8 %all-gather.7.cloned.1.call-done = bf16[1,1,4096,1024]{3,2,1,0:T(8,128)(2,1)} async-done(((bf16[1,1,64,1024]{3,2,1,0:T(8,128)(2,1)}), bf16[1,1,4096,1024]{3,2,1,0:T(8,128)(2,1)}) %all-gather.7.cloned.1.call-update) | async-done | bytes 8388624 | tf_op jit(solution)/shard_map/all_gather | solution.py:181
  234.7 47.1 %shard_map.48 = (f32[4,768,1]{2,1,0:T(8,128)}, f32[4,768,1]{2,1,0:T(8,128)}, f32[4,768,128]{2,1,0:T(8,128)}) custom-call(s32[2]{0:T(128)} %pad_add_fusion.1.bounds_ref, bf16[128,3072]{1,0:T(8,128)(2,1)} %get-tuple-element.30.q_ref, bf16[64,64,1024]{2,1,0:T(8,128)(2,1)} %bitcast.125, bf16[64,64,1024]{2,1,0:T(8,128)(2,1)} %bitcast.126, ...), custom_call_target="tpu_custom_call" | custom-call | flops 6442450944 | bytes 12320768 | tf_op jit(solution)/shard_map/pallas_call | solution.py:125
  281.8 0.0 copy-start.1
  281.8 2.0 reduce.3
  283.8 0.1 reshape.51
  284.0 3.1 collective-permute-start.6
  287.0 1.9 reduce.2
  288.9 0.1 reshape.50
  289.0 0.6 collective-permute-start.4
  289.7 0.0 copy-done.1
  289.7 0.1 slice_bitcast_fusion
  289.7 0.0 collective-permute-done.3
  289.7 3.3 %collective-permute-start.5 = (f32[4,6,64,128]{3,2,1,0:T(8,128)S(1)}, f32[4,6,64,128]{3,2,1,0:T(8,128)S(1)}, u32[]{:S(2)}, u32[]{:S(2)}) collective-permute-start(f32[4,6,64,128]{3,2,1,0:T(8,128)S(1)} %slice_bitcast_fusion), channel_id=1, source_target_pairs={{0,1},{1,0},{2,3},{3,2},{4,5},{5,4},{6,7},{7,6},{8,9},{9,8},{10,11... | collective-permute-start | bytes 2359304 | tf_op jit(solution)/shard_map/ppermute | solution.py:193
  293.0 0.0 collective-permute-done.1
  293.1 0.0 collective-permute-done.6
  293.1 1.4 collective-permute-done.4
  294.6 0.0 copy-start.4
  294.6 0.0 collective-permute-done.2
  294.6 2.0 multiply_reduce_fusion.1
  296.7 14.2 %collective-permute-done.5 = f32[4,6,64,128]{3,2,1,0:T(8,128)S(1)} collective-permute-done((f32[4,6,64,128]{3,2,1,0:T(8,128)S(1)}, f32[4,6,64,128]{3,2,1,0:T(8,128)S(1)}, u32[]{:S(2)}, u32[]{:S(2)}) %collective-permute-start.5) | collective-permute-done | bytes 786464 | tf_op jit(solution)/shard_map/ppermute | solution.py:193
  310.9 1.0 multiply_reduce_fusion
  312.0 0.0 copy-done.4
  312.0 3.0 fusion.4
  315.0 0.3 copy.125
  315.3 0.4 stack_reshape.7
  315.7 0.3 copy.110
  316.0 0.4 stack_reshape.6
  316.5 0.9 maximum_bitcast_fusion
  (20 shorter events, 0.2 us)
Async XLA Ops:
  6.5 9.3 %copy-start.3 = (bf16[2,1,64,3072]{3,2,1,0:T(8,128)(2,1)S(1)}, bf16[2,1,64,3072]{3,2,1,0:T(8,128)(2,1)}, u32[]{:S(2)}) copy-start(bf16[2,1,64,3072]{3,2,1,0:T(8,128)(2,1)} %param.4) | copy-start | bytes 2359300
  6.5 115.8 %all-gather.5.cloned.1.call-start = ((), (), s32[]{:S(2)}) async-start(), calls=%async_computation | async-start | bytes 8519680 | tf_op jit(solution)/shard_map/all_gather | solution.py:179
  9.2 225.5 %all-gather.7.cloned.1.call-start = ((), (), s32[]{:S(2)}) async-start(), calls=%async_computation.1 | async-start | bytes 8519680 | tf_op jit(solution)/shard_map/all_gather | solution.py:181
  10.0 29.3 %collective-permute-start = (bf16[2,1,64,3072]{3,2,1,0:T(8,128)(2,1)}, bf16[2,1,64,3072]{3,2,1,0:T(8,128)(2,1)S(1)}, u32[]{:S(2)}, u32[]{:S(2)}) collective-permute-start(bf16[2,1,64,3072]{3,2,1,0:T(8,128)(2,1)} %param.4), channel_id=1, source_target_pairs={{0,1},{1,0},{2,3},{3,2},{4,5},{5,4},{6,7},{7,6},{8,9},{9,8},{10,11... | collective-permute-start | bytes 2359304 | tf_op jit(solution)/shard_map/ppermute | solution.py:176
  141.6 4.9 %copy-start.2 = (f32[4,768,1]{2,1,0:T(8,128)S(1)}, f32[4,768,1]{2,1,0:T(8,128)}, u32[]{:S(2)}) copy-start(f32[4,768,1]{2,1,0:T(8,128)} %get-tuple-element.15) | copy-start | bytes 36868
  141.6 6.5 %copy-start = (f32[4,768,128]{2,1,0:T(8,128)S(1)}, f32[4,768,128]{2,1,0:T(8,128)}, u32[]{:S(2)}) copy-start(f32[4,768,128]{2,1,0:T(8,128)} %get-tuple-element.14) | copy-start | bytes 4718596
  143.8 145.9 %collective-permute-start.3 = (f32[4,6,64,1]{2,3,1,0:T(1,128)S(1)}, f32[4,6,64,1]{2,3,1,0:T(1,128)S(1)}, u32[]{:S(2)}, u32[]{:S(2)}) collective-permute-start(f32[4,6,64,1]{2,3,1,0:T(1,128)S(1)} %slice_bitcast_fusion.10), channel_id=1, source_target_pairs={{0,1},{1,0},{2,3},{3,2},{4,5},{5,4},{6,7},{7,6},{8,9},{9,8},{10,11... | collective-permute-start | bytes 18440 | tf_op jit(solution)/shard_map/ppermute | solution.py:188
  147.1 145.9 %collective-permute-start.1 = (f32[4,6,64,1]{2,3,1,0:T(1,128)S(1)}, f32[4,6,64,1]{2,3,1,0:T(1,128)S(1)}, u32[]{:S(2)}, u32[]{:S(2)}) collective-permute-start(f32[4,6,64,1]{2,3,1,0:T(1,128)S(1)} %slice_bitcast_fusion.12), channel_id=1, source_target_pairs={{0,1},{1,0},{2,3},{3,2},{4,5},{5,4},{6,7},{7,6},{8,9},{9,8},{10,11... | collective-permute-start | bytes 18440 | tf_op jit(solution)/shard_map/ppermute | solution.py:188
  149.1 145.6 %collective-permute-start.2 = (f32[4,6,64,128]{3,2,1,0:T(8,128)}, f32[4,6,64,128]{3,2,1,0:T(8,128)}, u32[]{:S(2)}, u32[]{:S(2)}) collective-permute-start(f32[4,6,64,128]{3,2,1,0:T(8,128)} %slice_bitcast_fusion.3), channel_id=1, source_target_pairs={{0,1},{1,0},{2,3},{3,2},{4,5},{5,4},{6,7},{7,6},{8,9},{9,8},{10,11... | collective-permute-start | bytes 2359304 | tf_op jit(solution)/shard_map/ppermute | solution.py:188
  281.8 7.8 %copy-start.1 = (f32[4,768,128]{2,1,0:T(8,128)S(1)}, f32[4,768,128]{2,1,0:T(8,128)}, u32[]{:S(2)}) copy-start(f32[4,768,128]{2,1,0:T(8,128)} %get-tuple-element.20) | copy-start | bytes 4718596
  284.0 9.1 %collective-permute-start.6 = (f32[4,6,64,1]{2,3,1,0:T(1,128)S(1)}, f32[4,6,64,1]{2,3,1,0:T(1,128)S(1)}, u32[]{:S(2)}, u32[]{:S(2)}) collective-permute-start(f32[4,6,64,1]{2,3,1,0:T(1,128)S(1)} %slice_bitcast_fusion.6), channel_id=1, source_target_pairs={{0,1},{1,0},{2,3},{3,2},{4,5},{5,4},{6,7},{7,6},{8,9},{9,8},{10,11... | collective-permute-start | bytes 18440 | tf_op jit(solution)/shard_map/ppermute | solution.py:193
  289.0 5.4 %collective-permute-start.4 = (f32[4,6,64,1]{2,3,1,0:T(1,128)S(1)}, f32[4,6,64,1]{2,3,1,0:T(1,128)S(1)}, u32[]{:S(2)}, u32[]{:S(2)}) collective-permute-start(f32[4,6,64,1]{2,3,1,0:T(1,128)S(1)} %slice_bitcast_fusion.8), channel_id=1, source_target_pairs={{0,1},{1,0},{2,3},{3,2},{4,5},{5,4},{6,7},{7,6},{8,9},{9,8},{10,11... | collective-permute-start | bytes 18440 | tf_op jit(solution)/shard_map/ppermute | solution.py:193
  289.7 21.1 %collective-permute-start.5 = (f32[4,6,64,128]{3,2,1,0:T(8,128)S(1)}, f32[4,6,64,128]{3,2,1,0:T(8,128)S(1)}, u32[]{:S(2)}, u32[]{:S(2)}) collective-permute-start(f32[4,6,64,128]{3,2,1,0:T(8,128)S(1)} %slice_bitcast_fusion), channel_id=1, source_target_pairs={{0,1},{1,0},{2,3},{3,2},{4,5},{5,4},{6,7},{7,6},{8,9},{9,8},{10,11... | collective-permute-start | bytes 2359304 | tf_op jit(solution)/shard_map/ppermute | solution.py:193
  294.6 17.3 %copy-start.4 = (f32[128]{0:T(128)S(1)}, f32[128]{0:T(128)}, u32[]{:S(2)}) copy-start(f32[128]{0:T(128)} %param.7) | copy-start | bytes 1540
Sparse Core Ops, SparseCore 0:
  9.3 112.9 all-gather.4
  124.0 110.6 all-gather.6

commit v3 on v2

--- a/solution.py
+++ b/solution.py
@@ -48,23 +48,29 @@
     def step(masked):
         keys = k_ref[...].reshape(tile_blocks * block_rows, HEAD_DIM)
         vals = v_ref[...].reshape(tile_blocks * block_rows, HEAD_DIM)
+        half = q_sc.shape[0] // 2
+        for part in range(2):
+            rows_here = pl.ds(part * half, half)
+            half_step(masked, keys, vals, rows_here)
+
+    def half_step(masked, keys, vals, rows_here):
         scores = lax.dot_general(
-            q_sc[...], keys, (((1,), (1,)), ((), ())), preferred_element_type=jnp.float32
+            q_sc[rows_here], keys, (((1,), (1,)), ((), ())), preferred_element_type=jnp.float32
         )
         scores = scores * (1.0 / math.sqrt(HEAD_DIM))
         if masked:
             key_block = first_block + lax.broadcasted_iota(jnp.int32, scores.shape, 1) // block_rows
             visible = (key_block >= lo) & (key_block <= hi)
             scores = jnp.where(visible, scores, -jnp.inf)
-        running_max = m_sc[...]
+        running_max = m_sc[rows_here]
         new_max = jnp.maximum(running_max, jnp.max(scores, axis=1, keepdims=True))
         raw_weights = jnp.exp(scores - new_max)
         factor = jnp.exp(running_max - new_max)
-        l_sc[...] = l_sc[...] * factor + jnp.sum(raw_weights, axis=1, keepdims=True)
-        acc_sc[...] = acc_sc[...] * factor + jnp.dot(
+        l_sc[rows_here] = l_sc[rows_here] * factor + jnp.sum(raw_weights, axis=1, keepdims=True)
+        acc_sc[rows_here] = acc_sc[rows_here] * factor + jnp.dot(
             raw_weights.astype(jnp.bfloat16), vals, preferred_element_type=jnp.float32
         )
-        m_sc[...] = new_max
+        m_sc[rows_here] = new_max
 
     active = tile <= hi // tile_blocks
     edge = (first_block < lo) | (first_block + tile_blocks - 1 > hi)
@@ -84,9 +90,9 @@
         acc_out[0] = acc_sc[...]
 
 
-def attend(bounds, q, kv, state=None):
+def attend(bounds, q, kv, half, state=None):
     rows = q.shape[0]
-    n_blocks, block_rows, _ = kv.shape
+    _, n_blocks, block_rows, _ = kv.shape
     tile_blocks = TILE_KEYS // block_rows
     n_tiles = n_blocks // tile_blocks
     qrows = rows * GROUP
@@ -96,9 +102,13 @@
 
     in_specs = [
         pl.BlockSpec((rows, GROUP * HEAD_DIM), lambda g, t, b: (0, g)),
-        pl.BlockSpec((tile_blocks, block_rows, HEAD_DIM), lambda g, t, b: (tile_of(t, b), 0, g)),
         pl.BlockSpec(
-            (tile_blocks, block_rows, HEAD_DIM), lambda g, t, b: (tile_of(t, b), 0, KV_HEADS + g)
+            (None, tile_blocks, block_rows, HEAD_DIM),
+            lambda g, t, b: (half, tile_of(t, b), 0, g),
+        ),
+        pl.BlockSpec(
+            (None, tile_blocks, block_rows, HEAD_DIM),
+            lambda g, t, b: (half, tile_of(t, b), 0, KV_HEADS + g),
         ),
     ]
     operands = [q, kv, kv]
@@ -120,7 +130,7 @@
     cost = pl.CostEstimate(
         flops=KV_HEADS * n_tiles * tile_flops,
         transcendentals=KV_HEADS * n_tiles * qrows * TILE_KEYS,
-        bytes_accessed=kv.size * 2 + q.size * 2 + KV_HEADS * qrows * HEAD_DIM * 8,
+        bytes_accessed=kv.size + q.size * 2 + KV_HEADS * qrows * HEAD_DIM * 8,
     )
     return pl.pallas_call(
         kernel,
@@ -176,19 +186,16 @@
     partner_queries = lax.ppermute(queries, "row", swap)
     both_queries = jnp.concatenate([queries, partner_queries], axis=2)
     pair = jnp.concatenate([keys, values], axis=-1)
-    low_blocks = lax.all_gather(pair[0, 0], "seq", axis=0, tiled=True)
-    low_blocks = low_blocks.reshape(-1, own_rows, pair.shape[3])
-    high_blocks = lax.all_gather(pair[1, 0], "seq", axis=0, tiled=True)
-    high_blocks = high_blocks.reshape(-1, own_rows, pair.shape[3])
+    blocks = lax.all_gather(pair[:, 0], "seq", axis=1, tiled=False)
     zero = jnp.int32(0)
     top = jnp.int32(last_index)
 
-    early = attend(jnp.stack([zero, seq_index]), both_queries[0, 0], low_blocks)
+    early = attend(jnp.stack([zero, seq_index]), both_queries[0, 0], blocks, 0)
     early_mine, early_theirs = split_halves(early, own_rows)
     early_back = [lax.ppermute(x, "row", swap) for x in early_theirs]
 
-    state = attend(jnp.stack([zero, top]), both_queries[1, 0], low_blocks)
-    late = attend(jnp.stack([seq_index, top]), both_queries[1, 0], high_blocks, state=state)
+    state = attend(jnp.stack([zero, top]), both_queries[1, 0], blocks, 0)
+    late = attend(jnp.stack([seq_index, top]), both_queries[1, 0], blocks, 1, state=state)
     late_mine, late_theirs = split_halves(late, own_rows)
     late_back = [lax.ppermute(x, "row", swap) for x in late_theirs]
 

time: 325 us -> 282 us (0.87); the launches traced: 324 us -> 277 us
  Pallas kernels: 113 us -> 90 us
  waiting for transfers between devices: 158 us -> 136 us
    pallas_call x3, Pallas kernels: 113 us -> 90 us  [attend(): pl.pallas_call(kernel, grid_spec=pltpu.PrefetchScalarGridSpec(num_scalar_...]
    all_gather x2 -> x1, waiting for transfers between devices: 119 us -> 96.7 us  [per_device(): blocks = lax.all_gather(pair[:, 0], 'seq', axis=1, tiled=False)]
    ppermute x3, waiting for transfers between devices: 15.5 us -> 0.01 us  [per_device(): late_back = [lax.ppermute(x, 'row', swap) for x in late_theirs]]
    ppermute x3, waiting for transfers between devices: 0.01 us -> 14.9 us  [per_device(): early_back = [lax.ppermute(x, 'row', swap) for x in early_theirs]]
  transfers between devices with their start and end apart: 9 -> 8, of which waited for: 5 -> 4; matrix products, arithmetic and copies ran while one was open for 4% -> 4% of each run, Pallas kernels for 35% -> 6%
where the time goes in v3:
time: 282 us; the launch traced here: 277 us
  waiting for transfers between devices  136 us (48%)
  Pallas kernels  90 us (32%)
  other arithmetic  16.5 us (6%)
  starting transfers between devices  15.1 us (5%)
  between operations  13.7 us (5%)
  local copies, waits for them, and re-layouts  5.43 us (2%)
    all_gather x1, waiting for transfers between devices, per_device(): blocks = lax.all_gather(pair[:, 0], 'seq', axis=1, tiled=False)  96.7 us
    pallas_call x3, Pallas kernels, attend(): pl.pallas_call(kernel, grid_spec=pltpu.PrefetchScalarGridSpec(num_scalar_...  90 us
    ppermute x1, waiting for transfers between devices, per_device(): partner_queries = lax.ppermute(queries, 'row', swap)  24.6 us
    ppermute x3, waiting for transfers between devices, per_device(): early_back = [lax.ppermute(x, 'row', swap) for x in early_theirs]  14.9 us
    pallas_call x4, other arithmetic, attend(): pl.pallas_call(kernel, grid_spec=pltpu.PrefetchScalarGridSpec(num_scalar_...  6.41 us
    ppermute x3, starting transfers between devices, per_device(): early_back = [lax.ppermute(x, 'row', swap) for x in early_theirs]  6.22 us
  transfers between devices with their start and end apart: 8, of which 4 were waited for; matrix products, arithmetic and copies ran while one was open for 4% of the time, Pallas kernels for 6%

profile of v3, /device:TPU:0, one launch (start us, length us, event | category | flops | bytes accessed | tf_op | source)
XLA Modules:
  0.0 276.9 jit_solution(14504500626977482335)
XLA Ops:
  6.5 0.0 all-gather.2.cloned.1.call-start
  6.5 1.7 pad_maximum_fusion
  8.2 0.0 all-gather.2.cloned.1.call-update
  8.2 4.1 %collective-permute-start = (bf16[2,1,64,3072]{3,2,1,0:T(8,128)(2,1)}, bf16[2,1,64,3072]{3,2,1,0:T(8,128)(2,1)S(1)}, u32[]{:S(2)}, u32[]{:S(2)}) collective-permute-start(bf16[2,1,64,3072]{3,2,1,0:T(8,128)(2,1)} %param.4), channel_id=1, source_target_pairs={{0,1},{1,0},{2,3},{3,2},{4,5},{5,4},{6,7},{7,6},{8,9},{9,8},{10,11... | collective-permute-start | bytes 2359304 | tf_op jit(solution)/shard_map/ppermute | solution.py:186
  12.3 0.6 iota_multiply_fusion.bounds_ref
  12.9 0.7 pad_add_fusion
  13.5 1.2 constant_dynamic-update-slice_fusion.1
  14.7 24.6 %collective-permute-done = bf16[2,1,64,3072]{3,2,1,0:T(8,128)(2,1)S(1)} collective-permute-done((bf16[2,1,64,3072]{3,2,1,0:T(8,128)(2,1)}, bf16[2,1,64,3072]{3,2,1,0:T(8,128)(2,1)S(1)}, u32[]{:S(2)}, u32[]{:S(2)}) %collective-permute-start) | collective-permute-done | bytes 786464 | tf_op jit(solution)/shard_map/ppermute | solution.py:186
  39.3 0.1 constant_dynamic-update-slice_fusion
  39.4 1.2 slice_bitcast_fusion.5
  40.6 96.7 %all-gather.2.cloned.1.call-done.k_ref.v_ref = bf16[2,64,64,1024]{3,2,1,0:T(8,128)(2,1)} async-done(((bf16[2,1,64,1024]{3,2,1,0:T(8,128)(2,1)}), bf16[2,64,64,1024]{3,2,1,0:T(8,128)(2,1)}) %all-gather.2.cloned.1.call-update) | async-done | bytes 16777232 | tf_op jit(solution)/shard_map/all_gather | solution.py:189
  137.3 36.4 %shard_map.47 = (f32[4,768,1]{2,1,0:T(8,128)}, f32[4,768,1]{2,1,0:T(8,128)}, f32[4,768,128]{2,1,0:T(8,128)}) custom-call(s32[2]{0:T(128)} %iota_multiply_fusion.bounds_ref, bf16[128,3072]{1,0:T(8,128)(2,1)} %get-tuple-element.30.q_ref, bf16[2,64,64,1024]{3,2,1,0:T(8,128)(2,1)} %all-gather.2.cloned.1.call-done.k_ref.v_ref, ...), custom_call_target="tpu_custom_call" | custom-call | flops 6442450944 | bytes 12320768 | tf_op jit(solution)/shard_map/pallas_call | solution.py:135
  173.7 37.2 %shard_map.48 = (f32[4,768,1]{2,1,0:T(8,128)}, f32[4,768,1]{2,1,0:T(8,128)}, f32[4,768,128]{2,1,0:T(8,128)}) custom-call(s32[2]{0:T(128)} %get-tuple-element.34.bounds_ref, bf16[128,3072]{1,0:T(8,128)(2,1)} %get-tuple-element.30.q_ref, bf16[2,64,64,1024]{3,2,1,0:T(8,128)(2,1)} %all-gather.2.cloned.1.call-done.k_ref.v_ref, ...), custom_call_target="tpu_custom_call" | custom-call | flops 6442450944 | bytes 12320768 | tf_op jit(solution)/shard_map/pallas_call | solution.py:135
  210.9 0.0 copy-start.2
  210.9 0.0 copy-start
  210.9 2.0 reduce.2
  213.0 0.1 reshape.42
  213.1 1.2 collective-permute-start.4
  214.2 0.0 copy-done.2
  214.2 0.5 reduce.3
  214.7 0.1 reshape.43
  214.8 2.5 collective-permute-start.6
  217.4 0.0 copy-done
  217.4 1.0 slice_bitcast_fusion
  218.4 1.1 collective-permute-start.5
  219.4 16.4 %shard_map.46 = (f32[4,768,1]{2,1,0:T(8,128)}, f32[4,768,1]{2,1,0:T(8,128)}, f32[4,768,128]{2,1,0:T(8,128)}) custom-call(s32[2]{0:T(128)} %get-tuple-element.33.bounds_ref, bf16[128,3072]{1,0:T(8,128)(2,1)} %get-tuple-element.29.q_ref, bf16[2,64,64,1024]{3,2,1,0:T(8,128)(2,1)} %all-gather.2.cloned.1.call-done.k_ref.v_ref, ...), custom_call_target="tpu_custom_call" | custom-call | flops 6442450944 | bytes 12320768 | tf_op jit(solution)/shard_map/pallas_call | solution.py:135
  235.8 0.0 copy-start.1
  235.8 2.0 reduce
  237.8 0.1 reshape.39
  238.0 2.5 collective-permute-start.1
  240.5 1.9 reduce.1
  242.4 0.1 reshape.40
  242.5 1.2 collective-permute-start.3
  243.7 0.0 copy-done.1
  243.7 0.1 slice_bitcast_fusion.3
  243.7 0.0 collective-permute-done.4
  243.7 2.5 collective-permute-start.2
  246.3 0.0 collective-permute-done.6
  246.4 0.0 collective-permute-done.1
  246.4 1.5 collective-permute-done.3
  248.0 0.0 copy-start.3
  248.1 0.0 collective-permute-done.5
  248.1 2.0 multiply_reduce_fusion
  250.2 13.4 %collective-permute-done.2 = f32[4,6,64,128]{3,2,1,0:T(8,128)S(1)} collective-permute-done((f32[4,6,64,128]{3,2,1,0:T(8,128)S(1)}, f32[4,6,64,128]{3,2,1,0:T(8,128)S(1)}, u32[]{:S(2)}, u32[]{:S(2)}) %collective-permute-start.2) | collective-permute-done | bytes 786464 | tf_op jit(solution)/shard_map/ppermute | solution.py:195
  263.5 1.0 multiply_reduce_fusion.1
  264.6 0.0 copy-done.3
  264.6 3.0 %fusion.4 = (bf16[64,4,6,128]{3,0,2,1:T(8,128)(2,1)S(1)}, bf16[64,4,6,128]{3,0,2,1:T(8,128)(2,1)S(1)}) fusion(f32[128]{0:T(128)S(1)} %copy-done.3, f32[4,6,64]{2,1,0:T(8,128)S(1)} %copy.109, f32[4,6,64,128]{3,2,1,0:T(8,128)S(1)} %collective-permute-done.2, f32[4,6,64]{2,1,0:T(8,128)S(1)} %copy.102, f32[4,6,64]{2,1,0:T(8,128)S(1)} %copy.99, ...), kind=kLoop, calls=%fused_computation.15 | loop fusion | flops 2359296 | bytes 3969536 | tf_op jit(solution)/shard_map/transpose | solution.py:178
  267.7 0.3 copy.110
  268.0 0.4 stack_reshape.6
  268.4 0.3 copy.125
  268.7 0.4 stack_reshape.7
  269.1 0.9 maximum_bitcast_fusion
  (22 shorter events, 0.2 us)
Async XLA Ops:
  6.5 130.8 %all-gather.2.cloned.1.call-start = ((), (), s32[]{:S(2)}) async-start(), calls=%async_computation | async-start | bytes 17039360 | tf_op jit(solution)/shard_map/all_gather | solution.py:189
  8.2 31.1 %collective-permute-start = (bf16[2,1,64,3072]{3,2,1,0:T(8,128)(2,1)}, bf16[2,1,64,3072]{3,2,1,0:T(8,128)(2,1)S(1)}, u32[]{:S(2)}, u32[]{:S(2)}) collective-permute-start(bf16[2,1,64,3072]{3,2,1,0:T(8,128)(2,1)} %param.4), channel_id=1, source_target_pairs={{0,1},{1,0},{2,3},{3,2},{4,5},{5,4},{6,7},{7,6},{8,9},{9,8},{10,11... | collective-permute-start | bytes 2359304 | tf_op jit(solution)/shard_map/ppermute | solution.py:186
  210.9 3.3 %copy-start.2 = (f32[4,768,1]{2,1,0:T(8,128)S(1)}, f32[4,768,1]{2,1,0:T(8,128)}, u32[]{:S(2)}) copy-start(f32[4,768,1]{2,1,0:T(8,128)} %get-tuple-element.22) | copy-start | bytes 36868
  210.9 6.5 %copy-start = (f32[4,768,128]{2,1,0:T(8,128)S(1)}, f32[4,768,128]{2,1,0:T(8,128)}, u32[]{:S(2)}) copy-start(f32[4,768,128]{2,1,0:T(8,128)} %get-tuple-element.20) | copy-start | bytes 4718596
  213.1 30.6 %collective-permute-start.4 = (f32[4,6,64,1]{2,3,1,0:T(1,128)S(1)}, f32[4,6,64,1]{2,3,1,0:T(1,128)S(1)}, u32[]{:S(2)}, u32[]{:S(2)}) collective-permute-start(f32[4,6,64,1]{2,3,1,0:T(1,128)S(1)} %slice_bitcast_fusion.8), channel_id=1, source_target_pairs={{0,1},{1,0},{2,3},{3,2},{4,5},{5,4},{6,7},{7,6},{8,9},{9,8},{10,11... | collective-permute-start | bytes 18440 | tf_op jit(solution)/shard_map/ppermute | solution.py:200
  214.8 31.4 %collective-permute-start.6 = (f32[4,6,64,1]{2,3,1,0:T(1,128)S(1)}, f32[4,6,64,1]{2,3,1,0:T(1,128)S(1)}, u32[]{:S(2)}, u32[]{:S(2)}) collective-permute-start(f32[4,6,64,1]{2,3,1,0:T(1,128)S(1)} %slice_bitcast_fusion.6), channel_id=1, source_target_pairs={{0,1},{1,0},{2,3},{3,2},{4,5},{5,4},{6,7},{7,6},{8,9},{9,8},{10,11... | collective-permute-start | bytes 18440 | tf_op jit(solution)/shard_map/ppermute | solution.py:200
  218.4 29.7 %collective-permute-start.5 = (f32[4,6,64,128]{3,2,1,0:T(8,128)}, f32[4,6,64,128]{3,2,1,0:T(8,128)}, u32[]{:S(2)}, u32[]{:S(2)}) collective-permute-start(f32[4,6,64,128]{3,2,1,0:T(8,128)} %slice_bitcast_fusion), channel_id=1, source_target_pairs={{0,1},{1,0},{2,3},{3,2},{4,5},{5,4},{6,7},{7,6},{8,9},{9,8},{10,11... | collective-permute-start | bytes 2359304 | tf_op jit(solution)/shard_map/ppermute | solution.py:200
  235.8 7.8 %copy-start.1 = (f32[4,768,128]{2,1,0:T(8,128)S(1)}, f32[4,768,128]{2,1,0:T(8,128)}, u32[]{:S(2)}) copy-start(f32[4,768,128]{2,1,0:T(8,128)} %get-tuple-element.14) | copy-start | bytes 4718596
  238.0 8.4 %collective-permute-start.1 = (f32[4,6,64,1]{2,3,1,0:T(1,128)S(1)}, f32[4,6,64,1]{2,3,1,0:T(1,128)S(1)}, u32[]{:S(2)}, u32[]{:S(2)}) collective-permute-start(f32[4,6,64,1]{2,3,1,0:T(1,128)S(1)} %slice_bitcast_fusion.12), channel_id=1, source_target_pairs={{0,1},{1,0},{2,3},{3,2},{4,5},{5,4},{6,7},{7,6},{8,9},{9,8},{10,11... | collective-permute-start | bytes 18440 | tf_op jit(solution)/shard_map/ppermute | solution.py:195
  242.5 5.4 %collective-permute-start.3 = (f32[4,6,64,1]{2,3,1,0:T(1,128)S(1)}, f32[4,6,64,1]{2,3,1,0:T(1,128)S(1)}, u32[]{:S(2)}, u32[]{:S(2)}) collective-permute-start(f32[4,6,64,1]{2,3,1,0:T(1,128)S(1)} %slice_bitcast_fusion.10), channel_id=1, source_target_pairs={{0,1},{1,0},{2,3},{3,2},{4,5},{5,4},{6,7},{7,6},{8,9},{9,8},{10,11... | collective-permute-start | bytes 18440 | tf_op jit(solution)/shard_map/ppermute | solution.py:195
  243.7 19.8 %collective-permute-start.2 = (f32[4,6,64,128]{3,2,1,0:T(8,128)S(1)}, f32[4,6,64,128]{3,2,1,0:T(8,128)S(1)}, u32[]{:S(2)}, u32[]{:S(2)}) collective-permute-start(f32[4,6,64,128]{3,2,1,0:T(8,128)S(1)} %slice_bitcast_fusion.3), channel_id=1, source_target_pairs={{0,1},{1,0},{2,3},{3,2},{4,5},{5,4},{6,7},{7,6},{8,9},{9,8},{10,11... | collective-permute-start | bytes 2359304 | tf_op jit(solution)/shard_map/ppermute | solution.py:195
  248.0 16.6 %copy-start.3 = (f32[128]{0:T(128)S(1)}, f32[128]{0:T(128)}, u32[]{:S(2)}) copy-start(f32[128]{0:T(128)} %param.7) | copy-start | bytes 1540
Sparse Core Ops, SparseCore 0:
  9.1 128.2 all-gather.1

commit v4 on v3

--- a/solution.py
+++ b/solution.py
@@ -49,19 +49,24 @@
         keys = k_ref[...].reshape(tile_blocks * block_rows, HEAD_DIM)
         vals = v_ref[...].reshape(tile_blocks * block_rows, HEAD_DIM)
         half = q_sc.shape[0] // 2
+        bias = None
+        if masked:
+            key_block = first_block + lax.broadcasted_iota(
+                jnp.int32, (1, tile_blocks * block_rows), 1
+            ) // block_rows
+            visible = (key_block >= lo) & (key_block <= hi)
+            bias = jnp.where(visible, 0.0, -jnp.inf).astype(jnp.float32)
         for part in range(2):
             rows_here = pl.ds(part * half, half)
-            half_step(masked, keys, vals, rows_here)
-
-    def half_step(masked, keys, vals, rows_here):
+            half_step(bias, keys, vals, rows_here)
+
+    def half_step(bias, keys, vals, rows_here):
         scores = lax.dot_general(
             q_sc[rows_here], keys, (((1,), (1,)), ((), ())), preferred_element_type=jnp.float32
         )
         scores = scores * (1.0 / math.sqrt(HEAD_DIM))
-        if masked:
-            key_block = first_block + lax.broadcasted_iota(jnp.int32, scores.shape, 1) // block_rows
-            visible = (key_block >= lo) & (key_block <= hi)
-            scores = jnp.where(visible, scores, -jnp.inf)
+        if bias is not None:
+            scores = scores + bias
         running_max = m_sc[rows_here]
         new_max = jnp.maximum(running_max, jnp.max(scores, axis=1, keepdims=True))
         raw_weights = jnp.exp(scores - new_max)

time: 282 us -> 282 us (level)
  no operation moved by 1% of the time
where the time goes in v4:
time: 282 us; the launch traced here: 277 us
  waiting for transfers between devices  136 us (48%)
  Pallas kernels  89.9 us (32%)
  other arithmetic  16.5 us (6%)
  starting transfers between devices  15.1 us (5%)
  between operations  13.7 us (5%)
  local copies, waits for them, and re-layouts  5.43 us (2%)
    all_gather x1, waiting for transfers between devices, per_device(): blocks = lax.all_gather(pair[:, 0], 'seq', axis=1, tiled=False)  96.7 us
    pallas_call x3, Pallas kernels, attend(): pl.pallas_call(kernel, grid_spec=pltpu.PrefetchScalarGridSpec(num_scalar_...  89.9 us
    ppermute x1, waiting for transfers between devices, per_device(): partner_queries = lax.ppermute(queries, 'row', swap)  24.6 us
    ppermute x3, waiting for transfers between devices, per_device(): early_back = [lax.ppermute(x, 'row', swap) for x in early_theirs]  14.9 us
    pallas_call x4, other arithmetic, attend(): pl.pallas_call(kernel, grid_spec=pltpu.PrefetchScalarGridSpec(num_scalar_...  6.41 us
    ppermute x3, starting transfers between devices, per_device(): early_back = [lax.ppermute(x, 'row', swap) for x in early_theirs]  6.22 us
  transfers between devices with their start and end apart: 8, of which 4 were waited for; matrix products, arithmetic and copies ran while one was open for 4% of the time, Pallas kernels for 6%

profile of v4, /device:TPU:0, one launch (start us, length us, event | category | flops | bytes accessed | tf_op | source)
XLA Modules:
  0.0 276.8 jit_solution(1402309337171365565)
XLA Ops:
  6.5 0.0 all-gather.2.cloned.1.call-start
  6.5 1.7 pad_maximum_fusion
  8.2 0.0 all-gather.2.cloned.1.call-update
  8.2 4.1 %collective-permute-start = (bf16[2,1,64,3072]{3,2,1,0:T(8,128)(2,1)}, bf16[2,1,64,3072]{3,2,1,0:T(8,128)(2,1)S(1)}, u32[]{:S(2)}, u32[]{:S(2)}) collective-permute-start(bf16[2,1,64,3072]{3,2,1,0:T(8,128)(2,1)} %param.4), channel_id=1, source_target_pairs={{0,1},{1,0},{2,3},{3,2},{4,5},{5,4},{6,7},{7,6},{8,9},{9,8},{10,11... | collective-permute-start | bytes 2359304 | tf_op jit(solution)/shard_map/ppermute | solution.py:191
  12.3 0.6 iota_multiply_fusion.bounds_ref
  12.9 0.7 pad_add_fusion
  13.5 1.2 constant_dynamic-update-slice_fusion.1
  14.7 24.6 %collective-permute-done = bf16[2,1,64,3072]{3,2,1,0:T(8,128)(2,1)S(1)} collective-permute-done((bf16[2,1,64,3072]{3,2,1,0:T(8,128)(2,1)}, bf16[2,1,64,3072]{3,2,1,0:T(8,128)(2,1)S(1)}, u32[]{:S(2)}, u32[]{:S(2)}) %collective-permute-start) | collective-permute-done | bytes 786464 | tf_op jit(solution)/shard_map/ppermute | solution.py:191
  39.3 0.1 constant_dynamic-update-slice_fusion
  39.4 1.2 slice_bitcast_fusion.5
  40.6 96.7 %all-gather.2.cloned.1.call-done.k_ref.v_ref = bf16[2,64,64,1024]{3,2,1,0:T(8,128)(2,1)} async-done(((bf16[2,1,64,1024]{3,2,1,0:T(8,128)(2,1)}), bf16[2,64,64,1024]{3,2,1,0:T(8,128)(2,1)}) %all-gather.2.cloned.1.call-update) | async-done | bytes 16777232 | tf_op jit(solution)/shard_map/all_gather | solution.py:194
  137.3 36.4 %shard_map.47 = (f32[4,768,1]{2,1,0:T(8,128)}, f32[4,768,1]{2,1,0:T(8,128)}, f32[4,768,128]{2,1,0:T(8,128)}) custom-call(s32[2]{0:T(128)} %iota_multiply_fusion.bounds_ref, bf16[128,3072]{1,0:T(8,128)(2,1)} %get-tuple-element.30.q_ref, bf16[2,64,64,1024]{3,2,1,0:T(8,128)(2,1)} %all-gather.2.cloned.1.call-done.k_ref.v_ref, ...), custom_call_target="tpu_custom_call" | custom-call | flops 6442450944 | bytes 12320768 | tf_op jit(solution)/shard_map/pallas_call | solution.py:140
  173.7 37.2 %shard_map.48 = (f32[4,768,1]{2,1,0:T(8,128)}, f32[4,768,1]{2,1,0:T(8,128)}, f32[4,768,128]{2,1,0:T(8,128)}) custom-call(s32[2]{0:T(128)} %get-tuple-element.34.bounds_ref, bf16[128,3072]{1,0:T(8,128)(2,1)} %get-tuple-element.30.q_ref, bf16[2,64,64,1024]{3,2,1,0:T(8,128)(2,1)} %all-gather.2.cloned.1.call-done.k_ref.v_ref, ...), custom_call_target="tpu_custom_call" | custom-call | flops 6442450944 | bytes 12320768 | tf_op jit(solution)/shard_map/pallas_call | solution.py:140
  210.9 0.0 copy-start.2
  210.9 0.0 copy-start
  210.9 2.0 reduce.2
  213.0 0.1 reshape.42
  213.1 1.2 collective-permute-start.4
  214.2 0.0 copy-done.2
  214.2 0.5 reduce.3
  214.7 0.1 reshape.43
  214.8 2.5 collective-permute-start.6
  217.4 0.0 copy-done
  217.4 1.0 slice_bitcast_fusion
  218.4 1.1 collective-permute-start.5
  219.4 16.3 %shard_map.46 = (f32[4,768,1]{2,1,0:T(8,128)}, f32[4,768,1]{2,1,0:T(8,128)}, f32[4,768,128]{2,1,0:T(8,128)}) custom-call(s32[2]{0:T(128)} %get-tuple-element.33.bounds_ref, bf16[128,3072]{1,0:T(8,128)(2,1)} %get-tuple-element.29.q_ref, bf16[2,64,64,1024]{3,2,1,0:T(8,128)(2,1)} %all-gather.2.cloned.1.call-done.k_ref.v_ref, ...), custom_call_target="tpu_custom_call" | custom-call | flops 6442450944 | bytes 12320768 | tf_op jit(solution)/shard_map/pallas_call | solution.py:140
  235.8 0.0 copy-start.1
  235.8 2.0 reduce
  237.8 0.1 reshape.39
  237.9 2.5 collective-permute-start.1
  240.4 1.9 reduce.1
  242.3 0.1 reshape.40
  242.4 1.2 collective-permute-start.3
  243.6 0.0 copy-done.1
  243.6 0.1 slice_bitcast_fusion.3
  243.7 0.0 collective-permute-done.4
  243.7 2.5 collective-permute-start.2
  246.2 0.0 collective-permute-done.6
  246.3 0.0 collective-permute-done.1
  246.3 1.5 collective-permute-done.3
  248.0 0.0 copy-start.3
  248.0 0.0 collective-permute-done.5
  248.0 2.0 multiply_reduce_fusion
  250.1 13.4 %collective-permute-done.2 = f32[4,6,64,128]{3,2,1,0:T(8,128)S(1)} collective-permute-done((f32[4,6,64,128]{3,2,1,0:T(8,128)S(1)}, f32[4,6,64,128]{3,2,1,0:T(8,128)S(1)}, u32[]{:S(2)}, u32[]{:S(2)}) %collective-permute-start.2) | collective-permute-done | bytes 786464 | tf_op jit(solution)/shard_map/ppermute | solution.py:200
  263.5 1.0 multiply_reduce_fusion.1
  264.5 0.0 copy-done.3
  264.5 3.0 %fusion.4 = (bf16[64,4,6,128]{3,0,2,1:T(8,128)(2,1)S(1)}, bf16[64,4,6,128]{3,0,2,1:T(8,128)(2,1)S(1)}) fusion(f32[128]{0:T(128)S(1)} %copy-done.3, f32[4,6,64]{2,1,0:T(8,128)S(1)} %copy.109, f32[4,6,64,128]{3,2,1,0:T(8,128)S(1)} %collective-permute-done.2, f32[4,6,64]{2,1,0:T(8,128)S(1)} %copy.102, f32[4,6,64]{2,1,0:T(8,128)S(1)} %copy.99, ...), kind=kLoop, calls=%fused_computation.15 | loop fusion | flops 2359296 | bytes 3969536 | tf_op jit(solution)/shard_map/transpose | solution.py:183
  267.6 0.3 copy.110
  267.9 0.4 stack_reshape.6
  268.3 0.3 copy.125
  268.6 0.4 stack_reshape.7
  269.0 0.9 maximum_bitcast_fusion
  (22 shorter events, 0.2 us)
Async XLA Ops:
  6.5 130.8 %all-gather.2.cloned.1.call-start = ((), (), s32[]{:S(2)}) async-start(), calls=%async_computation | async-start | bytes 17039360 | tf_op jit(solution)/shard_map/all_gather | solution.py:194
  8.2 31.1 %collective-permute-start = (bf16[2,1,64,3072]{3,2,1,0:T(8,128)(2,1)}, bf16[2,1,64,3072]{3,2,1,0:T(8,128)(2,1)S(1)}, u32[]{:S(2)}, u32[]{:S(2)}) collective-permute-start(bf16[2,1,64,3072]{3,2,1,0:T(8,128)(2,1)} %param.4), channel_id=1, source_target_pairs={{0,1},{1,0},{2,3},{3,2},{4,5},{5,4},{6,7},{7,6},{8,9},{9,8},{10,11... | collective-permute-start | bytes 2359304 | tf_op jit(solution)/shard_map/ppermute | solution.py:191
  210.9 3.3 %copy-start.2 = (f32[4,768,1]{2,1,0:T(8,128)S(1)}, f32[4,768,1]{2,1,0:T(8,128)}, u32[]{:S(2)}) copy-start(f32[4,768,1]{2,1,0:T(8,128)} %get-tuple-element.22) | copy-start | bytes 36868
  210.9 6.5 %copy-start = (f32[4,768,128]{2,1,0:T(8,128)S(1)}, f32[4,768,128]{2,1,0:T(8,128)}, u32[]{:S(2)}) copy-start(f32[4,768,128]{2,1,0:T(8,128)} %get-tuple-element.20) | copy-start | bytes 4718596
  213.1 30.6 %collective-permute-start.4 = (f32[4,6,64,1]{2,3,1,0:T(1,128)S(1)}, f32[4,6,64,1]{2,3,1,0:T(1,128)S(1)}, u32[]{:S(2)}, u32[]{:S(2)}) collective-permute-start(f32[4,6,64,1]{2,3,1,0:T(1,128)S(1)} %slice_bitcast_fusion.8), channel_id=1, source_target_pairs={{0,1},{1,0},{2,3},{3,2},{4,5},{5,4},{6,7},{7,6},{8,9},{9,8},{10,11... | collective-permute-start | bytes 18440 | tf_op jit(solution)/shard_map/ppermute | solution.py:205
  214.8 31.4 %collective-permute-start.6 = (f32[4,6,64,1]{2,3,1,0:T(1,128)S(1)}, f32[4,6,64,1]{2,3,1,0:T(1,128)S(1)}, u32[]{:S(2)}, u32[]{:S(2)}) collective-permute-start(f32[4,6,64,1]{2,3,1,0:T(1,128)S(1)} %slice_bitcast_fusion.6), channel_id=1, source_target_pairs={{0,1},{1,0},{2,3},{3,2},{4,5},{5,4},{6,7},{7,6},{8,9},{9,8},{10,11... | collective-permute-start | bytes 18440 | tf_op jit(solution)/shard_map/ppermute | solution.py:205
  218.4 29.6 %collective-permute-start.5 = (f32[4,6,64,128]{3,2,1,0:T(8,128)}, f32[4,6,64,128]{3,2,1,0:T(8,128)}, u32[]{:S(2)}, u32[]{:S(2)}) collective-permute-start(f32[4,6,64,128]{3,2,1,0:T(8,128)} %slice_bitcast_fusion), channel_id=1, source_target_pairs={{0,1},{1,0},{2,3},{3,2},{4,5},{5,4},{6,7},{7,6},{8,9},{9,8},{10,11... | collective-permute-start | bytes 2359304 | tf_op jit(solution)/shard_map/ppermute | solution.py:205
  235.8 7.8 %copy-start.1 = (f32[4,768,128]{2,1,0:T(8,128)S(1)}, f32[4,768,128]{2,1,0:T(8,128)}, u32[]{:S(2)}) copy-start(f32[4,768,128]{2,1,0:T(8,128)} %get-tuple-element.14) | copy-start | bytes 4718596
  237.9 8.4 %collective-permute-start.1 = (f32[4,6,64,1]{2,3,1,0:T(1,128)S(1)}, f32[4,6,64,1]{2,3,1,0:T(1,128)S(1)}, u32[]{:S(2)}, u32[]{:S(2)}) collective-permute-start(f32[4,6,64,1]{2,3,1,0:T(1,128)S(1)} %slice_bitcast_fusion.12), channel_id=1, source_target_pairs={{0,1},{1,0},{2,3},{3,2},{4,5},{5,4},{6,7},{7,6},{8,9},{9,8},{10,11... | collective-permute-start | bytes 18440 | tf_op jit(solution)/shard_map/ppermute | solution.py:200
  242.4 5.4 %collective-permute-start.3 = (f32[4,6,64,1]{2,3,1,0:T(1,128)S(1)}, f32[4,6,64,1]{2,3,1,0:T(1,128)S(1)}, u32[]{:S(2)}, u32[]{:S(2)}) collective-permute-start(f32[4,6,64,1]{2,3,1,0:T(1,128)S(1)} %slice_bitcast_fusion.10), channel_id=1, source_target_pairs={{0,1},{1,0},{2,3},{3,2},{4,5},{5,4},{6,7},{7,6},{8,9},{9,8},{10,11... | collective-permute-start | bytes 18440 | tf_op jit(solution)/shard_map/ppermute | solution.py:200
  243.7 19.8 %collective-permute-start.2 = (f32[4,6,64,128]{3,2,1,0:T(8,128)S(1)}, f32[4,6,64,128]{3,2,1,0:T(8,128)S(1)}, u32[]{:S(2)}, u32[]{:S(2)}) collective-permute-start(f32[4,6,64,128]{3,2,1,0:T(8,128)S(1)} %slice_bitcast_fusion.3), channel_id=1, source_target_pairs={{0,1},{1,0},{2,3},{3,2},{4,5},{5,4},{6,7},{7,6},{8,9},{9,8},{10,11... | collective-permute-start | bytes 2359304 | tf_op jit(solution)/shard_map/ppermute | solution.py:200
  248.0 16.6 %copy-start.3 = (f32[128]{0:T(128)S(1)}, f32[128]{0:T(128)}, u32[]{:S(2)}) copy-start(f32[128]{0:T(128)} %param.7) | copy-start | bytes 1540
Sparse Core Ops, SparseCore 0:
  9.1 128.2 all-gather.1

commit v5 on v4

--- a/solution.py
+++ b/solution.py
@@ -14,6 +14,7 @@
 TILE_KEYS = 1024
 
 lowest_score = -1e30
+EXP2_SCALE = math.log2(math.e) / math.sqrt(HEAD_DIM)
 
 
 def attend_kernel(bounds_ref, q_ref, k_ref, v_ref, *rest, carry_in):
@@ -21,7 +22,7 @@
         m_in, l_in, acc_in = rest[:3]
         rest = rest[3:]
     m_out, l_out, acc_out = rest[:3]
-    q_sc, m_sc, l_sc, acc_sc = rest[3:]
+    q_sc, m_sc, l_sc, acc_sc, vals_sc = rest[3:]
 
     t = pl.program_id(1)
     last = pl.num_programs(1) - 1
@@ -33,6 +34,7 @@
 
     @pl.when(t == 0)
     def _init():
+        vals_sc[:, HEAD_DIM:] = jnp.ones((vals_sc.shape[0], HEAD_DIM), jnp.bfloat16)
         q_sc[...] = jnp.concatenate(
             [q_ref[:, j * HEAD_DIM:(j + 1) * HEAD_DIM] for j in range(GROUP)], axis=0
         )
@@ -47,7 +49,8 @@
 
     def step(masked):
         keys = k_ref[...].reshape(tile_blocks * block_rows, HEAD_DIM)
-        vals = v_ref[...].reshape(tile_blocks * block_rows, HEAD_DIM)
+        vals_sc[:, :HEAD_DIM] = v_ref[...].reshape(tile_blocks * block_rows, HEAD_DIM)
+        vals = vals_sc[...]
         half = q_sc.shape[0] // 2
         bias = None
         if masked:
@@ -64,17 +67,17 @@
         scores = lax.dot_general(
             q_sc[rows_here], keys, (((1,), (1,)), ((), ())), preferred_element_type=jnp.float32
         )
-        scores = scores * (1.0 / math.sqrt(HEAD_DIM))
         if bias is not None:
             scores = scores + bias
         running_max = m_sc[rows_here]
         new_max = jnp.maximum(running_max, jnp.max(scores, axis=1, keepdims=True))
-        raw_weights = jnp.exp(scores - new_max)
-        factor = jnp.exp(running_max - new_max)
-        l_sc[rows_here] = l_sc[rows_here] * factor + jnp.sum(raw_weights, axis=1, keepdims=True)
-        acc_sc[rows_here] = acc_sc[rows_here] * factor + jnp.dot(
+        raw_weights = jnp.exp2((scores - new_max) * EXP2_SCALE)
+        factor = jnp.exp2((running_max - new_max) * EXP2_SCALE)
+        mixed = jnp.dot(
             raw_weights.astype(jnp.bfloat16), vals, preferred_element_type=jnp.float32
         )
+        l_sc[rows_here] = l_sc[rows_here] * factor + mixed[:, HEAD_DIM:HEAD_DIM + 1]
+        acc_sc[rows_here] = acc_sc[rows_here] * factor + mixed[:, :HEAD_DIM]
         m_sc[rows_here] = new_max
 
     active = tile <= hi // tile_blocks
@@ -149,6 +152,7 @@
                 pltpu.VMEM((qrows, 1), jnp.float32),
                 pltpu.VMEM((qrows, 1), jnp.float32),
                 pltpu.VMEM((qrows, HEAD_DIM), jnp.float32),
+                pltpu.VMEM((TILE_KEYS, 2 * HEAD_DIM), jnp.bfloat16),
             ],
         ),
         out_shape=state_shapes,
@@ -172,8 +176,8 @@
     own_max, own_sum, own_acc = mine
     far_max, far_sum, far_acc = theirs
     top = jnp.maximum(own_max, far_max)
-    own_factor = jnp.exp(own_max - top)
-    far_factor = jnp.exp(far_max - top)
+    own_factor = jnp.exp2((own_max - top) * EXP2_SCALE)
+    far_factor = jnp.exp2((far_max - top) * EXP2_SCALE)
     total = own_sum * own_factor + far_sum * far_factor
     acc = own_acc * own_factor + far_acc * far_factor
     mixed = acc / total

time: 282 us -> 277 us (0.982)
  Pallas kernels: 89.9 us -> 85.6 us
    pallas_call x3, Pallas kernels: 89.9 us -> 85.6 us  [attend(): pl.pallas_call(kernel, grid_spec=pltpu.PrefetchScalarGridSpec(num_scalar_...]
where the time goes in v5:
time: 277 us; the launch traced here: 273 us
  waiting for transfers between devices  136 us (49%)
  Pallas kernels  85.6 us (31%)
  other arithmetic  16.5 us (6%)
  starting transfers between devices  15.1 us (5%)
  between operations  13.7 us (5%)
  local copies, waits for them, and re-layouts  5.43 us (2%)
    all_gather x1, waiting for transfers between devices, per_device(): blocks = lax.all_gather(pair[:, 0], 'seq', axis=1, tiled=False)  96.7 us
    pallas_call x3, Pallas kernels, attend(): pl.pallas_call(kernel, grid_spec=pltpu.PrefetchScalarGridSpec(num_scalar_...  85.6 us
    ppermute x1, waiting for transfers between devices, per_device(): partner_queries = lax.ppermute(queries, 'row', swap)  24.6 us
    ppermute x3, waiting for transfers between devices, per_device(): early_back = [lax.ppermute(x, 'row', swap) for x in early_theirs]  15.1 us
    pallas_call x4, other arithmetic, attend(): pl.pallas_call(kernel, grid_spec=pltpu.PrefetchScalarGridSpec(num_scalar_...  6.41 us
    ppermute x3, starting transfers between devices, per_device(): early_back = [lax.ppermute(x, 'row', swap) for x in early_theirs]  6.22 us
  transfers between devices with their start and end apart: 8, of which 4 were waited for; matrix products, arithmetic and copies ran while one was open for 4% of the time, Pallas kernels for 6%

profile of v5, /device:TPU:0, one launch (start us, length us, event | category | flops | bytes accessed | tf_op | source)
XLA Modules:
  0.0 272.7 jit_solution(16734806949809132192)
XLA Ops:
  6.5 0.0 all-gather.2.cloned.1.call-start
  6.5 1.7 pad_maximum_fusion
  8.2 0.0 all-gather.2.cloned.1.call-update
  8.2 4.1 %collective-permute-start = (bf16[2,1,64,3072]{3,2,1,0:T(8,128)(2,1)}, bf16[2,1,64,3072]{3,2,1,0:T(8,128)(2,1)S(1)}, u32[]{:S(2)}, u32[]{:S(2)}) collective-permute-start(bf16[2,1,64,3072]{3,2,1,0:T(8,128)(2,1)} %param.4), channel_id=1, source_target_pairs={{0,1},{1,0},{2,3},{3,2},{4,5},{5,4},{6,7},{7,6},{8,9},{9,8},{10,11... | collective-permute-start | bytes 2359304 | tf_op jit(solution)/shard_map/ppermute | solution.py:195
  12.3 0.6 iota_multiply_fusion.bounds_ref
  12.9 0.7 pad_add_fusion
  13.5 1.2 constant_dynamic-update-slice_fusion.1
  14.7 24.6 %collective-permute-done = bf16[2,1,64,3072]{3,2,1,0:T(8,128)(2,1)S(1)} collective-permute-done((bf16[2,1,64,3072]{3,2,1,0:T(8,128)(2,1)}, bf16[2,1,64,3072]{3,2,1,0:T(8,128)(2,1)S(1)}, u32[]{:S(2)}, u32[]{:S(2)}) %collective-permute-start) | collective-permute-done | bytes 786464 | tf_op jit(solution)/shard_map/ppermute | solution.py:195
  39.3 0.1 constant_dynamic-update-slice_fusion
  39.4 1.2 slice_bitcast_fusion.5
  40.6 96.7 %all-gather.2.cloned.1.call-done.k_ref.v_ref = bf16[2,64,64,1024]{3,2,1,0:T(8,128)(2,1)} async-done(((bf16[2,1,64,1024]{3,2,1,0:T(8,128)(2,1)}), bf16[2,64,64,1024]{3,2,1,0:T(8,128)(2,1)}) %all-gather.2.cloned.1.call-update) | async-done | bytes 16777232 | tf_op jit(solution)/shard_map/all_gather | solution.py:198
  137.3 34.3 %shard_map.47 = (f32[4,768,1]{2,1,0:T(8,128)}, f32[4,768,1]{2,1,0:T(8,128)}, f32[4,768,128]{2,1,0:T(8,128)}) custom-call(s32[2]{0:T(128)} %iota_multiply_fusion.bounds_ref, bf16[128,3072]{1,0:T(8,128)(2,1)} %get-tuple-element.30.q_ref, bf16[2,64,64,1024]{3,2,1,0:T(8,128)(2,1)} %all-gather.2.cloned.1.call-done.k_ref.v_ref, ...), custom_call_target="tpu_custom_call" | custom-call | flops 6442450944 | bytes 12320768 | tf_op jit(solution)/shard_map/pallas_call | solution.py:143
  171.6 35.1 %shard_map.48 = (f32[4,768,1]{2,1,0:T(8,128)}, f32[4,768,1]{2,1,0:T(8,128)}, f32[4,768,128]{2,1,0:T(8,128)}) custom-call(s32[2]{0:T(128)} %get-tuple-element.34.bounds_ref, bf16[128,3072]{1,0:T(8,128)(2,1)} %get-tuple-element.30.q_ref, bf16[2,64,64,1024]{3,2,1,0:T(8,128)(2,1)} %all-gather.2.cloned.1.call-done.k_ref.v_ref, ...), custom_call_target="tpu_custom_call" | custom-call | flops 6442450944 | bytes 12320768 | tf_op jit(solution)/shard_map/pallas_call | solution.py:143
  206.7 0.0 copy-start.2
  206.7 0.0 copy-start
  206.8 2.0 reduce.2
  208.8 0.1 reshape.42
  208.9 1.2 collective-permute-start.4
  210.1 0.0 copy-done.2
  210.1 0.5 reduce.3
  210.6 0.1 reshape.43
  210.7 2.5 collective-permute-start.6
  213.2 0.0 copy-done
  213.2 1.0 slice_bitcast_fusion
  214.2 1.1 collective-permute-start.5
  215.3 16.2 %shard_map.46 = (f32[4,768,1]{2,1,0:T(8,128)}, f32[4,768,1]{2,1,0:T(8,128)}, f32[4,768,128]{2,1,0:T(8,128)}) custom-call(s32[2]{0:T(128)} %get-tuple-element.33.bounds_ref, bf16[128,3072]{1,0:T(8,128)(2,1)} %get-tuple-element.29.q_ref, bf16[2,64,64,1024]{3,2,1,0:T(8,128)(2,1)} %all-gather.2.cloned.1.call-done.k_ref.v_ref, ...), custom_call_target="tpu_custom_call" | custom-call | flops 6442450944 | bytes 12320768 | tf_op jit(solution)/shard_map/pallas_call | solution.py:143
  231.4 0.0 copy-start.1
  231.4 2.0 reduce
  233.4 0.1 reshape.39
  233.6 2.5 collective-permute-start.1
  236.1 1.9 reduce.1
  238.0 0.1 reshape.40
  238.1 1.2 collective-permute-start.3
  239.3 0.0 copy-done.1
  239.3 0.1 slice_bitcast_fusion.3
  239.3 0.0 collective-permute-done.4
  239.3 2.5 collective-permute-start.2
  241.9 0.0 collective-permute-done.6
  241.9 0.1 fusion.11
  242.0 0.0 collective-permute-done.1
  242.0 1.5 collective-permute-done.3
  243.5 0.1 fusion.13
  243.6 0.0 copy-start.3
  243.7 0.0 collective-permute-done.5
  243.7 2.0 multiply_reduce_fusion
  245.8 13.5 %collective-permute-done.2 = f32[4,6,64,128]{3,2,1,0:T(8,128)S(1)} collective-permute-done((f32[4,6,64,128]{3,2,1,0:T(8,128)S(1)}, f32[4,6,64,128]{3,2,1,0:T(8,128)S(1)}, u32[]{:S(2)}, u32[]{:S(2)}) %collective-permute-start.2) | collective-permute-done | bytes 786464 | tf_op jit(solution)/shard_map/ppermute | solution.py:204
  259.3 1.0 multiply_reduce_fusion.1
  260.4 0.0 copy-done.3
  260.4 3.0 %fusion.4 = (bf16[64,4,6,128]{3,0,2,1:T(8,128)(2,1)S(1)}, bf16[64,4,6,128]{3,0,2,1:T(8,128)(2,1)S(1)}) fusion(f32[128]{0:T(128)S(1)} %copy-done.3, f32[4,6,64]{2,1,0:T(8,128)S(1)} %copy.112, f32[4,6,64,128]{3,2,1,0:T(8,128)S(1)} %collective-permute-done.2, f32[4,6,64]{2,1,0:T(8,128)S(1)} %copy.105, f32[4,6,64]{2,1,0:T(8,128)S(1)} %copy.102, ...), kind=kLoop, calls=%fused_computation.15 | loop fusion | flops 2359296 | bytes 3969536 | tf_op jit(solution)/shard_map/transpose | solution.py:187
  263.4 0.3 copy.113
  263.7 0.4 stack_reshape.6
  264.2 0.3 copy.129
  264.4 0.4 stack_reshape.7
  264.9 0.9 maximum_bitcast_fusion
  (20 shorter events, 0.1 us)
Async XLA Ops:
  6.5 130.8 %all-gather.2.cloned.1.call-start = ((), (), s32[]{:S(2)}) async-start(), calls=%async_computation | async-start | bytes 17039360 | tf_op jit(solution)/shard_map/all_gather | solution.py:198
  8.2 31.1 %collective-permute-start = (bf16[2,1,64,3072]{3,2,1,0:T(8,128)(2,1)}, bf16[2,1,64,3072]{3,2,1,0:T(8,128)(2,1)S(1)}, u32[]{:S(2)}, u32[]{:S(2)}) collective-permute-start(bf16[2,1,64,3072]{3,2,1,0:T(8,128)(2,1)} %param.4), channel_id=1, source_target_pairs={{0,1},{1,0},{2,3},{3,2},{4,5},{5,4},{6,7},{7,6},{8,9},{9,8},{10,11... | collective-permute-start | bytes 2359304 | tf_op jit(solution)/shard_map/ppermute | solution.py:195
  206.7 3.3 %copy-start.2 = (f32[4,768,1]{2,1,0:T(8,128)S(1)}, f32[4,768,1]{2,1,0:T(8,128)}, u32[]{:S(2)}) copy-start(f32[4,768,1]{2,1,0:T(8,128)} %get-tuple-element.22) | copy-start | bytes 36868
  206.7 6.5 %copy-start = (f32[4,768,128]{2,1,0:T(8,128)S(1)}, f32[4,768,128]{2,1,0:T(8,128)}, u32[]{:S(2)}) copy-start(f32[4,768,128]{2,1,0:T(8,128)} %get-tuple-element.20) | copy-start | bytes 4718596
  208.9 30.4 %collective-permute-start.4 = (f32[4,6,64,1]{2,3,1,0:T(1,128)S(1)}, f32[4,6,64,1]{2,3,1,0:T(1,128)S(1)}, u32[]{:S(2)}, u32[]{:S(2)}) collective-permute-start(f32[4,6,64,1]{2,3,1,0:T(1,128)S(1)} %slice_bitcast_fusion.8), channel_id=1, source_target_pairs={{0,1},{1,0},{2,3},{3,2},{4,5},{5,4},{6,7},{7,6},{8,9},{9,8},{10,11... | collective-permute-start | bytes 18440 | tf_op jit(solution)/shard_map/ppermute | solution.py:209
  210.7 31.2 %collective-permute-start.6 = (f32[4,6,64,1]{2,3,1,0:T(1,128)S(1)}, f32[4,6,64,1]{2,3,1,0:T(1,128)S(1)}, u32[]{:S(2)}, u32[]{:S(2)}) collective-permute-start(f32[4,6,64,1]{2,3,1,0:T(1,128)S(1)} %slice_bitcast_fusion.6), channel_id=1, source_target_pairs={{0,1},{1,0},{2,3},{3,2},{4,5},{5,4},{6,7},{7,6},{8,9},{9,8},{10,11... | collective-permute-start | bytes 18440 | tf_op jit(solution)/shard_map/ppermute | solution.py:209
  214.2 29.5 %collective-permute-start.5 = (f32[4,6,64,128]{3,2,1,0:T(8,128)}, f32[4,6,64,128]{3,2,1,0:T(8,128)}, u32[]{:S(2)}, u32[]{:S(2)}) collective-permute-start(f32[4,6,64,128]{3,2,1,0:T(8,128)} %slice_bitcast_fusion), channel_id=1, source_target_pairs={{0,1},{1,0},{2,3},{3,2},{4,5},{5,4},{6,7},{7,6},{8,9},{9,8},{10,11... | collective-permute-start | bytes 2359304 | tf_op jit(solution)/shard_map/ppermute | solution.py:209
  231.4 7.8 %copy-start.1 = (f32[4,768,128]{2,1,0:T(8,128)S(1)}, f32[4,768,128]{2,1,0:T(8,128)}, u32[]{:S(2)}) copy-start(f32[4,768,128]{2,1,0:T(8,128)} %get-tuple-element.14) | copy-start | bytes 4718596
  233.6 8.4 %collective-permute-start.1 = (f32[4,6,64,1]{2,3,1,0:T(1,128)S(1)}, f32[4,6,64,1]{2,3,1,0:T(1,128)S(1)}, u32[]{:S(2)}, u32[]{:S(2)}) collective-permute-start(f32[4,6,64,1]{2,3,1,0:T(1,128)S(1)} %slice_bitcast_fusion.12), channel_id=1, source_target_pairs={{0,1},{1,0},{2,3},{3,2},{4,5},{5,4},{6,7},{7,6},{8,9},{9,8},{10,11... | collective-permute-start | bytes 18440 | tf_op jit(solution)/shard_map/ppermute | solution.py:204
  238.1 5.4 %collective-permute-start.3 = (f32[4,6,64,1]{2,3,1,0:T(1,128)S(1)}, f32[4,6,64,1]{2,3,1,0:T(1,128)S(1)}, u32[]{:S(2)}, u32[]{:S(2)}) collective-permute-start(f32[4,6,64,1]{2,3,1,0:T(1,128)S(1)} %slice_bitcast_fusion.10), channel_id=1, source_target_pairs={{0,1},{1,0},{2,3},{3,2},{4,5},{5,4},{6,7},{7,6},{8,9},{9,8},{10,11... | collective-permute-start | bytes 18440 | tf_op jit(solution)/shard_map/ppermute | solution.py:204
  239.3 20.0 %collective-permute-start.2 = (f32[4,6,64,128]{3,2,1,0:T(8,128)S(1)}, f32[4,6,64,128]{3,2,1,0:T(8,128)S(1)}, u32[]{:S(2)}, u32[]{:S(2)}) collective-permute-start(f32[4,6,64,128]{3,2,1,0:T(8,128)S(1)} %slice_bitcast_fusion.3), channel_id=1, source_target_pairs={{0,1},{1,0},{2,3},{3,2},{4,5},{5,4},{6,7},{7,6},{8,9},{9,8},{10,11... | collective-permute-start | bytes 2359304 | tf_op jit(solution)/shard_map/ppermute | solution.py:204
  243.6 16.7 %copy-start.3 = (f32[128]{0:T(128)S(1)}, f32[128]{0:T(128)}, u32[]{:S(2)}) copy-start(f32[128]{0:T(128)} %param.7) | copy-start | bytes 1540
Sparse Core Ops, SparseCore 0:
  9.1 128.2 all-gather.1

commit v6 on v5

--- a/solution.py
+++ b/solution.py
@@ -6,7 +6,7 @@
 from jax import lax
 from jax.experimental import pallas as pl
 from jax.experimental.pallas import tpu as pltpu
-from jax.sharding import PartitionSpec as P
+from jax.sharding import Mesh, PartitionSpec as P
 
 KV_HEADS = 4
 GROUP = 6
@@ -187,15 +187,17 @@
     return normed.transpose(2, 0, 1, 3).reshape(rows, KV_HEADS * GROUP * HEAD_DIM)
 
 
-def per_device(queries, keys, values, gain):
-    seq_index = lax.axis_index("seq")
-    last_index = lax.axis_size("seq") - 1
+def per_device(queries, keys, values, gain, outer, inner):
+    seq_index = lax.axis_index("outer") * inner + lax.axis_index("inner")
+    last_index = outer * inner - 1
     own_rows = queries.shape[2]
     swap = [(0, 1), (1, 0)]
     partner_queries = lax.ppermute(queries, "row", swap)
     both_queries = jnp.concatenate([queries, partner_queries], axis=2)
     pair = jnp.concatenate([keys, values], axis=-1)
-    blocks = lax.all_gather(pair[:, 0], "seq", axis=1, tiled=False)
+    blocks = lax.all_gather(pair[:, 0], "outer", axis=1, tiled=False)
+    blocks = lax.all_gather(blocks, "inner", axis=2, tiled=False)
+    blocks = blocks.reshape(2, outer * inner, own_rows, pair.shape[3])
     zero = jnp.int32(0)
     top = jnp.int32(last_index)
 
@@ -214,15 +216,15 @@
 
 
 def solution(mesh):
+    seq_count, row_count = mesh.devices.shape
+    outer = math.gcd(seq_count, 4)
+    inner = seq_count // outer
+    split = Mesh(mesh.devices.reshape(outer, inner, row_count), ("outer", "inner", "row"))
+    spec = P(None, ("outer", "inner"), "row", None)
     return jax.shard_map(
-        per_device,
-        mesh=mesh,
-        in_specs=(
-            P(None, "seq", "row", None),
-            P(None, "seq", "row", None),
-            P(None, "seq", "row", None),
-            P(),
-        ),
-        out_specs=P(None, "seq", "row", None),
+        functools.partial(per_device, outer=outer, inner=inner),
+        mesh=split,
+        in_specs=(spec, spec, spec, P()),
+        out_specs=spec,
         check_vma=False,
     )

time: 277 us -> 276 us (level)
    all_gather x1 -> x2, waiting for transfers between devices: 96.7 us -> 97.4 us  [the longest x1 70.2 us: per_device(): blocks = lax.all_gather(blocks, 'inner', axis=2, tiled=False)]
  transfers between devices with their start and end apart: 8 -> 9, of which waited for: 4 -> 5; matrix products, arithmetic and copies ran while one was open for 4% -> 4% of each run, Pallas kernels for 6% -> 6%
where the time goes in v6:
time: 276 us; the launch traced here: 271 us
  waiting for transfers between devices  137 us (50%)
  Pallas kernels  85.6 us (31%)
  other arithmetic  16.6 us (6%)
  starting transfers between devices  14.3 us (5%)
  between operations  13.7 us (5%)
  local copies, waits for them, and re-layouts  4.33 us (2%)
    pallas_call x3, Pallas kernels, attend(): pl.pallas_call(kernel, grid_spec=pltpu.PrefetchScalarGridSpec(num_scalar_...  85.6 us
    all_gather x1, waiting for transfers between devices, per_device(): blocks = lax.all_gather(blocks, 'inner', axis=2, tiled=False)  70.2 us
    all_gather x1, waiting for transfers between devices, per_device(): blocks = lax.all_gather(pair[:, 0], 'outer', axis=1, tiled=False)  27.2 us
    ppermute x1, waiting for transfers between devices, per_device(): partner_queries = lax.ppermute(queries, 'row', swap)  23.6 us
    ppermute x3, waiting for transfers between devices, per_device(): early_back = [lax.ppermute(x, 'row', swap) for x in early_theirs]  15.9 us
    pallas_call x4, other arithmetic, attend(): pl.pallas_call(kernel, grid_spec=pltpu.PrefetchScalarGridSpec(num_scalar_...  6.41 us
    ppermute x3, starting transfers between devices, per_device(): late_back = [lax.ppermute(x, 'row', swap) for x in late_theirs]  5.57 us
  transfers between devices with their start and end apart: 9, of which 5 were waited for; matrix products, arithmetic and copies ran while one was open for 4% of the time, Pallas kernels for 6%

profile of v6, /device:TPU:0, one launch (start us, length us, event | category | flops | bytes accessed | tf_op | source)
XLA Modules:
  0.0 271.4 jit_solution(13647037771077046190)
XLA Ops:
  6.5 0.0 copy-start.3
  6.5 0.0 all-gather.4.cloned.1.call-start
  6.5 1.8 pad_maximum_fusion
  8.3 0.0 all-gather.4.cloned.1.call-update
  8.3 0.0 all-gather.6.cloned.1.call-start
  8.4 27.2 %all-gather.4.cloned.1.call-done = bf16[2,4,64,1024]{3,2,1,0:T(8,128)(2,1)} async-done(((bf16[2,1,64,1024]{3,2,1,0:T(8,128)(2,1)}), bf16[2,4,64,1024]{3,2,1,0:T(8,128)(2,1)}) %all-gather.4.cloned.1.call-update) | async-done | bytes 1048592 | tf_op jit(solution)/shard_map/all_gather | solution.py:198
  35.6 0.0 all-gather.6.cloned.1.call-update
  35.6 0.0 copy-done.3
  35.6 3.2 %collective-permute-start = (bf16[2,1,64,3072]{3,2,1,0:T(8,128)(2,1)S(1)}, bf16[2,1,64,3072]{3,2,1,0:T(8,128)(2,1)S(1)}, u32[]{:S(2)}, u32[]{:S(2)}) collective-permute-start(bf16[2,1,64,3072]{3,2,1,0:T(8,128)(2,1)S(1)} %copy-done.3), channel_id=1, source_target_pairs={{0,1},{1,0},{2,3},{3,2},{4,5},{5,4},{6,7},{7,6},{8,9},{9,8},{10,11... | collective-permute-start | bytes 2359304 | tf_op jit(solution)/shard_map/ppermute | solution.py:195
  38.8 0.6 iota_multiply_fusion.bounds_ref
  39.4 0.7 pad_add_fusion
  40.1 0.1 constant_dynamic-update-slice_fusion.1
  40.1 23.6 %collective-permute-done = bf16[2,1,64,3072]{3,2,1,0:T(8,128)(2,1)S(1)} collective-permute-done((bf16[2,1,64,3072]{3,2,1,0:T(8,128)(2,1)S(1)}, bf16[2,1,64,3072]{3,2,1,0:T(8,128)(2,1)S(1)}, u32[]{:S(2)}, u32[]{:S(2)}) %collective-permute-start) | collective-permute-done | bytes 786464 | tf_op jit(solution)/shard_map/ppermute | solution.py:195
  63.7 0.1 constant_dynamic-update-slice_fusion
  63.8 1.2 slice_bitcast_fusion.5
  65.0 70.2 %all-gather.6.cloned.1.call-done = bf16[2,4,1024,1024]{3,2,1,0:T(8,128)(2,1)} async-done(((bf16[2,4,64,1024]{3,2,1,0:T(8,128)(2,1)}), bf16[2,4,1024,1024]{3,2,1,0:T(8,128)(2,1)}) %all-gather.6.cloned.1.call-update) | async-done | bytes 16777232 | tf_op jit(solution)/shard_map/all_gather | solution.py:199
  135.2 34.3 %shard_map.47 = (f32[4,768,1]{2,1,0:T(8,128)}, f32[4,768,1]{2,1,0:T(8,128)}, f32[4,768,128]{2,1,0:T(8,128)}) custom-call(s32[2]{0:T(128)} %iota_multiply_fusion.bounds_ref, bf16[128,3072]{1,0:T(8,128)(2,1)} %get-tuple-element.30.q_ref, bf16[2,64,64,1024]{3,2,1,0:T(8,128)(2,1)} %bitcast.110, bf16[2,64,64,1024]{3,2,1,0:T(8,128)(2,1)} %bitcast.111), custom_call_target="tpu_custom_call" | custom-call | flops 6442450944 | bytes 12320768 | tf_op jit(solution)/shard_map/pallas_call | solution.py:143
  169.5 35.1 %shard_map.48 = (f32[4,768,1]{2,1,0:T(8,128)}, f32[4,768,1]{2,1,0:T(8,128)}, f32[4,768,128]{2,1,0:T(8,128)}) custom-call(s32[2]{0:T(128)} %get-tuple-element.34.bounds_ref, bf16[128,3072]{1,0:T(8,128)(2,1)} %get-tuple-element.30.q_ref, bf16[2,64,64,1024]{3,2,1,0:T(8,128)(2,1)} %bitcast.112, bf16[2,64,64,1024]{3,2,1,0:T(8,128)(2,1)} %bitcast.113, ...), custom_call_target="tpu_custom_call" | custom-call | flops 6442450944 | bytes 12320768 | tf_op jit(solution)/shard_map/pallas_call | solution.py:143
  204.6 0.0 copy-start.2
  204.6 0.0 copy-start
  204.6 2.0 reduce.2
  206.7 0.1 reshape.46
  206.8 2.0 collective-permute-start.4
  208.8 0.0 copy-done.2
  208.8 0.5 reduce.3
  209.2 0.1 reshape.47
  209.4 1.7 collective-permute-start.6
  211.1 0.0 copy-done
  211.1 1.0 slice_bitcast_fusion
  212.1 1.9 collective-permute-start.5
  214.0 16.2 %shard_map.46 = (f32[4,768,1]{2,1,0:T(8,128)}, f32[4,768,1]{2,1,0:T(8,128)}, f32[4,768,128]{2,1,0:T(8,128)}) custom-call(s32[2]{0:T(128)} %get-tuple-element.33.bounds_ref, bf16[128,3072]{1,0:T(8,128)(2,1)} %get-tuple-element.29.q_ref, bf16[2,64,64,1024]{3,2,1,0:T(8,128)(2,1)} %bitcast.114, bf16[2,64,64,1024]{3,2,1,0:T(8,128)(2,1)} %bitcast.115), custom_call_target="tpu_custom_call" | custom-call | flops 6442450944 | bytes 12320768 | tf_op jit(solution)/shard_map/pallas_call | solution.py:143
  230.2 0.0 copy-start.1
  230.2 2.0 reduce
  232.2 0.1 reshape.43
  232.3 1.7 collective-permute-start.1
  234.0 1.9 reduce.1
  235.9 0.1 reshape.44
  236.0 2.0 collective-permute-start.3
  238.0 0.0 copy-done.1
  238.0 0.1 slice_bitcast_fusion.3
  238.1 0.0 collective-permute-done.4
  238.1 1.7 collective-permute-start.2
  239.8 0.0 collective-permute-done.6
  239.8 0.1 fusion.11
  239.9 0.0 collective-permute-done.1
  239.9 1.5 collective-permute-done.3
  241.4 0.1 fusion.13
  241.6 0.0 copy-start.4
  241.6 0.0 collective-permute-done.5
  241.6 2.0 multiply_reduce_fusion
  243.7 14.4 %collective-permute-done.2 = f32[4,6,64,128]{3,2,1,0:T(8,128)S(1)} collective-permute-done((f32[4,6,64,128]{3,2,1,0:T(8,128)S(1)}, f32[4,6,64,128]{3,2,1,0:T(8,128)S(1)}, u32[]{:S(2)}, u32[]{:S(2)}) %collective-permute-start.2) | collective-permute-done | bytes 786464 | tf_op jit(solution)/shard_map/ppermute | solution.py:206
  258.1 1.0 multiply_reduce_fusion.1
  259.1 0.0 copy-done.4
  259.1 3.0 %fusion.4 = (bf16[64,4,6,128]{3,0,2,1:T(8,128)(2,1)S(1)}, bf16[64,4,6,128]{3,0,2,1:T(8,128)(2,1)S(1)}) fusion(f32[128]{0:T(128)S(1)} %copy-done.4, f32[4,6,64]{2,1,0:T(8,128)S(1)} %copy.112, f32[4,6,64,128]{3,2,1,0:T(8,128)S(1)} %collective-permute-done.2, f32[4,6,64]{2,1,0:T(8,128)S(1)} %copy.105, f32[4,6,64]{2,1,0:T(8,128)S(1)} %copy.102, ...), kind=kLoop, calls=%fused_computation.15 | loop fusion | flops 2359296 | bytes 3969536 | tf_op jit(solution)/shard_map/transpose | solution.py:187
  262.2 0.3 copy.113
  262.5 0.4 stack_reshape.6
  262.9 0.3 copy.129
  263.2 0.4 stack_reshape.7
  263.6 0.9 maximum_bitcast_fusion
  (20 shorter events, 0.1 us)
Async XLA Ops:
  6.5 29.1 %copy-start.3 = (bf16[2,1,64,3072]{3,2,1,0:T(8,128)(2,1)S(1)}, bf16[2,1,64,3072]{3,2,1,0:T(8,128)(2,1)}, u32[]{:S(2)}) copy-start(bf16[2,1,64,3072]{3,2,1,0:T(8,128)(2,1)} %param.4) | copy-start | bytes 2359300
  6.5 29.0 %all-gather.4.cloned.1.call-start = ((), (), s32[]{:S(2)}) async-start(), calls=%async_computation | async-start | bytes 1310720 | tf_op jit(solution)/shard_map/all_gather | solution.py:198
  8.3 126.9 %all-gather.6.cloned.1.call-start = ((), (), s32[]{:S(2)}) async-start(), calls=%async_computation.1 | async-start | bytes 17825792 | tf_op jit(solution)/shard_map/all_gather | solution.py:199
  35.6 28.1 %collective-permute-start = (bf16[2,1,64,3072]{3,2,1,0:T(8,128)(2,1)S(1)}, bf16[2,1,64,3072]{3,2,1,0:T(8,128)(2,1)S(1)}, u32[]{:S(2)}, u32[]{:S(2)}) collective-permute-start(bf16[2,1,64,3072]{3,2,1,0:T(8,128)(2,1)S(1)} %copy-done.3), channel_id=1, source_target_pairs={{0,1},{1,0},{2,3},{3,2},{4,5},{5,4},{6,7},{7,6},{8,9},{9,8},{10,11... | collective-permute-start | bytes 2359304 | tf_op jit(solution)/shard_map/ppermute | solution.py:195
  204.6 4.1 %copy-start.2 = (f32[4,768,1]{2,1,0:T(8,128)S(1)}, f32[4,768,1]{2,1,0:T(8,128)}, u32[]{:S(2)}) copy-start(f32[4,768,1]{2,1,0:T(8,128)} %get-tuple-element.22) | copy-start | bytes 36868
  204.6 6.5 %copy-start = (f32[4,768,128]{2,1,0:T(8,128)S(1)}, f32[4,768,128]{2,1,0:T(8,128)}, u32[]{:S(2)}) copy-start(f32[4,768,128]{2,1,0:T(8,128)} %get-tuple-element.20) | copy-start | bytes 4718596
  206.8 31.3 %collective-permute-start.4 = (f32[4,6,64,1]{2,3,1,0:T(1,128)S(1)}, f32[4,6,64,1]{2,3,1,0:T(1,128)S(1)}, u32[]{:S(2)}, u32[]{:S(2)}) collective-permute-start(f32[4,6,64,1]{2,3,1,0:T(1,128)S(1)} %slice_bitcast_fusion.8), channel_id=1, source_target_pairs={{0,1},{1,0},{2,3},{3,2},{4,5},{5,4},{6,7},{7,6},{8,9},{9,8},{10,11... | collective-permute-start | bytes 18440 | tf_op jit(solution)/shard_map/ppermute | solution.py:211
  209.4 30.4 %collective-permute-start.6 = (f32[4,6,64,1]{2,3,1,0:T(1,128)S(1)}, f32[4,6,64,1]{2,3,1,0:T(1,128)S(1)}, u32[]{:S(2)}, u32[]{:S(2)}) collective-permute-start(f32[4,6,64,1]{2,3,1,0:T(1,128)S(1)} %slice_bitcast_fusion.6), channel_id=1, source_target_pairs={{0,1},{1,0},{2,3},{3,2},{4,5},{5,4},{6,7},{7,6},{8,9},{9,8},{10,11... | collective-permute-start | bytes 18440 | tf_op jit(solution)/shard_map/ppermute | solution.py:211
  212.1 29.5 %collective-permute-start.5 = (f32[4,6,64,128]{3,2,1,0:T(8,128)}, f32[4,6,64,128]{3,2,1,0:T(8,128)}, u32[]{:S(2)}, u32[]{:S(2)}) collective-permute-start(f32[4,6,64,128]{3,2,1,0:T(8,128)} %slice_bitcast_fusion), channel_id=1, source_target_pairs={{0,1},{1,0},{2,3},{3,2},{4,5},{5,4},{6,7},{7,6},{8,9},{9,8},{10,11... | collective-permute-start | bytes 2359304 | tf_op jit(solution)/shard_map/ppermute | solution.py:211
  230.2 7.8 %copy-start.1 = (f32[4,768,128]{2,1,0:T(8,128)S(1)}, f32[4,768,128]{2,1,0:T(8,128)}, u32[]{:S(2)}) copy-start(f32[4,768,128]{2,1,0:T(8,128)} %get-tuple-element.14) | copy-start | bytes 4718596
  232.3 7.6 %collective-permute-start.1 = (f32[4,6,64,1]{2,3,1,0:T(1,128)S(1)}, f32[4,6,64,1]{2,3,1,0:T(1,128)S(1)}, u32[]{:S(2)}, u32[]{:S(2)}) collective-permute-start(f32[4,6,64,1]{2,3,1,0:T(1,128)S(1)} %slice_bitcast_fusion.12), channel_id=1, source_target_pairs={{0,1},{1,0},{2,3},{3,2},{4,5},{5,4},{6,7},{7,6},{8,9},{9,8},{10,11... | collective-permute-start | bytes 18440 | tf_op jit(solution)/shard_map/ppermute | solution.py:206
  236.0 5.4 %collective-permute-start.3 = (f32[4,6,64,1]{2,3,1,0:T(1,128)S(1)}, f32[4,6,64,1]{2,3,1,0:T(1,128)S(1)}, u32[]{:S(2)}, u32[]{:S(2)}) collective-permute-start(f32[4,6,64,1]{2,3,1,0:T(1,128)S(1)} %slice_bitcast_fusion.10), channel_id=1, source_target_pairs={{0,1},{1,0},{2,3},{3,2},{4,5},{5,4},{6,7},{7,6},{8,9},{9,8},{10,11... | collective-permute-start | bytes 18440 | tf_op jit(solution)/shard_map/ppermute | solution.py:206
  238.1 20.0 %collective-permute-start.2 = (f32[4,6,64,128]{3,2,1,0:T(8,128)S(1)}, f32[4,6,64,128]{3,2,1,0:T(8,128)S(1)}, u32[]{:S(2)}, u32[]{:S(2)}) collective-permute-start(f32[4,6,64,128]{3,2,1,0:T(8,128)S(1)} %slice_bitcast_fusion.3), channel_id=1, source_target_pairs={{0,1},{1,0},{2,3},{3,2},{4,5},{5,4},{6,7},{7,6},{8,9},{9,8},{10,11... | collective-permute-start | bytes 2359304 | tf_op jit(solution)/shard_map/ppermute | solution.py:206
  241.6 17.6 %copy-start.4 = (f32[128]{0:T(128)S(1)}, f32[128]{0:T(128)}, u32[]{:S(2)}) copy-start(f32[128]{0:T(128)} %param.7) | copy-start | bytes 1540
Sparse Core Ops, SparseCore 0:
  9.0 26.5 all-gather.3
  37.2 97.9 all-gather.5

commit v7 on v6

--- a/solution.py
+++ b/solution.py
@@ -172,6 +172,12 @@
     return mine, theirs
 
 
+def send_back(theirs, swap):
+    run_max, run_sum, acc = theirs
+    acc = lax.ppermute(acc.astype(jnp.bfloat16), "row", swap).astype(jnp.float32)
+    return [lax.ppermute(run_max, "row", swap), lax.ppermute(run_sum, "row", swap), acc]
+
+
 def finish(mine, theirs, gain):
     own_max, own_sum, own_acc = mine
     far_max, far_sum, far_acc = theirs
@@ -203,12 +209,12 @@
 
     early = attend(jnp.stack([zero, seq_index]), both_queries[0, 0], blocks, 0)
     early_mine, early_theirs = split_halves(early, own_rows)
-    early_back = [lax.ppermute(x, "row", swap) for x in early_theirs]
+    early_back = send_back(early_theirs, swap)
 
     state = attend(jnp.stack([zero, top]), both_queries[1, 0], blocks, 0)
     late = attend(jnp.stack([seq_index, top]), both_queries[1, 0], blocks, 1, state=state)
     late_mine, late_theirs = split_halves(late, own_rows)
-    late_back = [lax.ppermute(x, "row", swap) for x in late_theirs]
+    late_back = send_back(late_theirs, swap)
 
     early_out = finish(early_mine, early_back, gain)
     late_out = finish(late_mine, late_back, gain)

time: 276 us -> 272 us (0.986)
  waiting for transfers between devices: 137 us -> 128 us
  local copies, waits for them, and re-layouts: 4.33 us -> 8.88 us
    ppermute x6, waiting for transfers between devices: 15.9 us -> 6.98 us  [the longest x2 6.25 us: send_back(): lax.ppermute(acc.astype(jnp.bfloat16), 'row', swap).astype(jnp.float32)]
  transfers between devices with their start and end apart: 9 -> 9, of which waited for: 5 -> 5; matrix products, arithmetic and copies ran while one was open for 4% -> 5% of each run, Pallas kernels for 6% -> 6%
where the time goes in v7:
time: 272 us; the launch traced here: 267 us
  waiting for transfers between devices  128 us (47%)
  Pallas kernels  85.6 us (31%)
  other arithmetic  16.4 us (6%)
  starting transfers between devices  13.9 us (5%)
  between operations  13.7 us (5%)
  local copies, waits for them, and re-layouts  8.88 us (3%)
    pallas_call x3, Pallas kernels, attend(): pl.pallas_call(kernel, grid_spec=pltpu.PrefetchScalarGridSpec(num_scalar_...  85.6 us
    all_gather x1, waiting for transfers between devices, per_device(): blocks = lax.all_gather(blocks, 'inner', axis=2, tiled=False)  70.2 us
    all_gather x1, waiting for transfers between devices, per_device(): blocks = lax.all_gather(pair[:, 0], 'outer', axis=1, tiled=False)  27.2 us
    ppermute x1, waiting for transfers between devices, per_device(): partner_queries = lax.ppermute(queries, 'row', swap)  23.7 us
    pallas_call x4, other arithmetic, attend(): pl.pallas_call(kernel, grid_spec=pltpu.PrefetchScalarGridSpec(num_scalar_...  6.41 us
    ppermute x2, waiting for transfers between devices, send_back(): lax.ppermute(acc.astype(jnp.bfloat16), 'row', swap).astype(jnp.float32)  6.25 us
  transfers between devices with their start and end apart: 9, of which 5 were waited for; matrix products, arithmetic and copies ran while one was open for 5% of the time, Pallas kernels for 6%

profile of v7, /device:TPU:0, one launch (start us, length us, event | category | flops | bytes accessed | tf_op | source)
XLA Modules:
  0.0 266.6 jit_solution(787499422743178430)
XLA Ops:
  6.5 0.0 all-gather.4.cloned.1.call-start
  6.5 1.8 pad_maximum_fusion
  8.3 0.0 all-gather.4.cloned.1.call-update
  8.3 0.0 all-gather.6.cloned.1.call-start
  8.4 27.2 %all-gather.4.cloned.1.call-done = bf16[2,4,64,1024]{3,2,1,0:T(8,128)(2,1)} async-done(((bf16[2,1,64,1024]{3,2,1,0:T(8,128)(2,1)}), bf16[2,4,64,1024]{3,2,1,0:T(8,128)(2,1)}) %all-gather.4.cloned.1.call-update) | async-done | bytes 1048592 | tf_op jit(solution)/shard_map/all_gather | solution.py:204
  35.6 0.0 all-gather.6.cloned.1.call-update
  35.6 0.0 copy-done.4
  35.6 3.2 %collective-permute-start = (bf16[2,1,64,3072]{3,2,1,0:T(8,128)(2,1)S(1)}, bf16[2,1,64,3072]{3,2,1,0:T(8,128)(2,1)S(1)}, u32[]{:S(2)}, u32[]{:S(2)}) collective-permute-start(bf16[2,1,64,3072]{3,2,1,0:T(8,128)(2,1)S(1)} %copy-done.4), channel_id=1, source_target_pairs={{0,1},{1,0},{2,3},{3,2},{4,5},{5,4},{6,7},{7,6},{8,9},{9,8},{10,11... | collective-permute-start | bytes 2359304 | tf_op jit(solution)/shard_map/ppermute | solution.py:201
  38.8 0.5 iota_multiply_fusion.bounds_ref
  39.4 0.6 pad_add_fusion
  40.0 0.1 constant_dynamic-update-slice_fusion.1
  40.0 23.7 %collective-permute-done = bf16[2,1,64,3072]{3,2,1,0:T(8,128)(2,1)S(1)} collective-permute-done((bf16[2,1,64,3072]{3,2,1,0:T(8,128)(2,1)S(1)}, bf16[2,1,64,3072]{3,2,1,0:T(8,128)(2,1)S(1)}, u32[]{:S(2)}, u32[]{:S(2)}) %collective-permute-start) | collective-permute-done | bytes 786464 | tf_op jit(solution)/shard_map/ppermute | solution.py:201
  63.7 0.1 constant_dynamic-update-slice_fusion
  63.8 1.2 slice_bitcast_fusion.3
  65.0 70.2 %all-gather.6.cloned.1.call-done = bf16[2,4,1024,1024]{3,2,1,0:T(8,128)(2,1)} async-done(((bf16[2,4,64,1024]{3,2,1,0:T(8,128)(2,1)}), bf16[2,4,1024,1024]{3,2,1,0:T(8,128)(2,1)}) %all-gather.6.cloned.1.call-update) | async-done | bytes 16777232 | tf_op jit(solution)/shard_map/all_gather | solution.py:205
  135.2 34.3 %shard_map.47 = (f32[4,768,1]{2,1,0:T(8,128)}, f32[4,768,1]{2,1,0:T(8,128)}, f32[4,768,128]{2,1,0:T(8,128)}) custom-call(s32[2]{0:T(128)} %iota_multiply_fusion.bounds_ref, bf16[128,3072]{1,0:T(8,128)(2,1)} %get-tuple-element.30.q_ref, bf16[2,64,64,1024]{3,2,1,0:T(8,128)(2,1)} %bitcast.112, bf16[2,64,64,1024]{3,2,1,0:T(8,128)(2,1)} %bitcast.113), custom_call_target="tpu_custom_call" | custom-call | flops 6442450944 | bytes 12320768 | tf_op jit(solution)/shard_map/pallas_call | solution.py:143
  169.5 35.2 %shard_map.48 = (f32[4,768,1]{2,1,0:T(8,128)}, f32[4,768,1]{2,1,0:T(8,128)}, f32[4,768,128]{2,1,0:T(8,128)}) custom-call(s32[2]{0:T(128)} %get-tuple-element.34.bounds_ref, bf16[128,3072]{1,0:T(8,128)(2,1)} %get-tuple-element.30.q_ref, bf16[2,64,64,1024]{3,2,1,0:T(8,128)(2,1)} %bitcast.114, bf16[2,64,64,1024]{3,2,1,0:T(8,128)(2,1)} %bitcast.115, ...), custom_call_target="tpu_custom_call" | custom-call | flops 6442450944 | bytes 12320768 | tf_op jit(solution)/shard_map/pallas_call | solution.py:143
  204.7 2.0 reduce.2
  206.7 0.1 reshape.48
  206.8 0.0 copy-start.5
  206.8 0.6 slice_bitcast_fusion.6
  207.4 1.9 collective-permute-start.4
  209.3 0.0 copy-done.2
  209.3 0.5 reduce.3
  209.8 0.1 reshape.49
  209.9 0.0 copy-start.6
  209.9 0.6 slice_bitcast_fusion.4
  210.5 1.6 collective-permute-start.6
  212.2 0.0 copy-done.6
  212.2 0.0 copy-done
  212.2 0.8 fusion.5
  213.0 1.9 collective-permute-start.5
  214.9 16.2 %shard_map.46 = (f32[4,768,1]{2,1,0:T(8,128)}, f32[4,768,1]{2,1,0:T(8,128)}, f32[4,768,128]{2,1,0:T(8,128)}) custom-call(s32[2]{0:T(128)} %get-tuple-element.33.bounds_ref, bf16[128,3072]{1,0:T(8,128)(2,1)} %get-tuple-element.29.q_ref, bf16[2,64,64,1024]{3,2,1,0:T(8,128)(2,1)} %bitcast.116, bf16[2,64,64,1024]{3,2,1,0:T(8,128)(2,1)} %bitcast.117), custom_call_target="tpu_custom_call" | custom-call | flops 6442450944 | bytes 12320768 | tf_op jit(solution)/shard_map/pallas_call | solution.py:143
  231.0 0.0 copy-done.5
  231.1 2.0 reduce
  233.1 0.7 reshape.45
  233.8 1.3 slice_bitcast_fusion.10
  235.1 1.6 collective-permute-start.1
  236.8 1.9 reduce.1
  238.6 0.7 reshape.46
  239.4 0.7 slice_bitcast_fusion.8
  240.1 1.9 collective-permute-start.3
  241.9 0.0 copy-done.1
  242.0 0.1 fusion.4
  242.0 0.0 copy-start.7
  242.0 0.0 collective-permute-done.4
  242.0 1.7 collective-permute-start.2
  243.8 0.0 collective-permute-done.6
  243.8 0.8 fusion.13
  244.7 0.0 collective-permute-done.1
  244.7 0.7 collective-permute-done.3
  245.4 0.8 fusion.15
  246.3 0.0 collective-permute-done.5
  246.3 1.0 multiply_reduce_fusion
  247.4 6.2 %collective-permute-done.2 = bf16[4,6,64,128]{3,2,1,0:T(8,128)(2,1)S(1)} collective-permute-done((bf16[4,6,64,128]{3,2,1,0:T(8,128)(2,1)S(1)}, bf16[4,6,64,128]{3,2,1,0:T(8,128)(2,1)S(1)}, u32[]{:S(2)}, u32[]{:S(2)}) %collective-permute-start.2) | collective-permute-done | bytes 393248 | tf_op jit(solution)/shard_map/ppermute | solution.py:177
  253.6 1.0 multiply_reduce_fusion.1
  254.7 0.0 copy-done.7
  254.7 2.4 fusion.6
  257.1 0.3 copy.106
  257.4 0.4 stack_reshape.6
  257.8 0.3 copy-done.3
  258.1 0.3 copy.122
  258.4 0.4 stack_reshape.7
  258.8 0.9 maximum_bitcast_fusion
  (21 shorter events, 0.1 us)
Async XLA Ops:
  6.5 29.1 %copy-start.4 = (bf16[2,1,64,3072]{3,2,1,0:T(8,128)(2,1)S(1)}, bf16[2,1,64,3072]{3,2,1,0:T(8,128)(2,1)}, u32[]{:S(2)}) copy-start(bf16[2,1,64,3072]{3,2,1,0:T(8,128)(2,1)} %param.4) | copy-start | bytes 2359300
  6.5 29.0 %all-gather.4.cloned.1.call-start = ((), (), s32[]{:S(2)}) async-start(), calls=%async_computation | async-start | bytes 1310720 | tf_op jit(solution)/shard_map/all_gather | solution.py:204
  8.3 126.9 %all-gather.6.cloned.1.call-start = ((), (), s32[]{:S(2)}) async-start(), calls=%async_computation.1 | async-start | bytes 17825792 | tf_op jit(solution)/shard_map/all_gather | solution.py:205
  35.6 28.1 %collective-permute-start = (bf16[2,1,64,3072]{3,2,1,0:T(8,128)(2,1)S(1)}, bf16[2,1,64,3072]{3,2,1,0:T(8,128)(2,1)S(1)}, u32[]{:S(2)}, u32[]{:S(2)}) collective-permute-start(bf16[2,1,64,3072]{3,2,1,0:T(8,128)(2,1)S(1)} %copy-done.4), channel_id=1, source_target_pairs={{0,1},{1,0},{2,3},{3,2},{4,5},{5,4},{6,7},{7,6},{8,9},{9,8},{10,11... | collective-permute-start | bytes 2359304 | tf_op jit(solution)/shard_map/ppermute | solution.py:201
  204.7 4.6 %copy-start.2 = (f32[4,768,1]{2,1,0:T(8,128)S(1)}, f32[4,768,1]{2,1,0:T(8,128)}, u32[]{:S(2)}) copy-start(f32[4,768,1]{2,1,0:T(8,128)} %get-tuple-element.22) | copy-start | bytes 36868
  204.7 7.5 %copy-start = (f32[4,768,128]{2,1,0:T(8,128)S(1)}, f32[4,768,128]{2,1,0:T(8,128)}, u32[]{:S(2)}) copy-start(f32[4,768,128]{2,1,0:T(8,128)} %get-tuple-element.20) | copy-start | bytes 4718596
  206.8 24.2 %copy-start.5 = (f32[4,6,2,64,1]{3,2,1,0,4:T(2,128)}, f32[4,6,2,64,1]{3,2,1,0,4:T(2,128)S(1)}, u32[]{:S(2)}) copy-start(f32[4,6,2,64,1]{3,2,1,0,4:T(2,128)S(1)} %reshape.48) | copy-start | bytes 36868
  207.4 34.6 %collective-permute-start.4 = (f32[4,6,64,1]{2,3,1,0:T(1,128)}, f32[4,6,64,1]{2,3,1,0:T(1,128)}, u32[]{:S(2)}, u32[]{:S(2)}) collective-permute-start(f32[4,6,64,1]{2,3,1,0:T(1,128)} %slice_bitcast_fusion.6), channel_id=1, source_target_pairs={{0,1},{1,0},{2,3},{3,2},{4,5},{5,4},{6,7},{7,6},{8,9},{9,8},{10,11... | collective-permute-start | bytes 18440 | tf_op jit(solution)/shard_map/ppermute | solution.py:178
  209.9 2.3 copy-start.6
  210.5 33.2 %collective-permute-start.6 = (f32[4,6,64,1]{2,3,1,0:T(1,128)}, f32[4,6,64,1]{2,3,1,0:T(1,128)}, u32[]{:S(2)}, u32[]{:S(2)}) collective-permute-start(f32[4,6,64,1]{2,3,1,0:T(1,128)} %slice_bitcast_fusion.4), channel_id=1, source_target_pairs={{0,1},{1,0},{2,3},{3,2},{4,5},{5,4},{6,7},{7,6},{8,9},{9,8},{10,11... | collective-permute-start | bytes 18440 | tf_op jit(solution)/shard_map/ppermute | solution.py:178
  213.0 33.3 %collective-permute-start.5 = (bf16[4,6,64,128]{3,2,1,0:T(8,128)(2,1)}, bf16[4,6,64,128]{3,2,1,0:T(8,128)(2,1)S(1)}, u32[]{:S(2)}, u32[]{:S(2)}) collective-permute-start(bf16[4,6,64,128]{3,2,1,0:T(8,128)(2,1)} %fusion.5), channel_id=1, source_target_pairs={{0,1},{1,0},{2,3},{3,2},{4,5},{5,4},{6,7},{7,6},{8,9},{9,8},{10,11... | collective-permute-start | bytes 1179656 | tf_op jit(solution)/shard_map/ppermute | solution.py:177
  231.1 10.9 %copy-start.1 = (f32[4,768,128]{2,1,0:T(8,128)S(1)}, f32[4,768,128]{2,1,0:T(8,128)}, u32[]{:S(2)}) copy-start(f32[4,768,128]{2,1,0:T(8,128)} %get-tuple-element.14) | copy-start | bytes 4718596
  235.1 9.6 %collective-permute-start.1 = (f32[4,6,64,1]{2,3,1,0:T(1,128)}, f32[4,6,64,1]{2,3,1,0:T(1,128)}, u32[]{:S(2)}, u32[]{:S(2)}) collective-permute-start(f32[4,6,64,1]{2,3,1,0:T(1,128)} %slice_bitcast_fusion.10), channel_id=1, source_target_pairs={{0,1},{1,0},{2,3},{3,2},{4,5},{5,4},{6,7},{7,6},{8,9},{9,8},{10,11... | collective-permute-start | bytes 18440 | tf_op jit(solution)/shard_map/ppermute | solution.py:178
  240.1 5.3 %collective-permute-start.3 = (f32[4,6,64,1]{2,3,1,0:T(1,128)S(1)}, f32[4,6,64,1]{2,3,1,0:T(1,128)S(1)}, u32[]{:S(2)}, u32[]{:S(2)}) collective-permute-start(f32[4,6,64,1]{2,3,1,0:T(1,128)S(1)} %slice_bitcast_fusion.8), channel_id=1, source_target_pairs={{0,1},{1,0},{2,3},{3,2},{4,5},{5,4},{6,7},{7,6},{8,9},{9,8},{10,11... | collective-permute-start | bytes 18440 | tf_op jit(solution)/shard_map/ppermute | solution.py:178
  242.0 12.7 %copy-start.7 = (f32[128]{0:T(128)S(1)}, f32[128]{0:T(128)}, u32[]{:S(2)}) copy-start(f32[128]{0:T(128)} %param.7) | copy-start | bytes 1540
  242.0 11.6 %collective-permute-start.2 = (bf16[4,6,64,128]{3,2,1,0:T(8,128)(2,1)S(1)}, bf16[4,6,64,128]{3,2,1,0:T(8,128)(2,1)S(1)}, u32[]{:S(2)}, u32[]{:S(2)}) collective-permute-start(bf16[4,6,64,128]{3,2,1,0:T(8,128)(2,1)S(1)} %fusion.4), channel_id=1, source_target_pairs={{0,1},{1,0},{2,3},{3,2},{4,5},{5,4},{6,7},{7,6},{8,9},{9,8},{10,11... | collective-permute-start | bytes 1179656 | tf_op jit(solution)/shard_map/ppermute | solution.py:177
  257.1 1.0 copy-start.3
Sparse Core Ops, SparseCore 0:
  9.0 26.5 all-gather.3
  37.2 97.9 all-gather.5

commit v8 on v7

--- a/solution.py
+++ b/solution.py
@@ -35,9 +35,10 @@
     @pl.when(t == 0)
     def _init():
         vals_sc[:, HEAD_DIM:] = jnp.ones((vals_sc.shape[0], HEAD_DIM), jnp.bfloat16)
-        q_sc[...] = jnp.concatenate(
+        grouped = jnp.concatenate(
             [q_ref[:, j * HEAD_DIM:(j + 1) * HEAD_DIM] for j in range(GROUP)], axis=0
         )
+        q_sc[...] = (grouped.astype(jnp.float32) * EXP2_SCALE).astype(q_sc.dtype)
         if carry_in:
             m_sc[...] = m_in[0]
             l_sc[...] = l_in[0]
@@ -71,8 +72,8 @@
             scores = scores + bias
         running_max = m_sc[rows_here]
         new_max = jnp.maximum(running_max, jnp.max(scores, axis=1, keepdims=True))
-        raw_weights = jnp.exp2((scores - new_max) * EXP2_SCALE)
-        factor = jnp.exp2((running_max - new_max) * EXP2_SCALE)
+        raw_weights = jnp.exp2(scores - new_max)
+        factor = jnp.exp2(running_max - new_max)
         mixed = jnp.dot(
             raw_weights.astype(jnp.bfloat16), vals, preferred_element_type=jnp.float32
         )
@@ -182,8 +183,8 @@
     own_max, own_sum, own_acc = mine
     far_max, far_sum, far_acc = theirs
     top = jnp.maximum(own_max, far_max)
-    own_factor = jnp.exp2((own_max - top) * EXP2_SCALE)
-    far_factor = jnp.exp2((far_max - top) * EXP2_SCALE)
+    own_factor = jnp.exp2(own_max - top)
+    far_factor = jnp.exp2(far_max - top)
     total = own_sum * own_factor + far_sum * far_factor
     acc = own_acc * own_factor + far_acc * far_factor
     mixed = acc / total

time: 272 us -> 271 us (level)
  transfers between devices with their start and end apart: 9 -> 9, of which waited for: 5 -> 5; matrix products, arithmetic and copies ran while one was open for 5% -> 6% of each run, Pallas kernels for 6% -> 6%
where the time goes in v8:
time: 271 us; the launch traced here: 266 us
  waiting for transfers between devices  128 us (47%)
  Pallas kernels  84.7 us (31%)
  other arithmetic  16.4 us (6%)
  starting transfers between devices  13.9 us (5%)
  between operations  13.7 us (5%)
  local copies, waits for them, and re-layouts  8.88 us (3%)
    pallas_call x3, Pallas kernels, attend(): pl.pallas_call(kernel, grid_spec=pltpu.PrefetchScalarGridSpec(num_scalar_...  84.7 us
    all_gather x1, waiting for transfers between devices, per_device(): blocks = lax.all_gather(blocks, 'inner', axis=2, tiled=False)  70.2 us
    all_gather x1, waiting for transfers between devices, per_device(): blocks = lax.all_gather(pair[:, 0], 'outer', axis=1, tiled=False)  27.2 us
    ppermute x1, waiting for transfers between devices, per_device(): partner_queries = lax.ppermute(queries, 'row', swap)  23.7 us
    pallas_call x4, other arithmetic, attend(): pl.pallas_call(kernel, grid_spec=pltpu.PrefetchScalarGridSpec(num_scalar_...  6.41 us
    ppermute x2, waiting for transfers between devices, send_back(): lax.ppermute(acc.astype(jnp.bfloat16), 'row', swap).astype(jnp.float32)  6.37 us
  transfers between devices with their start and end apart: 9, of which 5 were waited for; matrix products, arithmetic and copies ran while one was open for 6% of the time, Pallas kernels for 6%

profile of v8, /device:TPU:0, one launch (start us, length us, event | category | flops | bytes accessed | tf_op | source)
XLA Modules:
  0.0 265.7 jit_solution(17162606027308346079)
XLA Ops:
  6.5 0.0 all-gather.4.cloned.1.call-start
  6.5 1.8 pad_maximum_fusion
  8.3 0.0 all-gather.4.cloned.1.call-update
  8.3 0.0 all-gather.6.cloned.1.call-start
  8.4 27.2 %all-gather.4.cloned.1.call-done = bf16[2,4,64,1024]{3,2,1,0:T(8,128)(2,1)} async-done(((bf16[2,1,64,1024]{3,2,1,0:T(8,128)(2,1)}), bf16[2,4,64,1024]{3,2,1,0:T(8,128)(2,1)}) %all-gather.4.cloned.1.call-update) | async-done | bytes 1048592 | tf_op jit(solution)/shard_map/all_gather | solution.py:205
  35.6 0.0 all-gather.6.cloned.1.call-update
  35.6 0.0 copy-done.4
  35.6 3.2 %collective-permute-start = (bf16[2,1,64,3072]{3,2,1,0:T(8,128)(2,1)S(1)}, bf16[2,1,64,3072]{3,2,1,0:T(8,128)(2,1)S(1)}, u32[]{:S(2)}, u32[]{:S(2)}) collective-permute-start(bf16[2,1,64,3072]{3,2,1,0:T(8,128)(2,1)S(1)} %copy-done.4), channel_id=1, source_target_pairs={{0,1},{1,0},{2,3},{3,2},{4,5},{5,4},{6,7},{7,6},{8,9},{9,8},{10,11... | collective-permute-start | bytes 2359304 | tf_op jit(solution)/shard_map/ppermute | solution.py:202
  38.8 0.5 iota_multiply_fusion.bounds_ref
  39.4 0.6 pad_add_fusion
  40.0 0.1 constant_dynamic-update-slice_fusion.1
  40.0 23.7 %collective-permute-done = bf16[2,1,64,3072]{3,2,1,0:T(8,128)(2,1)S(1)} collective-permute-done((bf16[2,1,64,3072]{3,2,1,0:T(8,128)(2,1)S(1)}, bf16[2,1,64,3072]{3,2,1,0:T(8,128)(2,1)S(1)}, u32[]{:S(2)}, u32[]{:S(2)}) %collective-permute-start) | collective-permute-done | bytes 786464 | tf_op jit(solution)/shard_map/ppermute | solution.py:202
  63.7 0.1 constant_dynamic-update-slice_fusion
  63.8 1.2 slice_bitcast_fusion.3
  65.0 70.2 %all-gather.6.cloned.1.call-done = bf16[2,4,1024,1024]{3,2,1,0:T(8,128)(2,1)} async-done(((bf16[2,4,64,1024]{3,2,1,0:T(8,128)(2,1)}), bf16[2,4,1024,1024]{3,2,1,0:T(8,128)(2,1)}) %all-gather.6.cloned.1.call-update) | async-done | bytes 16777232 | tf_op jit(solution)/shard_map/all_gather | solution.py:206
  135.2 33.8 %shard_map.47 = (f32[4,768,1]{2,1,0:T(8,128)}, f32[4,768,1]{2,1,0:T(8,128)}, f32[4,768,128]{2,1,0:T(8,128)}) custom-call(s32[2]{0:T(128)} %iota_multiply_fusion.bounds_ref, bf16[128,3072]{1,0:T(8,128)(2,1)} %get-tuple-element.30.q_ref, bf16[2,64,64,1024]{3,2,1,0:T(8,128)(2,1)} %bitcast.112, bf16[2,64,64,1024]{3,2,1,0:T(8,128)(2,1)} %bitcast.113), custom_call_target="tpu_custom_call" | custom-call | flops 6442450944 | bytes 12320768 | tf_op jit(solution)/shard_map/pallas_call | solution.py:144
  169.0 34.7 %shard_map.48 = (f32[4,768,1]{2,1,0:T(8,128)}, f32[4,768,1]{2,1,0:T(8,128)}, f32[4,768,128]{2,1,0:T(8,128)}) custom-call(s32[2]{0:T(128)} %get-tuple-element.34.bounds_ref, bf16[128,3072]{1,0:T(8,128)(2,1)} %get-tuple-element.30.q_ref, bf16[2,64,64,1024]{3,2,1,0:T(8,128)(2,1)} %bitcast.114, bf16[2,64,64,1024]{3,2,1,0:T(8,128)(2,1)} %bitcast.115, ...), custom_call_target="tpu_custom_call" | custom-call | flops 6442450944 | bytes 12320768 | tf_op jit(solution)/shard_map/pallas_call | solution.py:144
  203.7 2.0 reduce.2
  205.8 0.1 reshape.48
  205.9 0.0 copy-start.5
  205.9 0.6 slice_bitcast_fusion.6
  206.5 1.9 collective-permute-start.4
  208.3 0.0 copy-done.2
  208.4 0.5 reduce.3
  208.8 0.1 reshape.49
  208.9 0.0 copy-start.6
  208.9 0.6 slice_bitcast_fusion.4
  209.6 1.7 collective-permute-start.6
  211.2 0.0 copy-done.6
  211.2 0.0 copy-done
  211.2 0.8 fusion.5
  212.0 1.9 collective-permute-start.5
  213.9 16.2 %shard_map.46 = (f32[4,768,1]{2,1,0:T(8,128)}, f32[4,768,1]{2,1,0:T(8,128)}, f32[4,768,128]{2,1,0:T(8,128)}) custom-call(s32[2]{0:T(128)} %get-tuple-element.33.bounds_ref, bf16[128,3072]{1,0:T(8,128)(2,1)} %get-tuple-element.29.q_ref, bf16[2,64,64,1024]{3,2,1,0:T(8,128)(2,1)} %bitcast.116, bf16[2,64,64,1024]{3,2,1,0:T(8,128)(2,1)} %bitcast.117), custom_call_target="tpu_custom_call" | custom-call | flops 6442450944 | bytes 12320768 | tf_op jit(solution)/shard_map/pallas_call | solution.py:144
  230.1 0.0 copy-done.5
  230.1 2.0 reduce
  232.1 0.7 reshape.45
  232.8 1.3 slice_bitcast_fusion.10
  234.1 1.7 collective-permute-start.1
  235.8 1.9 reduce.1
  237.7 0.7 reshape.46
  238.4 0.7 slice_bitcast_fusion.8
  239.1 1.9 collective-permute-start.3
  241.0 0.0 copy-done.1
  241.0 0.1 fusion.4
  241.0 0.0 copy-start.7
  241.1 0.0 collective-permute-done.4
  241.1 1.7 collective-permute-start.2
  242.8 0.0 collective-permute-done.6
  242.8 0.8 fusion.13
  243.7 0.0 collective-permute-done.1
  243.7 0.7 collective-permute-done.3
  244.4 0.8 fusion.15
  245.3 0.0 collective-permute-done.5
  245.3 1.0 multiply_reduce_fusion
  246.4 6.4 %collective-permute-done.2 = bf16[4,6,64,128]{3,2,1,0:T(8,128)(2,1)S(1)} collective-permute-done((bf16[4,6,64,128]{3,2,1,0:T(8,128)(2,1)S(1)}, bf16[4,6,64,128]{3,2,1,0:T(8,128)(2,1)S(1)}, u32[]{:S(2)}, u32[]{:S(2)}) %collective-permute-start.2) | collective-permute-done | bytes 393248 | tf_op jit(solution)/shard_map/ppermute | solution.py:178
  252.7 1.0 multiply_reduce_fusion.1
  253.8 0.0 copy-done.7
  253.8 2.4 fusion.6
  256.2 0.3 copy.106
  256.5 0.4 stack_reshape.6
  257.0 0.3 copy-done.3
  257.2 0.3 copy.122
  257.5 0.4 stack_reshape.7
  258.0 0.9 maximum_bitcast_fusion
  (21 shorter events, 0.1 us)
Async XLA Ops:
  6.5 29.1 %copy-start.4 = (bf16[2,1,64,3072]{3,2,1,0:T(8,128)(2,1)S(1)}, bf16[2,1,64,3072]{3,2,1,0:T(8,128)(2,1)}, u32[]{:S(2)}) copy-start(bf16[2,1,64,3072]{3,2,1,0:T(8,128)(2,1)} %param.4) | copy-start | bytes 2359300
  6.5 29.0 %all-gather.4.cloned.1.call-start = ((), (), s32[]{:S(2)}) async-start(), calls=%async_computation | async-start | bytes 1310720 | tf_op jit(solution)/shard_map/all_gather | solution.py:205
  8.3 126.9 %all-gather.6.cloned.1.call-start = ((), (), s32[]{:S(2)}) async-start(), calls=%async_computation.1 | async-start | bytes 17825792 | tf_op jit(solution)/shard_map/all_gather | solution.py:206
  35.6 28.1 %collective-permute-start = (bf16[2,1,64,3072]{3,2,1,0:T(8,128)(2,1)S(1)}, bf16[2,1,64,3072]{3,2,1,0:T(8,128)(2,1)S(1)}, u32[]{:S(2)}, u32[]{:S(2)}) collective-permute-start(bf16[2,1,64,3072]{3,2,1,0:T(8,128)(2,1)S(1)} %copy-done.4), channel_id=1, source_target_pairs={{0,1},{1,0},{2,3},{3,2},{4,5},{5,4},{6,7},{7,6},{8,9},{9,8},{10,11... | collective-permute-start | bytes 2359304 | tf_op jit(solution)/shard_map/ppermute | solution.py:202
  203.7 4.6 %copy-start.2 = (f32[4,768,1]{2,1,0:T(8,128)S(1)}, f32[4,768,1]{2,1,0:T(8,128)}, u32[]{:S(2)}) copy-start(f32[4,768,1]{2,1,0:T(8,128)} %get-tuple-element.22) | copy-start | bytes 36868
  203.7 7.5 %copy-start = (f32[4,768,128]{2,1,0:T(8,128)S(1)}, f32[4,768,128]{2,1,0:T(8,128)}, u32[]{:S(2)}) copy-start(f32[4,768,128]{2,1,0:T(8,128)} %get-tuple-element.20) | copy-start | bytes 4718596
  205.9 24.2 %copy-start.5 = (f32[4,6,2,64,1]{3,2,1,0,4:T(2,128)}, f32[4,6,2,64,1]{3,2,1,0,4:T(2,128)S(1)}, u32[]{:S(2)}) copy-start(f32[4,6,2,64,1]{3,2,1,0,4:T(2,128)S(1)} %reshape.48) | copy-start | bytes 36868
  206.5 34.6 %collective-permute-start.4 = (f32[4,6,64,1]{2,3,1,0:T(1,128)}, f32[4,6,64,1]{2,3,1,0:T(1,128)}, u32[]{:S(2)}, u32[]{:S(2)}) collective-permute-start(f32[4,6,64,1]{2,3,1,0:T(1,128)} %slice_bitcast_fusion.6), channel_id=1, source_target_pairs={{0,1},{1,0},{2,3},{3,2},{4,5},{5,4},{6,7},{7,6},{8,9},{9,8},{10,11... | collective-permute-start | bytes 18440 | tf_op jit(solution)/shard_map/ppermute | solution.py:179
  208.9 2.3 copy-start.6
  209.6 33.3 %collective-permute-start.6 = (f32[4,6,64,1]{2,3,1,0:T(1,128)}, f32[4,6,64,1]{2,3,1,0:T(1,128)}, u32[]{:S(2)}, u32[]{:S(2)}) collective-permute-start(f32[4,6,64,1]{2,3,1,0:T(1,128)} %slice_bitcast_fusion.4), channel_id=1, source_target_pairs={{0,1},{1,0},{2,3},{3,2},{4,5},{5,4},{6,7},{7,6},{8,9},{9,8},{10,11... | collective-permute-start | bytes 18440 | tf_op jit(solution)/shard_map/ppermute | solution.py:179
  212.0 33.2 %collective-permute-start.5 = (bf16[4,6,64,128]{3,2,1,0:T(8,128)(2,1)}, bf16[4,6,64,128]{3,2,1,0:T(8,128)(2,1)S(1)}, u32[]{:S(2)}, u32[]{:S(2)}) collective-permute-start(bf16[4,6,64,128]{3,2,1,0:T(8,128)(2,1)} %fusion.5), channel_id=1, source_target_pairs={{0,1},{1,0},{2,3},{3,2},{4,5},{5,4},{6,7},{7,6},{8,9},{9,8},{10,11... | collective-permute-start | bytes 1179656 | tf_op jit(solution)/shard_map/ppermute | solution.py:178
  230.1 10.9 %copy-start.1 = (f32[4,768,128]{2,1,0:T(8,128)S(1)}, f32[4,768,128]{2,1,0:T(8,128)}, u32[]{:S(2)}) copy-start(f32[4,768,128]{2,1,0:T(8,128)} %get-tuple-element.14) | copy-start | bytes 4718596
  234.1 9.6 %collective-permute-start.1 = (f32[4,6,64,1]{2,3,1,0:T(1,128)}, f32[4,6,64,1]{2,3,1,0:T(1,128)}, u32[]{:S(2)}, u32[]{:S(2)}) collective-permute-start(f32[4,6,64,1]{2,3,1,0:T(1,128)} %slice_bitcast_fusion.10), channel_id=1, source_target_pairs={{0,1},{1,0},{2,3},{3,2},{4,5},{5,4},{6,7},{7,6},{8,9},{9,8},{10,11... | collective-permute-start | bytes 18440 | tf_op jit(solution)/shard_map/ppermute | solution.py:179
  239.1 5.3 %collective-permute-start.3 = (f32[4,6,64,1]{2,3,1,0:T(1,128)S(1)}, f32[4,6,64,1]{2,3,1,0:T(1,128)S(1)}, u32[]{:S(2)}, u32[]{:S(2)}) collective-permute-start(f32[4,6,64,1]{2,3,1,0:T(1,128)S(1)} %slice_bitcast_fusion.8), channel_id=1, source_target_pairs={{0,1},{1,0},{2,3},{3,2},{4,5},{5,4},{6,7},{7,6},{8,9},{9,8},{10,11... | collective-permute-start | bytes 18440 | tf_op jit(solution)/shard_map/ppermute | solution.py:179
  241.0 12.8 %copy-start.7 = (f32[128]{0:T(128)S(1)}, f32[128]{0:T(128)}, u32[]{:S(2)}) copy-start(f32[128]{0:T(128)} %param.7) | copy-start | bytes 1540
  241.1 11.7 %collective-permute-start.2 = (bf16[4,6,64,128]{3,2,1,0:T(8,128)(2,1)S(1)}, bf16[4,6,64,128]{3,2,1,0:T(8,128)(2,1)S(1)}, u32[]{:S(2)}, u32[]{:S(2)}) collective-permute-start(bf16[4,6,64,128]{3,2,1,0:T(8,128)(2,1)S(1)} %fusion.4), channel_id=1, source_target_pairs={{0,1},{1,0},{2,3},{3,2},{4,5},{5,4},{6,7},{7,6},{8,9},{9,8},{10,11... | collective-permute-start | bytes 1179656 | tf_op jit(solution)/shard_map/ppermute | solution.py:178
  256.2 1.0 copy-start.3
Sparse Core Ops, SparseCore 0:
  9.0 26.5 all-gather.3
  37.2 97.9 all-gather.5

commit v9 on v7

--- a/solution.py
+++ b/solution.py
@@ -19,10 +19,10 @@
 
 def attend_kernel(bounds_ref, q_ref, k_ref, v_ref, *rest, carry_in):
     if carry_in:
-        m_in, l_in, acc_in = rest[:3]
-        rest = rest[3:]
-    m_out, l_out, acc_out = rest[:3]
-    q_sc, m_sc, l_sc, acc_sc, vals_sc = rest[3:]
+        stats_in, acc_in = rest[:2]
+        rest = rest[2:]
+    stats_out, acc_out = rest[:2]
+    q_sc, m_sc, l_sc, acc_sc, vals_sc = rest[2:]
 
     t = pl.program_id(1)
     last = pl.num_programs(1) - 1
@@ -39,8 +39,8 @@
             [q_ref[:, j * HEAD_DIM:(j + 1) * HEAD_DIM] for j in range(GROUP)], axis=0
         )
         if carry_in:
-            m_sc[...] = m_in[0]
-            l_sc[...] = l_in[0]
+            m_sc[...] = stats_in[0][:, 0:1]
+            l_sc[...] = stats_in[0][:, 1:2]
             acc_sc[...] = acc_in[0]
         else:
             m_sc[...] = jnp.full(m_sc.shape, lowest_score, jnp.float32)
@@ -93,8 +93,8 @@
 
     @pl.when(t == last)
     def _done():
-        m_out[0] = m_sc[...]
-        l_out[0] = l_sc[...]
+        column = lax.broadcasted_iota(jnp.int32, (m_sc.shape[0], HEAD_DIM), 1)
+        stats_out[0] = jnp.where(column == 0, m_sc[...], jnp.where(column == 1, l_sc[...], 0.0))
         acc_out[0] = acc_sc[...]
 
 
@@ -121,13 +121,11 @@
     ]
     operands = [q, kv, kv]
     state_specs = [
-        pl.BlockSpec((1, qrows, 1), lambda g, t, b: (g, 0, 0)),
-        pl.BlockSpec((1, qrows, 1), lambda g, t, b: (g, 0, 0)),
+        pl.BlockSpec((1, qrows, HEAD_DIM), lambda g, t, b: (g, 0, 0)),
         pl.BlockSpec((1, qrows, HEAD_DIM), lambda g, t, b: (g, 0, 0)),
     ]
     state_shapes = [
-        jax.ShapeDtypeStruct((KV_HEADS, qrows, 1), jnp.float32),
-        jax.ShapeDtypeStruct((KV_HEADS, qrows, 1), jnp.float32),
+        jax.ShapeDtypeStruct((KV_HEADS, qrows, HEAD_DIM), jnp.float32),
         jax.ShapeDtypeStruct((KV_HEADS, qrows, HEAD_DIM), jnp.float32),
     ]
     if state is not None:
@@ -164,18 +162,17 @@
 
 
 def split_halves(state, own_rows):
-    mine, theirs = [], []
-    for part in state:
-        shaped = part.reshape(KV_HEADS, GROUP, 2, own_rows, part.shape[-1])
-        mine.append(shaped[:, :, 0])
-        theirs.append(shaped[:, :, 1])
+    stats, acc = (part.reshape(KV_HEADS, GROUP, 2, own_rows, HEAD_DIM) for part in state)
+    mine = [stats[:, :, 0, :, 0:1], stats[:, :, 0, :, 1:2], acc[:, :, 0]]
+    theirs = [stats[:, :, 1, :, 0:2], acc[:, :, 1]]
     return mine, theirs
 
 
 def send_back(theirs, swap):
-    run_max, run_sum, acc = theirs
+    stats, acc = theirs
     acc = lax.ppermute(acc.astype(jnp.bfloat16), "row", swap).astype(jnp.float32)
-    return [lax.ppermute(run_max, "row", swap), lax.ppermute(run_sum, "row", swap), acc]
+    stats = lax.ppermute(stats, "row", swap)
+    return [stats[..., 0:1], stats[..., 1:2], acc]
 
 
 def finish(mine, theirs, gain):

time: 272 us -> 298 us (1.096)
  local copies, waits for them, and re-layouts: 8.88 us -> 41 us
  waiting for transfers between devices: 128 us -> 123 us
  other arithmetic: 16.4 us -> 20 us
  starting transfers between devices: 13.9 us -> 10.3 us
    unnamed x17 -> x21, local copies, waits for them, and re-layouts: 0.36 us -> 17.6 us
    pallas_call x4 -> x0, other arithmetic: 6.41 us -> none  [attend(): pl.pallas_call(kernel, grid_spec=pltpu.PrefetchScalarGridSpec(num_scalar_...]
    ppermute x2, waiting for transfers between devices: 6.25 us -> 0.01 us  [send_back(): lax.ppermute(acc.astype(jnp.bfloat16), 'row', swap).astype(jnp.float32)]
    mul x4, local copies, waits for them, and re-layouts: 0.01 us -> 5.81 us  [finish(): acc = own_acc * own_factor + far_acc * far_factor]
    slice x0 -> x4, local copies, waits for them, and re-layouts: none -> 4.87 us  [the longest x2 4.73 us: split_halves(): mine = [stats[:, :, 0, :, 0:1], stats[:, :, 0, :, 1:2], acc[:, :, 0]]]
    mul x0 -> x2, other arithmetic: none -> 3.9 us  [finish(): acc = own_acc * own_factor + far_acc * far_factor]
    another operation x3, other arithmetic: 0.58 us -> 3.98 us
    ppermute x4 -> x2, starting transfers between devices: 7.06 us -> 3.77 us  [send_back(): stats = lax.ppermute(stats, 'row', swap)]
  transfers between devices with their start and end apart: 9 -> 7, of which waited for: 5 -> 4; matrix products, arithmetic and copies ran while one was open for 5% -> 11% of each run, Pallas kernels for 6% -> 0%
where the time goes in v9:
time: 298 us; the launch traced here: 294 us
  waiting for transfers between devices  123 us (41%)
  Pallas kernels  86 us (29%)
  local copies, waits for them, and re-layouts  41 us (14%)
  other arithmetic  20 us (7%)
  between operations  13.5 us (5%)
  starting transfers between devices  10.3 us (3%)
    pallas_call x3, Pallas kernels, attend(): pl.pallas_call(kernel, grid_spec=pltpu.PrefetchScalarGridSpec(num_scalar_...  86 us
    all_gather x1, waiting for transfers between devices, per_device(): blocks = lax.all_gather(blocks, 'inner', axis=2, tiled=False)  70.1 us
    all_gather x1, waiting for transfers between devices, per_device(): blocks = lax.all_gather(pair[:, 0], 'outer', axis=1, tiled=False)  27.2 us
    ppermute x1, waiting for transfers between devices, per_device(): partner_queries = lax.ppermute(queries, 'row', swap)  23.6 us
    unnamed x21, local copies, waits for them, and re-layouts  17.6 us
  transfers between devices with their start and end apart: 7, of which 4 were waited for; matrix products, arithmetic and copies ran while one was open for 11% of the time, Pallas kernels for 0%

profile of v9, /device:TPU:0, one launch (start us, length us, event | category | flops | bytes accessed | tf_op | source)
XLA Modules:
  0.0 293.9 jit_solution(7993932049390060471)
XLA Ops:
  6.5 0.0 all-gather.4.cloned.1.call-start
  6.5 1.8 pad_maximum_fusion
  8.3 0.0 all-gather.4.cloned.1.call-update
  8.3 0.0 all-gather.6.cloned.1.call-start
  8.4 27.2 %all-gather.4.cloned.1.call-done = bf16[2,4,64,1024]{3,2,1,0:T(8,128)(2,1)} async-done(((bf16[2,1,64,1024]{3,2,1,0:T(8,128)(2,1)}), bf16[2,4,64,1024]{3,2,1,0:T(8,128)(2,1)}) %all-gather.4.cloned.1.call-update) | async-done | bytes 1048592 | tf_op jit(solution)/shard_map/all_gather | solution.py:201
  35.6 0.0 all-gather.6.cloned.1.call-update
  35.6 0.0 copy-done.5
  35.6 3.2 %collective-permute-start = (bf16[2,1,64,3072]{3,2,1,0:T(8,128)(2,1)S(1)}, bf16[2,1,64,3072]{3,2,1,0:T(8,128)(2,1)S(1)}, u32[]{:S(2)}, u32[]{:S(2)}) collective-permute-start(bf16[2,1,64,3072]{3,2,1,0:T(8,128)(2,1)S(1)} %copy-done.5), channel_id=1, source_target_pairs={{0,1},{1,0},{2,3},{3,2},{4,5},{5,4},{6,7},{7,6},{8,9},{9,8},{10,11... | collective-permute-start | bytes 2359304 | tf_op jit(solution)/shard_map/ppermute | solution.py:198
  38.8 0.6 iota_multiply_fusion.bounds_ref
  39.4 0.6 pad_add_fusion
  40.0 0.1 constant_dynamic-update-slice_fusion.1
  40.1 23.6 %collective-permute-done = bf16[2,1,64,3072]{3,2,1,0:T(8,128)(2,1)S(1)} collective-permute-done((bf16[2,1,64,3072]{3,2,1,0:T(8,128)(2,1)S(1)}, bf16[2,1,64,3072]{3,2,1,0:T(8,128)(2,1)S(1)}, u32[]{:S(2)}, u32[]{:S(2)}) %collective-permute-start) | collective-permute-done | bytes 786464 | tf_op jit(solution)/shard_map/ppermute | solution.py:198
  63.7 0.1 constant_dynamic-update-slice_fusion
  63.8 1.3 slice_bitcast_fusion.3
  65.0 70.1 %all-gather.6.cloned.1.call-done = bf16[2,4,1024,1024]{3,2,1,0:T(8,128)(2,1)} async-done(((bf16[2,4,64,1024]{3,2,1,0:T(8,128)(2,1)}), bf16[2,4,1024,1024]{3,2,1,0:T(8,128)(2,1)}) %all-gather.6.cloned.1.call-update) | async-done | bytes 16777232 | tf_op jit(solution)/shard_map/all_gather | solution.py:202
  135.2 34.9 %shard_map.47 = (f32[4,768,128]{2,1,0:T(8,128)}, f32[4,768,128]{2,1,0:T(8,128)}) custom-call(s32[2]{0:T(128)} %iota_multiply_fusion.bounds_ref, bf16[128,3072]{1,0:T(8,128)(2,1)} %get-tuple-element.20.q_ref, bf16[2,64,64,1024]{3,2,1,0:T(8,128)(2,1)} %bitcast.93, bf16[2,64,64,1024]{3,2,1,0:T(8,128)(2,1)} %bitcast.94), custom_call_target="tpu_custom_call" | custom-call | flops 6442450944 | bytes 12320768 | tf_op jit(solution)/shard_map/pallas_call | solution.py:141
  170.0 35.9 %shard_map.48 = (f32[4,768,128]{2,1,0:T(8,128)}, f32[4,768,128]{2,1,0:T(8,128)}) custom-call(s32[2]{0:T(128)} %get-tuple-element.32.bounds_ref, bf16[128,3072]{1,0:T(8,128)(2,1)} %get-tuple-element.20.q_ref, bf16[2,64,64,1024]{3,2,1,0:T(8,128)(2,1)} %bitcast.95, bf16[2,64,64,1024]{3,2,1,0:T(8,128)(2,1)} %bitcast.96, ...), custom_call_target="tpu_custom_call" | custom-call | flops 6442450944 | bytes 12320768 | tf_op jit(solution)/shard_map/pallas_call | solution.py:141
  205.9 2.9 %fusion.25 = (f32[4,6,1,64,1]{4,3,2,1,0:T(8,128)}, f32[4,6,1,64,1]{4,3,2,1,0:T(8,128)}) fusion(f32[4,6,2,64,128]{4,3,2,1,0:T(8,128)} %bitcast.99), kind=kLoop, calls=%fused_computation.51 | loop fusion | bytes 24576 | tf_op jit(solution)/shard_map/slice | solution.py:166
  208.9 0.1 slice.78
  208.9 15.3 %shard_map.46 = (f32[4,768,128]{2,1,0:T(8,128)}, f32[4,768,128]{2,1,0:T(8,128)}) custom-call(s32[2]{0:T(128)} %get-tuple-element.31.bounds_ref, bf16[128,3072]{1,0:T(8,128)(2,1)} %get-tuple-element.19.q_ref, bf16[2,64,64,1024]{3,2,1,0:T(8,128)(2,1)} %bitcast.97, bf16[2,64,64,1024]{3,2,1,0:T(8,128)(2,1)} %bitcast.98), custom_call_target="tpu_custom_call" | custom-call | flops 6442450944 | bytes 12320768 | tf_op jit(solution)/shard_map/pallas_call | solution.py:141
  224.3 1.8 fusion.24
  226.0 0.1 copy-done.1
  226.1 0.1 slice.70
  226.2 1.4 copy.79
  227.6 0.8 copy.63
  228.4 3.4 %copy.76 = f32[4,6,1,64,1]{1,0,3,4,2:T(4,128)} copy(f32[4,6,1,64,1]{4,3,2,1,0:T(8,128)} %get-tuple-element.21) | data formatting | bytes 12288
  231.8 2.5 copy.77
  234.2 1.9 collective-permute-start.3
  236.1 1.9 fusion.5
  238.1 1.6 collective-permute-start.4
  239.7 2.3 copy.72
  242.0 2.3 copy.74
  244.2 2.5 copy.73
  246.7 1.9 collective-permute-start.1
  248.6 0.8 fusion.4
  249.4 1.6 collective-permute-start.2
  251.0 0.0 collective-permute-done.3
  251.0 1.9 fusion.21
  253.0 1.0 copy.59
  254.0 1.6 copy.61
  255.6 1.6 copy.64
  257.2 2.1 collective-permute-done.1
  259.3 2.0 fusion.23
  261.2 1.6 copy.49
  262.8 1.6 copy.50
  264.4 1.6 copy.52
  266.0 0.0 collective-permute-done.4
  266.0 0.0 copy-done.2
  266.0 2.4 multiply_reduce_fusion
  268.4 1.5 copy.70
  269.9 1.7 sqrt_multiply_fusion
  271.6 1.6 copy.66
  273.2 0.0 collective-permute-done.2
  273.2 2.6 multiply_reduce_fusion.1
  275.8 1.5 copy.69
  277.3 1.7 sqrt_multiply_fusion.1
  279.0 1.6 copy.54
  280.6 3.8 %fusion.6 = (bf16[64,4,6,128]{3,0,2,1:T(8,128)(2,1)S(1)}, bf16[64,4,6,128]{3,0,2,1:T(8,128)(2,1)}) fusion(f32[128]{0:T(128)} %param.7, f32[4,6,64]{2,1,0:T(8,128)} %copy.54, f32[4,6,64]{2,1,0:T(8,128)} %copy.50, bf16[4,6,64,128]{3,2,1,0:T(8,128)(2,1)} %collective-permute-done.2, f32[4,6,64]{2,1,0:T(8,128)} %copy.49, f32[4,6,2,64,128]{4,3,2,1,0:T(8,128)S(1)} %bitcast.108, ...), kind=kLoop, calls=%fused_computation.17 | loop fusion | flops 2752512 | bytes 3183104 | tf_op jit(solution)/shard_map/transpose | solution.py:190
  284.4 0.3 copy.55
  284.7 0.4 stack_reshape.6
  285.1 0.3 copy-done.4
  285.4 0.3 copy.67
  285.7 0.4 stack_reshape.7
  286.1 0.9 maximum_bitcast_fusion
  (8 shorter events, 0.0 us)
Async XLA Ops:
  6.5 29.1 %copy-start.5 = (bf16[2,1,64,3072]{3,2,1,0:T(8,128)(2,1)S(1)}, bf16[2,1,64,3072]{3,2,1,0:T(8,128)(2,1)}, u32[]{:S(2)}) copy-start(bf16[2,1,64,3072]{3,2,1,0:T(8,128)(2,1)} %param.4) | copy-start | bytes 2359300
  6.5 29.0 %all-gather.4.cloned.1.call-start = ((), (), s32[]{:S(2)}) async-start(), calls=%async_computation | async-start | bytes 1310720 | tf_op jit(solution)/shard_map/all_gather | solution.py:201
  8.3 126.9 %all-gather.6.cloned.1.call-start = ((), (), s32[]{:S(2)}) async-start(), calls=%async_computation.1 | async-start | bytes 17825792 | tf_op jit(solution)/shard_map/all_gather | solution.py:202
  35.6 28.1 %collective-permute-start = (bf16[2,1,64,3072]{3,2,1,0:T(8,128)(2,1)S(1)}, bf16[2,1,64,3072]{3,2,1,0:T(8,128)(2,1)S(1)}, u32[]{:S(2)}, u32[]{:S(2)}) collective-permute-start(bf16[2,1,64,3072]{3,2,1,0:T(8,128)(2,1)S(1)} %copy-done.5), channel_id=1, source_target_pairs={{0,1},{1,0},{2,3},{3,2},{4,5},{5,4},{6,7},{7,6},{8,9},{9,8},{10,11... | collective-permute-start | bytes 2359304 | tf_op jit(solution)/shard_map/ppermute | solution.py:198
  205.9 3.0 %copy-start = (f32[4,768,128]{2,1,0:T(8,128)S(1)}, f32[4,768,128]{2,1,0:T(8,128)}, u32[]{:S(2)}) copy-start(f32[4,768,128]{2,1,0:T(8,128)} %get-tuple-element.16) | copy-start | bytes 4718596
  224.2 1.9 copy-start.1
  234.2 16.8 %collective-permute-start.3 = (f32[4,6,64,2]{1,0,2,3:T(4,128)}, f32[4,6,64,2]{1,0,2,3:T(4,128)}, u32[]{:S(2)}, u32[]{:S(2)}) collective-permute-start(f32[4,6,64,2]{1,0,2,3:T(4,128)} %bitcast.19), channel_id=1, source_target_pairs={{0,1},{1,0},{2,3},{3,2},{4,5},{5,4},{6,7},{7,6},{8,9},{9,8},{10,11... | collective-permute-start | bytes 36872 | tf_op jit(solution)/shard_map/ppermute | solution.py:174
  238.1 28.0 %collective-permute-start.4 = (bf16[4,6,64,128]{3,2,1,0:T(8,128)(2,1)}, bf16[4,6,64,128]{3,2,1,0:T(8,128)(2,1)S(1)}, u32[]{:S(2)}, u32[]{:S(2)}) collective-permute-start(bf16[4,6,64,128]{3,2,1,0:T(8,128)(2,1)} %fusion.5), channel_id=1, source_target_pairs={{0,1},{1,0},{2,3},{3,2},{4,5},{5,4},{6,7},{7,6},{8,9},{9,8},{10,11... | collective-permute-start | bytes 1179656 | tf_op jit(solution)/shard_map/ppermute | solution.py:173
  242.0 6.6 %copy-start.3 = (f32[4,768,128]{2,1,0:T(8,128)S(1)}, f32[4,768,128]{2,1,0:T(8,128)}, u32[]{:S(2)}) copy-start(f32[4,768,128]{2,1,0:T(8,128)} %get-tuple-element.11) | copy-start | bytes 4718596
  246.7 12.6 %collective-permute-start.1 = (f32[4,6,64,2]{1,0,2,3:T(4,128)}, f32[4,6,64,2]{1,0,2,3:T(4,128)}, u32[]{:S(2)}, u32[]{:S(2)}) collective-permute-start(f32[4,6,64,2]{1,0,2,3:T(4,128)} %bitcast.7), channel_id=1, source_target_pairs={{0,1},{1,0},{2,3},{3,2},{4,5},{5,4},{6,7},{7,6},{8,9},{9,8},{10,11... | collective-permute-start | bytes 36872 | tf_op jit(solution)/shard_map/ppermute | solution.py:174
  248.6 17.5 %copy-start.2 = (f32[4,768,128]{2,1,0:T(8,128)S(1)}, f32[4,768,128]{2,1,0:T(8,128)}, u32[]{:S(2)}) copy-start(f32[4,768,128]{2,1,0:T(8,128)} %get-tuple-element.15) | copy-start | bytes 4718596
  249.4 23.8 %collective-permute-start.2 = (bf16[4,6,64,128]{3,2,1,0:T(8,128)(2,1)}, bf16[4,6,64,128]{3,2,1,0:T(8,128)(2,1)}, u32[]{:S(2)}, u32[]{:S(2)}) collective-permute-start(bf16[4,6,64,128]{3,2,1,0:T(8,128)(2,1)} %fusion.4), channel_id=1, source_target_pairs={{0,1},{1,0},{2,3},{3,2},{4,5},{5,4},{6,7},{7,6},{8,9},{9,8},{10,11... | collective-permute-start | bytes 1179656 | tf_op jit(solution)/shard_map/ppermute | solution.py:173
  284.4 1.0 copy-start.4
Sparse Core Ops, SparseCore 0:
  9.0 26.5 all-gather.3
  37.2 97.9 all-gather.5

commit v10 on v7

--- a/solution.py
+++ b/solution.py
@@ -175,7 +175,8 @@
 def send_back(theirs, swap):
     run_max, run_sum, acc = theirs
     acc = lax.ppermute(acc.astype(jnp.bfloat16), "row", swap).astype(jnp.float32)
-    return [lax.ppermute(run_max, "row", swap), lax.ppermute(run_sum, "row", swap), acc]
+    stats = lax.ppermute(jnp.concatenate([run_max, run_sum], axis=-1), "row", swap)
+    return [stats[..., 0:1], stats[..., 1:2], acc]
 
 
 def finish(mine, theirs, gain):

time: 272 us -> 269 us (0.989)
  starting transfers between devices: 13.9 us -> 10.5 us
    ppermute x4 -> x2, starting transfers between devices: 7.06 us -> 3.84 us  [send_back(): lax.ppermute(jnp.concatenate([run_max, run_sum], axis=-1), 'row', swap)]
  transfers between devices with their start and end apart: 9 -> 7, of which waited for: 5 -> 5; matrix products, arithmetic and copies ran while one was open for 5% -> 5% of each run, Pallas kernels for 6% -> 6%
where the time goes in v10:
time: 269 us; the launch traced here: 264 us
  waiting for transfers between devices  128 us (48%)
  Pallas kernels  85.6 us (32%)
  other arithmetic  17.8 us (7%)
  between operations  13.7 us (5%)
  starting transfers between devices  10.5 us (4%)
  local copies, waits for them, and re-layouts  7.69 us (3%)
    pallas_call x3, Pallas kernels, attend(): pl.pallas_call(kernel, grid_spec=pltpu.PrefetchScalarGridSpec(num_scalar_...  85.6 us
    all_gather x1, waiting for transfers between devices, per_device(): blocks = lax.all_gather(blocks, 'inner', axis=2, tiled=False)  70.2 us
    all_gather x1, waiting for transfers between devices, per_device(): blocks = lax.all_gather(pair[:, 0], 'outer', axis=1, tiled=False)  27.2 us
    ppermute x1, waiting for transfers between devices, per_device(): partner_queries = lax.ppermute(queries, 'row', swap)  23.7 us
    ppermute x2, waiting for transfers between devices, send_back(): lax.ppermute(acc.astype(jnp.bfloat16), 'row', swap).astype(jnp.float32)  6.68 us
    pallas_call x4, other arithmetic, attend(): pl.pallas_call(kernel, grid_spec=pltpu.PrefetchScalarGridSpec(num_scalar_...  6.41 us
  transfers between devices with their start and end apart: 7, of which 5 were waited for; matrix products, arithmetic and copies ran while one was open for 5% of the time, Pallas kernels for 6%

profile of v10, /device:TPU:0, one launch (start us, length us, event | category | flops | bytes accessed | tf_op | source)
XLA Modules:
  0.0 263.8 jit_solution(39480560267979836)
XLA Ops:
  6.5 0.0 all-gather.4.cloned.1.call-start
  6.5 1.8 pad_maximum_fusion
  8.3 0.0 all-gather.4.cloned.1.call-update
  8.3 0.0 all-gather.6.cloned.1.call-start
  8.4 27.2 %all-gather.4.cloned.1.call-done = bf16[2,4,64,1024]{3,2,1,0:T(8,128)(2,1)} async-done(((bf16[2,1,64,1024]{3,2,1,0:T(8,128)(2,1)}), bf16[2,4,64,1024]{3,2,1,0:T(8,128)(2,1)}) %all-gather.4.cloned.1.call-update) | async-done | bytes 1048592 | tf_op jit(solution)/shard_map/all_gather | solution.py:205
  35.6 0.0 all-gather.6.cloned.1.call-update
  35.6 0.0 copy-done.4
  35.6 3.2 %collective-permute-start = (bf16[2,1,64,3072]{3,2,1,0:T(8,128)(2,1)S(1)}, bf16[2,1,64,3072]{3,2,1,0:T(8,128)(2,1)S(1)}, u32[]{:S(2)}, u32[]{:S(2)}) collective-permute-start(bf16[2,1,64,3072]{3,2,1,0:T(8,128)(2,1)S(1)} %copy-done.4), channel_id=1, source_target_pairs={{0,1},{1,0},{2,3},{3,2},{4,5},{5,4},{6,7},{7,6},{8,9},{9,8},{10,11... | collective-permute-start | bytes 2359304 | tf_op jit(solution)/shard_map/ppermute | solution.py:202
  38.8 0.5 iota_multiply_fusion.bounds_ref
  39.4 0.6 pad_add_fusion
  40.0 0.1 constant_dynamic-update-slice_fusion.1
  40.0 23.7 %collective-permute-done = bf16[2,1,64,3072]{3,2,1,0:T(8,128)(2,1)S(1)} collective-permute-done((bf16[2,1,64,3072]{3,2,1,0:T(8,128)(2,1)S(1)}, bf16[2,1,64,3072]{3,2,1,0:T(8,128)(2,1)S(1)}, u32[]{:S(2)}, u32[]{:S(2)}) %collective-permute-start) | collective-permute-done | bytes 786464 | tf_op jit(solution)/shard_map/ppermute | solution.py:202
  63.7 0.1 constant_dynamic-update-slice_fusion
  63.8 1.2 slice_bitcast_fusion.3
  65.0 70.2 %all-gather.6.cloned.1.call-done = bf16[2,4,1024,1024]{3,2,1,0:T(8,128)(2,1)} async-done(((bf16[2,4,64,1024]{3,2,1,0:T(8,128)(2,1)}), bf16[2,4,1024,1024]{3,2,1,0:T(8,128)(2,1)}) %all-gather.6.cloned.1.call-update) | async-done | bytes 16777232 | tf_op jit(solution)/shard_map/all_gather | solution.py:206
  135.2 34.2 %shard_map.47 = (f32[4,768,1]{2,1,0:T(8,128)}, f32[4,768,1]{2,1,0:T(8,128)}, f32[4,768,128]{2,1,0:T(8,128)}) custom-call(s32[2]{0:T(128)} %iota_multiply_fusion.bounds_ref, bf16[128,3072]{1,0:T(8,128)(2,1)} %get-tuple-element.30.q_ref, bf16[2,64,64,1024]{3,2,1,0:T(8,128)(2,1)} %bitcast.112, bf16[2,64,64,1024]{3,2,1,0:T(8,128)(2,1)} %bitcast.113), custom_call_target="tpu_custom_call" | custom-call | flops 6442450944 | bytes 12320768 | tf_op jit(solution)/shard_map/pallas_call | solution.py:143
  169.4 35.2 %shard_map.48 = (f32[4,768,1]{2,1,0:T(8,128)}, f32[4,768,1]{2,1,0:T(8,128)}, f32[4,768,128]{2,1,0:T(8,128)}) custom-call(s32[2]{0:T(128)} %get-tuple-element.34.bounds_ref, bf16[128,3072]{1,0:T(8,128)(2,1)} %get-tuple-element.30.q_ref, bf16[2,64,64,1024]{3,2,1,0:T(8,128)(2,1)} %bitcast.114, bf16[2,64,64,1024]{3,2,1,0:T(8,128)(2,1)} %bitcast.115, ...), custom_call_target="tpu_custom_call" | custom-call | flops 6442450944 | bytes 12320768 | tf_op jit(solution)/shard_map/pallas_call | solution.py:143
  204.7 0.0 copy-start.2
  204.7 0.0 copy-start
  204.7 2.0 reduce.3
  206.7 0.1 reshape.49
  206.8 0.0 copy-start.5
  206.8 0.0 copy-done.2
  206.8 0.5 reduce.2
  207.3 0.1 reshape.48
  207.4 0.0 copy-start.6
  207.5 0.6 pad_maximum_fusion.2
  208.1 1.9 collective-permute-start.3
  210.0 0.0 copy-done.6
  210.0 0.0 copy-done
  210.0 0.8 fusion.5
  210.8 1.6 collective-permute-start.4
  212.5 16.2 %shard_map.46 = (f32[4,768,1]{2,1,0:T(8,128)}, f32[4,768,1]{2,1,0:T(8,128)}, f32[4,768,128]{2,1,0:T(8,128)}) custom-call(s32[2]{0:T(128)} %get-tuple-element.33.bounds_ref, bf16[128,3072]{1,0:T(8,128)(2,1)} %get-tuple-element.29.q_ref, bf16[2,64,64,1024]{3,2,1,0:T(8,128)(2,1)} %bitcast.116, bf16[2,64,64,1024]{3,2,1,0:T(8,128)(2,1)} %bitcast.117), custom_call_target="tpu_custom_call" | custom-call | flops 6442450944 | bytes 12320768 | tf_op jit(solution)/shard_map/pallas_call | solution.py:143
  228.6 0.0 copy-done.5
  228.6 0.0 copy-start.1
  228.6 2.0 reduce
  230.6 0.7 reshape.45
  231.3 1.3 slice_bitcast_fusion.10
  232.7 1.9 reduce.1
  234.6 0.7 reshape.46
  235.3 0.7 slice_bitcast_fusion.9
  236.0 0.7 pad_maximum_fusion.1
  236.7 2.0 collective-permute-start.1
  238.7 0.0 copy-done.1
  238.7 0.1 fusion.4
  238.8 0.0 copy-start.7
  238.8 1.7 collective-permute-start.2
  240.5 0.0 collective-permute-done.3
  240.5 0.9 fusion.12
  241.5 0.7 collective-permute-done.1
  242.2 0.8 fusion.14
  243.0 0.0 collective-permute-done.4
  243.0 1.0 multiply_reduce_fusion
  244.1 6.7 %collective-permute-done.2 = bf16[4,6,64,128]{3,2,1,0:T(8,128)(2,1)S(1)} collective-permute-done((bf16[4,6,64,128]{3,2,1,0:T(8,128)(2,1)S(1)}, bf16[4,6,64,128]{3,2,1,0:T(8,128)(2,1)S(1)}, u32[]{:S(2)}, u32[]{:S(2)}) %collective-permute-start.2) | collective-permute-done | bytes 393248 | tf_op jit(solution)/shard_map/ppermute | solution.py:177
  250.8 1.0 multiply_reduce_fusion.1
  251.9 0.0 copy-done.7
  251.9 2.4 fusion.6
  254.3 0.0 copy-start.3
  254.3 0.3 copy.106
  254.6 0.4 stack_reshape.6
  255.0 0.3 copy-done.3
  255.3 0.3 copy.122
  255.6 0.4 stack_reshape.7
  256.0 0.9 maximum_bitcast_fusion
  (19 shorter events, 0.1 us)
Async XLA Ops:
  6.5 29.1 %copy-start.4 = (bf16[2,1,64,3072]{3,2,1,0:T(8,128)(2,1)S(1)}, bf16[2,1,64,3072]{3,2,1,0:T(8,128)(2,1)}, u32[]{:S(2)}) copy-start(bf16[2,1,64,3072]{3,2,1,0:T(8,128)(2,1)} %param.4) | copy-start | bytes 2359300
  6.5 29.0 %all-gather.4.cloned.1.call-start = ((), (), s32[]{:S(2)}) async-start(), calls=%async_computation | async-start | bytes 1310720 | tf_op jit(solution)/shard_map/all_gather | solution.py:205
  8.3 126.9 %all-gather.6.cloned.1.call-start = ((), (), s32[]{:S(2)}) async-start(), calls=%async_computation.1 | async-start | bytes 17825792 | tf_op jit(solution)/shard_map/all_gather | solution.py:206
  35.6 28.1 %collective-permute-start = (bf16[2,1,64,3072]{3,2,1,0:T(8,128)(2,1)S(1)}, bf16[2,1,64,3072]{3,2,1,0:T(8,128)(2,1)S(1)}, u32[]{:S(2)}, u32[]{:S(2)}) collective-permute-start(bf16[2,1,64,3072]{3,2,1,0:T(8,128)(2,1)S(1)} %copy-done.4), channel_id=1, source_target_pairs={{0,1},{1,0},{2,3},{3,2},{4,5},{5,4},{6,7},{7,6},{8,9},{9,8},{10,11... | collective-permute-start | bytes 2359304 | tf_op jit(solution)/shard_map/ppermute | solution.py:202
  204.7 2.2 copy-start.2
  204.7 5.3 %copy-start = (f32[4,768,128]{2,1,0:T(8,128)S(1)}, f32[4,768,128]{2,1,0:T(8,128)}, u32[]{:S(2)}) copy-start(f32[4,768,128]{2,1,0:T(8,128)} %get-tuple-element.20) | copy-start | bytes 4718596
  206.8 21.8 %copy-start.5 = (f32[4,6,2,64,1]{3,2,1,0,4:T(2,128)}, f32[4,6,2,64,1]{3,2,1,0,4:T(2,128)S(1)}, u32[]{:S(2)}) copy-start(f32[4,6,2,64,1]{3,2,1,0,4:T(2,128)S(1)} %reshape.49) | copy-start | bytes 36868
  207.4 2.5 copy-start.6
  208.1 32.4 %collective-permute-start.3 = (f32[4,6,64,2]{2,3,1,0:T(2,128)}, f32[4,6,64,2]{2,3,1,0:T(2,128)}, u32[]{:S(2)}, u32[]{:S(2)}) collective-permute-start(f32[4,6,64,2]{2,3,1,0:T(2,128)} %pad_maximum_fusion.2), channel_id=1, source_target_pairs={{0,1},{1,0},{2,3},{3,2},{4,5},{5,4},{6,7},{7,6},{8,9},{9,8},{10,11... | collective-permute-start | bytes 36872 | tf_op jit(solution)/shard_map/ppermute | solution.py:178
  210.8 32.2 %collective-permute-start.4 = (bf16[4,6,64,128]{3,2,1,0:T(8,128)(2,1)}, bf16[4,6,64,128]{3,2,1,0:T(8,128)(2,1)S(1)}, u32[]{:S(2)}, u32[]{:S(2)}) collective-permute-start(bf16[4,6,64,128]{3,2,1,0:T(8,128)(2,1)} %fusion.5), channel_id=1, source_target_pairs={{0,1},{1,0},{2,3},{3,2},{4,5},{5,4},{6,7},{7,6},{8,9},{9,8},{10,11... | collective-permute-start | bytes 1179656 | tf_op jit(solution)/shard_map/ppermute | solution.py:177
  228.6 10.1 %copy-start.1 = (f32[4,768,128]{2,1,0:T(8,128)S(1)}, f32[4,768,128]{2,1,0:T(8,128)}, u32[]{:S(2)}) copy-start(f32[4,768,128]{2,1,0:T(8,128)} %get-tuple-element.14) | copy-start | bytes 4718596
  236.7 5.4 %collective-permute-start.1 = (f32[4,6,64,2]{2,3,1,0:T(2,128)S(1)}, f32[4,6,64,2]{2,3,1,0:T(2,128)S(1)}, u32[]{:S(2)}, u32[]{:S(2)}) collective-permute-start(f32[4,6,64,2]{2,3,1,0:T(2,128)S(1)} %pad_maximum_fusion.1), channel_id=1, source_target_pairs={{0,1},{1,0},{2,3},{3,2},{4,5},{5,4},{6,7},{7,6},{8,9},{9,8},{10,11... | collective-permute-start | bytes 36872 | tf_op jit(solution)/shard_map/ppermute | solution.py:178
  238.8 13.1 %copy-start.7 = (f32[128]{0:T(128)S(1)}, f32[128]{0:T(128)}, u32[]{:S(2)}) copy-start(f32[128]{0:T(128)} %param.7) | copy-start | bytes 1540
  238.8 12.0 %collective-permute-start.2 = (bf16[4,6,64,128]{3,2,1,0:T(8,128)(2,1)S(1)}, bf16[4,6,64,128]{3,2,1,0:T(8,128)(2,1)S(1)}, u32[]{:S(2)}, u32[]{:S(2)}) collective-permute-start(bf16[4,6,64,128]{3,2,1,0:T(8,128)(2,1)S(1)} %fusion.4), channel_id=1, source_target_pairs={{0,1},{1,0},{2,3},{3,2},{4,5},{5,4},{6,7},{7,6},{8,9},{9,8},{10,11... | collective-permute-start | bytes 1179656 | tf_op jit(solution)/shard_map/ppermute | solution.py:177
  254.3 1.0 copy-start.3
Sparse Core Ops, SparseCore 0:
  9.0 26.5 all-gather.3
  37.2 97.9 all-gather.5

commit v11 on v10

--- a/solution.py
+++ b/solution.py
@@ -17,7 +17,7 @@
 EXP2_SCALE = math.log2(math.e) / math.sqrt(HEAD_DIM)
 
 
-def attend_kernel(bounds_ref, q_ref, k_ref, v_ref, *rest, carry_in):
+def attend_kernel(bounds_ref, q_ref, k_ref, v_ref, *rest, carry_in, tiles_per_phase):
     if carry_in:
         m_in, l_in, acc_in = rest[:3]
         rest = rest[3:]
@@ -27,9 +27,10 @@
     t = pl.program_id(1)
     last = pl.num_programs(1) - 1
     tile_blocks, block_rows, _ = k_ref.shape
-    lo = bounds_ref[0]
-    hi = bounds_ref[1]
-    tile = lo // tile_blocks + t
+    phase = t // tiles_per_phase
+    lo = bounds_ref[2 * phase]
+    hi = bounds_ref[2 * phase + 1]
+    tile = lo // tile_blocks + t % tiles_per_phase
     first_block = tile * tile_blocks
 
     @pl.when(t == 0)
@@ -98,25 +99,32 @@
         acc_out[0] = acc_sc[...]
 
 
-def attend(bounds, q, kv, half, state=None):
+def attend(bounds, q, kv, halves, state=None):
     rows = q.shape[0]
     _, n_blocks, block_rows, _ = kv.shape
     tile_blocks = TILE_KEYS // block_rows
     n_tiles = n_blocks // tile_blocks
     qrows = rows * GROUP
 
+    phases = len(halves)
+
+    def half_of(t):
+        return halves[0] if phases == 1 else t // n_tiles
+
     def tile_of(t, b):
-        return jnp.minimum(b[0] // tile_blocks + t, b[1] // tile_blocks)
+        phase = t // n_tiles
+        first = b[2 * phase] // tile_blocks + t % n_tiles
+        return jnp.minimum(first, b[2 * phase + 1] // tile_blocks)
 
     in_specs = [
         pl.BlockSpec((rows, GROUP * HEAD_DIM), lambda g, t, b: (0, g)),
         pl.BlockSpec(
             (None, tile_blocks, block_rows, HEAD_DIM),
-            lambda g, t, b: (half, tile_of(t, b), 0, g),
+            lambda g, t, b: (half_of(t), tile_of(t, b), 0, g),
         ),
         pl.BlockSpec(
             (None, tile_blocks, block_rows, HEAD_DIM),
-            lambda g, t, b: (half, tile_of(t, b), 0, KV_HEADS + g),
+            lambda g, t, b: (half_of(t), tile_of(t, b), 0, KV_HEADS + g),
         ),
     ]
     operands = [q, kv, kv]
@@ -133,18 +141,20 @@
     if state is not None:
         in_specs += state_specs
         operands += list(state)
-    kernel = functools.partial(attend_kernel, carry_in=state is not None)
+    kernel = functools.partial(
+        attend_kernel, carry_in=state is not None, tiles_per_phase=n_tiles
+    )
     tile_flops = 4 * qrows * TILE_KEYS * HEAD_DIM
     cost = pl.CostEstimate(
-        flops=KV_HEADS * n_tiles * tile_flops,
-        transcendentals=KV_HEADS * n_tiles * qrows * TILE_KEYS,
+        flops=KV_HEADS * n_tiles * phases * tile_flops,
+        transcendentals=KV_HEADS * n_tiles * phases * qrows * TILE_KEYS,
         bytes_accessed=kv.size + q.size * 2 + KV_HEADS * qrows * HEAD_DIM * 8,
     )
     return pl.pallas_call(
         kernel,
         grid_spec=pltpu.PrefetchScalarGridSpec(
             num_scalar_prefetch=1,
-            grid=(KV_HEADS, n_tiles),
+            grid=(KV_HEADS, n_tiles * phases),
             in_specs=in_specs,
             out_specs=state_specs,
             scratch_shapes=[
@@ -208,12 +218,13 @@
     zero = jnp.int32(0)
     top = jnp.int32(last_index)
 
-    early = attend(jnp.stack([zero, seq_index]), both_queries[0, 0], blocks, 0)
+    early = attend(jnp.stack([zero, seq_index]), both_queries[0, 0], blocks, (0,))
     early_mine, early_theirs = split_halves(early, own_rows)
     early_back = send_back(early_theirs, swap)
 
-    state = attend(jnp.stack([zero, top]), both_queries[1, 0], blocks, 0)
-    late = attend(jnp.stack([seq_index, top]), both_queries[1, 0], blocks, 1, state=state)
+    late = attend(
+        jnp.stack([zero, top, seq_index, top]), both_queries[1, 0], blocks, (0, 1)
+    )
     late_mine, late_theirs = split_halves(late, own_rows)
     late_back = send_back(late_theirs, swap)
 

time: 269 us -> 266 us (0.989)
    pallas_call x3 -> x2, Pallas kernels: 85.6 us -> 84.6 us  [attend(): pl.pallas_call(kernel, grid_spec=pltpu.PrefetchScalarGridSpec(num_scalar_...]
where the time goes in v11:
time: 266 us; the launch traced here: 263 us
  waiting for transfers between devices  128 us (48%)
  Pallas kernels  84.6 us (32%)
  other arithmetic  17.9 us (7%)
  between operations  13.7 us (5%)
  starting transfers between devices  10.7 us (4%)
  local copies, waits for them, and re-layouts  7.74 us (3%)
    pallas_call x2, Pallas kernels, attend(): pl.pallas_call(kernel, grid_spec=pltpu.PrefetchScalarGridSpec(num_scalar_...  84.6 us
    all_gather x1, waiting for transfers between devices, per_device(): blocks = lax.all_gather(blocks, 'inner', axis=2, tiled=False)  70.1 us
    all_gather x1, waiting for transfers between devices, per_device(): blocks = lax.all_gather(pair[:, 0], 'outer', axis=1, tiled=False)  27.2 us
    ppermute x1, waiting for transfers between devices, per_device(): partner_queries = lax.ppermute(queries, 'row', swap)  23.6 us
    ppermute x2, waiting for transfers between devices, send_back(): lax.ppermute(acc.astype(jnp.bfloat16), 'row', swap).astype(jnp.float32)  6.89 us
    pallas_call x4, other arithmetic, attend(): pl.pallas_call(kernel, grid_spec=pltpu.PrefetchScalarGridSpec(num_scalar_...  6.41 us
  transfers between devices with their start and end apart: 7, of which 5 were waited for; matrix products, arithmetic and copies ran while one was open for 5% of the time, Pallas kernels for 6%

profile of v11, /device:TPU:0, one launch (start us, length us, event | category | flops | bytes accessed | tf_op | source)
XLA Modules:
  0.0 263.0 jit_solution(16020496049784327881)
XLA Ops:
  6.5 0.0 copy-start.4
  6.5 0.0 all-gather.4.cloned.1.call-start
  6.5 1.8 pad_maximum_fusion
  8.3 0.0 all-gather.4.cloned.1.call-update
  8.3 0.0 all-gather.6.cloned.1.call-start
  8.4 27.2 %all-gather.4.cloned.1.call-done = bf16[2,4,64,1024]{3,2,1,0:T(8,128)(2,1)} async-done(((bf16[2,1,64,1024]{3,2,1,0:T(8,128)(2,1)}), bf16[2,4,64,1024]{3,2,1,0:T(8,128)(2,1)}) %all-gather.4.cloned.1.call-update) | async-done | bytes 1048592 | tf_op jit(solution)/shard_map/all_gather | solution.py:215
  35.6 0.0 all-gather.6.cloned.1.call-update
  35.6 0.0 copy-done.4
  35.6 3.2 %collective-permute-start = (bf16[2,1,64,3072]{3,2,1,0:T(8,128)(2,1)S(1)}, bf16[2,1,64,3072]{3,2,1,0:T(8,128)(2,1)S(1)}, u32[]{:S(2)}, u32[]{:S(2)}) collective-permute-start(bf16[2,1,64,3072]{3,2,1,0:T(8,128)(2,1)S(1)} %copy-done.4), channel_id=1, source_target_pairs={{0,1},{1,0},{2,3},{3,2},{4,5},{5,4},{6,7},{7,6},{8,9},{9,8},{10,11... | collective-permute-start | bytes 2359304 | tf_op jit(solution)/shard_map/ppermute | solution.py:212
  38.8 0.6 pad_add_fusion.bounds_ref
  39.4 0.7 pad_add_fusion.1.bounds_ref
  40.1 0.1 constant_dynamic-update-slice_fusion.1
  40.2 23.6 %collective-permute-done = bf16[2,1,64,3072]{3,2,1,0:T(8,128)(2,1)S(1)} collective-permute-done((bf16[2,1,64,3072]{3,2,1,0:T(8,128)(2,1)S(1)}, bf16[2,1,64,3072]{3,2,1,0:T(8,128)(2,1)S(1)}, u32[]{:S(2)}, u32[]{:S(2)}) %collective-permute-start) | collective-permute-done | bytes 786464 | tf_op jit(solution)/shard_map/ppermute | solution.py:212
  63.7 0.1 constant_dynamic-update-slice_fusion
  63.8 1.3 slice_bitcast_fusion.3
  65.1 70.1 %all-gather.6.cloned.1.call-done = bf16[2,4,1024,1024]{3,2,1,0:T(8,128)(2,1)} async-done(((bf16[2,4,64,1024]{3,2,1,0:T(8,128)(2,1)}), bf16[2,4,1024,1024]{3,2,1,0:T(8,128)(2,1)}) %all-gather.6.cloned.1.call-update) | async-done | bytes 16777232 | tf_op jit(solution)/shard_map/all_gather | solution.py:216
  135.2 67.7 %shard_map.47 = (f32[4,768,1]{2,1,0:T(8,128)}, f32[4,768,1]{2,1,0:T(8,128)}, f32[4,768,128]{2,1,0:T(8,128)}) custom-call(s32[4]{0:T(128)} %pad_add_fusion.1.bounds_ref, bf16[128,3072]{1,0:T(8,128)(2,1)} %get-tuple-element.24.q_ref, bf16[2,64,64,1024]{3,2,1,0:T(8,128)(2,1)} %bitcast.110, bf16[2,64,64,1024]{3,2,1,0:T(8,128)(2,1)} %bitcast.111), custom_call_target="tpu_custom_call" | custom-call | flops 12884901888 | bytes 12320768 | tf_op jit(solution)/shard_map/pallas_call | solution.py:153
  202.9 0.0 copy-start.2
  202.9 0.0 copy-start
  202.9 2.0 reduce.2
  205.0 0.1 reshape.48
  205.1 0.0 copy-start.5
  205.1 0.0 copy-done.2
  205.1 0.5 reduce.3
  205.6 0.1 reshape.49
  205.7 0.0 copy-start.6
  205.7 0.6 pad_maximum_fusion.2
  206.4 1.9 collective-permute-start.3
  208.2 0.0 copy-done.6
  208.2 0.0 copy-done
  208.2 0.8 fusion.5
  209.1 1.6 collective-permute-start.4
  210.7 16.9 %shard_map.46 = (f32[4,768,1]{2,1,0:T(8,128)}, f32[4,768,1]{2,1,0:T(8,128)}, f32[4,768,128]{2,1,0:T(8,128)}) custom-call(s32[2]{0:T(128)} %pad_add_fusion.bounds_ref, bf16[128,3072]{1,0:T(8,128)(2,1)} %get-tuple-element.23.q_ref, bf16[2,64,64,1024]{3,2,1,0:T(8,128)(2,1)} %bitcast.112, bf16[2,64,64,1024]{3,2,1,0:T(8,128)(2,1)} %bitcast.113), custom_call_target="tpu_custom_call" | custom-call | flops 6442450944 | bytes 12320768 | tf_op jit(solution)/shard_map/pallas_call | solution.py:153
  227.6 0.0 copy-done.5
  227.6 0.0 copy-start.1
  227.6 2.0 reduce
  229.6 0.7 reshape.45
  230.3 1.3 slice_bitcast_fusion.10
  231.6 1.9 reduce.1
  233.5 0.7 reshape.46
  234.2 0.7 slice_bitcast_fusion.9
  235.0 0.7 pad_maximum_fusion.1
  235.7 2.0 collective-permute-start.1
  237.7 0.0 copy-done.1
  237.7 0.1 fusion.4
  237.7 0.0 copy-start.7
  237.7 1.9 collective-permute-start.2
  239.6 0.0 collective-permute-done.3
  239.6 0.9 fusion.12
  240.6 0.5 collective-permute-done.1
  241.1 0.8 fusion.14
  241.9 0.0 collective-permute-done.4
  242.0 1.0 multiply_reduce_fusion
  243.1 6.9 %collective-permute-done.2 = bf16[4,6,64,128]{3,2,1,0:T(8,128)(2,1)S(1)} collective-permute-done((bf16[4,6,64,128]{3,2,1,0:T(8,128)(2,1)S(1)}, bf16[4,6,64,128]{3,2,1,0:T(8,128)(2,1)S(1)}, u32[]{:S(2)}, u32[]{:S(2)}) %collective-permute-start.2) | collective-permute-done | bytes 393248 | tf_op jit(solution)/shard_map/ppermute | solution.py:187
  249.9 1.0 multiply_reduce_fusion.1
  251.0 0.0 copy-done.7
  251.0 2.4 fusion.6
  253.4 0.0 copy-start.3
  253.4 0.3 copy.106
  253.7 0.4 stack_reshape.6
  254.2 0.3 copy-done.3
  254.4 0.3 copy.122
  254.7 0.4 stack_reshape.7
  255.2 0.9 maximum_bitcast_fusion
  (16 shorter events, 0.1 us)
Async XLA Ops:
  6.5 29.1 %copy-start.4 = (bf16[2,1,64,3072]{3,2,1,0:T(8,128)(2,1)S(1)}, bf16[2,1,64,3072]{3,2,1,0:T(8,128)(2,1)}, u32[]{:S(2)}) copy-start(bf16[2,1,64,3072]{3,2,1,0:T(8,128)(2,1)} %param.4) | copy-start | bytes 2359300
  6.5 29.0 %all-gather.4.cloned.1.call-start = ((), (), s32[]{:S(2)}) async-start(), calls=%async_computation | async-start | bytes 1310720 | tf_op jit(solution)/shard_map/all_gather | solution.py:215
  8.3 126.9 %all-gather.6.cloned.1.call-start = ((), (), s32[]{:S(2)}) async-start(), calls=%async_computation.1 | async-start | bytes 17825792 | tf_op jit(solution)/shard_map/all_gather | solution.py:216
  35.6 28.1 %collective-permute-start = (bf16[2,1,64,3072]{3,2,1,0:T(8,128)(2,1)S(1)}, bf16[2,1,64,3072]{3,2,1,0:T(8,128)(2,1)S(1)}, u32[]{:S(2)}, u32[]{:S(2)}) collective-permute-start(bf16[2,1,64,3072]{3,2,1,0:T(8,128)(2,1)S(1)} %copy-done.4), channel_id=1, source_target_pairs={{0,1},{1,0},{2,3},{3,2},{4,5},{5,4},{6,7},{7,6},{8,9},{9,8},{10,11... | collective-permute-start | bytes 2359304 | tf_op jit(solution)/shard_map/ppermute | solution.py:212
  202.9 2.2 copy-start.2
  202.9 5.3 %copy-start = (f32[4,768,128]{2,1,0:T(8,128)S(1)}, f32[4,768,128]{2,1,0:T(8,128)}, u32[]{:S(2)}) copy-start(f32[4,768,128]{2,1,0:T(8,128)} %get-tuple-element.14) | copy-start | bytes 4718596
  205.1 22.5 %copy-start.5 = (f32[4,6,2,64,1]{3,2,1,0,4:T(2,128)}, f32[4,6,2,64,1]{3,2,1,0,4:T(2,128)S(1)}, u32[]{:S(2)}) copy-start(f32[4,6,2,64,1]{3,2,1,0,4:T(2,128)S(1)} %reshape.48) | copy-start | bytes 36868
  205.7 2.5 copy-start.6
  206.4 33.3 %collective-permute-start.3 = (f32[4,6,64,2]{2,3,1,0:T(2,128)}, f32[4,6,64,2]{2,3,1,0:T(2,128)}, u32[]{:S(2)}, u32[]{:S(2)}) collective-permute-start(f32[4,6,64,2]{2,3,1,0:T(2,128)} %pad_maximum_fusion.2), channel_id=1, source_target_pairs={{0,1},{1,0},{2,3},{3,2},{4,5},{5,4},{6,7},{7,6},{8,9},{9,8},{10,11... | collective-permute-start | bytes 36872 | tf_op jit(solution)/shard_map/ppermute | solution.py:188
  209.1 32.9 %collective-permute-start.4 = (bf16[4,6,64,128]{3,2,1,0:T(8,128)(2,1)}, bf16[4,6,64,128]{3,2,1,0:T(8,128)(2,1)S(1)}, u32[]{:S(2)}, u32[]{:S(2)}) collective-permute-start(bf16[4,6,64,128]{3,2,1,0:T(8,128)(2,1)} %fusion.5), channel_id=1, source_target_pairs={{0,1},{1,0},{2,3},{3,2},{4,5},{5,4},{6,7},{7,6},{8,9},{9,8},{10,11... | collective-permute-start | bytes 1179656 | tf_op jit(solution)/shard_map/ppermute | solution.py:187
  227.6 10.1 %copy-start.1 = (f32[4,768,128]{2,1,0:T(8,128)S(1)}, f32[4,768,128]{2,1,0:T(8,128)}, u32[]{:S(2)}) copy-start(f32[4,768,128]{2,1,0:T(8,128)} %get-tuple-element.11) | copy-start | bytes 4718596
  235.7 5.4 %collective-permute-start.1 = (f32[4,6,64,2]{2,3,1,0:T(2,128)S(1)}, f32[4,6,64,2]{2,3,1,0:T(2,128)S(1)}, u32[]{:S(2)}, u32[]{:S(2)}) collective-permute-start(f32[4,6,64,2]{2,3,1,0:T(2,128)S(1)} %pad_maximum_fusion.1), channel_id=1, source_target_pairs={{0,1},{1,0},{2,3},{3,2},{4,5},{5,4},{6,7},{7,6},{8,9},{9,8},{10,11... | collective-permute-start | bytes 36872 | tf_op jit(solution)/shard_map/ppermute | solution.py:188
  237.7 13.3 %copy-start.7 = (f32[128]{0:T(128)S(1)}, f32[128]{0:T(128)}, u32[]{:S(2)}) copy-start(f32[128]{0:T(128)} %param.7) | copy-start | bytes 1540
  237.7 12.2 %collective-permute-start.2 = (bf16[4,6,64,128]{3,2,1,0:T(8,128)(2,1)S(1)}, bf16[4,6,64,128]{3,2,1,0:T(8,128)(2,1)S(1)}, u32[]{:S(2)}, u32[]{:S(2)}) collective-permute-start(bf16[4,6,64,128]{3,2,1,0:T(8,128)(2,1)S(1)} %fusion.4), channel_id=1, source_target_pairs={{0,1},{1,0},{2,3},{3,2},{4,5},{5,4},{6,7},{7,6},{8,9},{9,8},{10,11... | collective-permute-start | bytes 1179656 | tf_op jit(solution)/shard_map/ppermute | solution.py:187
  253.4 1.0 copy-start.3
Sparse Core Ops, SparseCore 0:
  9.0 26.5 all-gather.3
  37.2 97.9 all-gather.5

commit v12 on v11

--- a/solution.py
+++ b/solution.py
@@ -15,6 +15,14 @@
 
 lowest_score = -1e30
 EXP2_SCALE = math.log2(math.e) / math.sqrt(HEAD_DIM)
+
+
+def to_row(column):
+    return jnp.transpose(jnp.broadcast_to(column, (column.shape[0], HEAD_DIM)))[0:1, :]
+
+
+def from_row(row):
+    return jnp.transpose(jnp.broadcast_to(row, (HEAD_DIM, row.shape[1])))[:, 0:1]
 
 
 def attend_kernel(bounds_ref, q_ref, k_ref, v_ref, *rest, carry_in, tiles_per_phase):
@@ -40,8 +48,8 @@
             [q_ref[:, j * HEAD_DIM:(j + 1) * HEAD_DIM] for j in range(GROUP)], axis=0
         )
         if carry_in:
-            m_sc[...] = m_in[0]
-            l_sc[...] = l_in[0]
+            m_sc[...] = from_row(m_in[0])
+            l_sc[...] = from_row(l_in[0])
             acc_sc[...] = acc_in[0]
         else:
             m_sc[...] = jnp.full(m_sc.shape, lowest_score, jnp.float32)
@@ -94,8 +102,8 @@
 
     @pl.when(t == last)
     def _done():
-        m_out[0] = m_sc[...]
-        l_out[0] = l_sc[...]
+        m_out[0] = to_row(m_sc[...])
+        l_out[0] = to_row(l_sc[...])
         acc_out[0] = acc_sc[...]
 
 
@@ -129,13 +137,13 @@
     ]
     operands = [q, kv, kv]
     state_specs = [
-        pl.BlockSpec((1, qrows, 1), lambda g, t, b: (g, 0, 0)),
-        pl.BlockSpec((1, qrows, 1), lambda g, t, b: (g, 0, 0)),
+        pl.BlockSpec((1, 1, qrows), lambda g, t, b: (g, 0, 0)),
+        pl.BlockSpec((1, 1, qrows), lambda g, t, b: (g, 0, 0)),
         pl.BlockSpec((1, qrows, HEAD_DIM), lambda g, t, b: (g, 0, 0)),
     ]
     state_shapes = [
-        jax.ShapeDtypeStruct((KV_HEADS, qrows, 1), jnp.float32),
-        jax.ShapeDtypeStruct((KV_HEADS, qrows, 1), jnp.float32),
+        jax.ShapeDtypeStruct((KV_HEADS, 1, qrows), jnp.float32),
+        jax.ShapeDtypeStruct((KV_HEADS, 1, qrows), jnp.float32),
         jax.ShapeDtypeStruct((KV_HEADS, qrows, HEAD_DIM), jnp.float32),
     ]
     if state is not None:
@@ -176,7 +184,8 @@
 def split_halves(state, own_rows):
     mine, theirs = [], []
     for part in state:
-        shaped = part.reshape(KV_HEADS, GROUP, 2, own_rows, part.shape[-1])
+        width = part.shape[-1] if part.shape[1] != 1 else 1
+        shaped = part.reshape(KV_HEADS, GROUP, 2, own_rows, width)
         mine.append(shaped[:, :, 0])
         theirs.append(shaped[:, :, 1])
     return mine, theirs

time: 266 us -> 263 us (0.989)
  waiting for transfers between devices: 128 us -> 137 us
  other arithmetic: 17.9 us -> 10.7 us
  local copies, waits for them, and re-layouts: 7.74 us -> 4.58 us
    ppermute x2, waiting for transfers between devices: 6.89 us -> 15.9 us  [send_back(): lax.ppermute(acc.astype(jnp.bfloat16), 'row', swap).astype(jnp.float32)]
    pallas_call x4, other arithmetic: 6.41 us -> 3.1 us  [attend(): pl.pallas_call(kernel, grid_spec=pltpu.PrefetchScalarGridSpec(num_scalar_...]
  transfers between devices with their start and end apart: 7 -> 7, of which waited for: 5 -> 5; matrix products, arithmetic and copies ran while one was open for 5% -> 2% of each run, Pallas kernels for 6% -> 0%
where the time goes in v12:
time: 263 us; the launch traced here: 262 us
  waiting for transfers between devices  137 us (52%)
  Pallas kernels  85.5 us (33%)
  between operations  13.7 us (5%)
  other arithmetic  10.7 us (4%)
  starting transfers between devices  10.5 us (4%)
  local copies, waits for them, and re-layouts  4.58 us (2%)
    pallas_call x2, Pallas kernels, attend(): pl.pallas_call(kernel, grid_spec=pltpu.PrefetchScalarGridSpec(num_scalar_...  85.5 us
    all_gather x1, waiting for transfers between devices, per_device(): blocks = lax.all_gather(blocks, 'inner', axis=2, tiled=False)  70.2 us
    all_gather x1, waiting for transfers between devices, per_device(): blocks = lax.all_gather(pair[:, 0], 'outer', axis=1, tiled=False)  27.2 us
    ppermute x1, waiting for transfers between devices, per_device(): partner_queries = lax.ppermute(queries, 'row', swap)  23.6 us
    ppermute x2, waiting for transfers between devices, send_back(): lax.ppermute(acc.astype(jnp.bfloat16), 'row', swap).astype(jnp.float32)  15.9 us
  transfers between devices with their start and end apart: 7, of which 5 were waited for; matrix products, arithmetic and copies ran while one was open for 2% of the time, Pallas kernels for 0%

profile of v12, /device:TPU:0, one launch (start us, length us, event | category | flops | bytes accessed | tf_op | source)
XLA Modules:
  0.0 261.9 jit_solution(10827759593825571519)
XLA Ops:
  6.5 0.0 copy-start.2
  6.5 0.0 all-gather.4.cloned.1.call-start
  6.5 1.8 pad_maximum_fusion
  8.3 0.0 all-gather.4.cloned.1.call-update
  8.3 0.0 all-gather.6.cloned.1.call-start
  8.4 27.2 %all-gather.4.cloned.1.call-done = bf16[2,4,64,1024]{3,2,1,0:T(8,128)(2,1)} async-done(((bf16[2,1,64,1024]{3,2,1,0:T(8,128)(2,1)}), bf16[2,4,64,1024]{3,2,1,0:T(8,128)(2,1)}) %all-gather.4.cloned.1.call-update) | async-done | bytes 1048592 | tf_op jit(solution)/shard_map/all_gather | solution.py:224
  35.6 0.0 all-gather.6.cloned.1.call-update
  35.6 0.0 copy-done.2
  35.6 3.2 %collective-permute-start = (bf16[2,1,64,3072]{3,2,1,0:T(8,128)(2,1)S(1)}, bf16[2,1,64,3072]{3,2,1,0:T(8,128)(2,1)S(1)}, u32[]{:S(2)}, u32[]{:S(2)}) collective-permute-start(bf16[2,1,64,3072]{3,2,1,0:T(8,128)(2,1)S(1)} %copy-done.2), channel_id=1, source_target_pairs={{0,1},{1,0},{2,3},{3,2},{4,5},{5,4},{6,7},{7,6},{8,9},{9,8},{10,11... | collective-permute-start | bytes 2359304 | tf_op jit(solution)/shard_map/ppermute | solution.py:221
  38.8 0.6 pad_add_fusion.bounds_ref
  39.5 0.6 pad_add_fusion.1.bounds_ref
  40.1 0.1 constant_dynamic-update-slice_fusion.1
  40.1 23.6 %collective-permute-done = bf16[2,1,64,3072]{3,2,1,0:T(8,128)(2,1)S(1)} collective-permute-done((bf16[2,1,64,3072]{3,2,1,0:T(8,128)(2,1)S(1)}, bf16[2,1,64,3072]{3,2,1,0:T(8,128)(2,1)S(1)}, u32[]{:S(2)}, u32[]{:S(2)}) %collective-permute-start) | collective-permute-done | bytes 786464 | tf_op jit(solution)/shard_map/ppermute | solution.py:221
  63.7 0.1 constant_dynamic-update-slice_fusion
  63.8 1.2 slice_bitcast_fusion.3
  65.0 70.2 %all-gather.6.cloned.1.call-done = bf16[2,4,1024,1024]{3,2,1,0:T(8,128)(2,1)} async-done(((bf16[2,4,64,1024]{3,2,1,0:T(8,128)(2,1)}), bf16[2,4,1024,1024]{3,2,1,0:T(8,128)(2,1)}) %all-gather.6.cloned.1.call-update) | async-done | bytes 16777232 | tf_op jit(solution)/shard_map/all_gather | solution.py:225
  135.2 16.4 %shard_map.46 = (f32[4,1,768]{2,1,0:T(1,128)}, f32[4,1,768]{2,1,0:T(1,128)}, f32[4,768,128]{2,1,0:T(8,128)}) custom-call(s32[2]{0:T(128)} %pad_add_fusion.bounds_ref, bf16[128,3072]{1,0:T(8,128)(2,1)} %get-tuple-element.17.q_ref, bf16[2,64,64,1024]{3,2,1,0:T(8,128)(2,1)} %bitcast.110, bf16[2,64,64,1024]{3,2,1,0:T(8,128)(2,1)} %bitcast.111), custom_call_target="tpu_custom_call" | custom-call | flops 6442450944 | bytes 12320768 | tf_op jit(solution)/shard_map/pallas_call | solution.py:161
  151.6 0.7 reduce
  152.3 0.1 reshape.45
  152.4 0.7 reduce.1
  153.2 0.1 reshape.46
  153.3 0.0 copy-start
  153.3 69.1 %shard_map.47 = (f32[4,1,768]{2,1,0:T(1,128)}, f32[4,1,768]{2,1,0:T(1,128)}, f32[4,768,128]{2,1,0:T(8,128)}) custom-call(s32[4]{0:T(128)} %pad_add_fusion.1.bounds_ref, bf16[128,3072]{1,0:T(8,128)(2,1)} %get-tuple-element.18.q_ref, bf16[2,64,64,1024]{3,2,1,0:T(8,128)(2,1)} %bitcast.112, bf16[2,64,64,1024]{3,2,1,0:T(8,128)(2,1)} %bitcast.113), custom_call_target="tpu_custom_call" | custom-call | flops 12884901888 | bytes 12320768 | tf_op jit(solution)/shard_map/pallas_call | solution.py:161
  222.4 0.0 copy-start.1
  222.4 0.9 reduce.2
  223.3 0.7 reduce.3
  224.1 0.1 reshape.49
  224.2 0.1 reshape.48
  224.4 2.0 collective-permute-start.1
  226.4 1.6 collective-permute-start.3
  228.0 0.0 copy-done
  228.0 0.1 fusion.4
  228.1 1.2 fusion.5
  229.3 0.0 copy-start.3
  229.3 2.0 collective-permute-start.4
  231.3 1.6 collective-permute-start.2
  232.9 0.0 collective-permute-done.1
  233.0 0.0 collective-permute-done.3
  233.0 9.8 %collective-permute-done.4 = bf16[4,6,64,128]{3,2,1,0:T(8,128)(2,1)S(1)} collective-permute-done((bf16[4,6,64,128]{3,2,1,0:T(8,128)(2,1)S(1)}, bf16[4,6,64,128]{3,2,1,0:T(8,128)(2,1)S(1)}, u32[]{:S(2)}, u32[]{:S(2)}) %collective-permute-start.4) | collective-permute-done | bytes 393248 | tf_op jit(solution)/shard_map/ppermute | solution.py:196
  242.9 0.0 copy-done.1
  242.9 1.0 multiply_reduce_fusion
  243.9 6.0 %collective-permute-done.2 = bf16[4,6,64,128]{3,2,1,0:T(8,128)(2,1)S(1)} collective-permute-done((bf16[4,6,64,128]{3,2,1,0:T(8,128)(2,1)S(1)}, bf16[4,6,64,128]{3,2,1,0:T(8,128)(2,1)S(1)}, u32[]{:S(2)}, u32[]{:S(2)}) %collective-permute-start.2) | collective-permute-done | bytes 393248 | tf_op jit(solution)/shard_map/ppermute | solution.py:196
  250.0 1.0 multiply_reduce_fusion.1
  251.1 0.0 copy-done.3
  251.1 1.5 fusion.6
  252.6 0.3 copy.86
  252.9 0.4 stack_reshape.6
  253.4 0.3 copy.100
  253.6 0.4 stack_reshape.7
  254.1 0.9 maximum_bitcast_fusion
  (22 shorter events, 0.2 us)
Async XLA Ops:
  6.5 29.1 %copy-start.2 = (bf16[2,1,64,3072]{3,2,1,0:T(8,128)(2,1)S(1)}, bf16[2,1,64,3072]{3,2,1,0:T(8,128)(2,1)}, u32[]{:S(2)}) copy-start(bf16[2,1,64,3072]{3,2,1,0:T(8,128)(2,1)} %param.4) | copy-start | bytes 2359300
  6.5 29.0 %all-gather.4.cloned.1.call-start = ((), (), s32[]{:S(2)}) async-start(), calls=%async_computation | async-start | bytes 1310720 | tf_op jit(solution)/shard_map/all_gather | solution.py:224
  8.3 126.9 %all-gather.6.cloned.1.call-start = ((), (), s32[]{:S(2)}) async-start(), calls=%async_computation.1 | async-start | bytes 17825792 | tf_op jit(solution)/shard_map/all_gather | solution.py:225
  35.6 28.1 %collective-permute-start = (bf16[2,1,64,3072]{3,2,1,0:T(8,128)(2,1)S(1)}, bf16[2,1,64,3072]{3,2,1,0:T(8,128)(2,1)S(1)}, u32[]{:S(2)}, u32[]{:S(2)}) collective-permute-start(bf16[2,1,64,3072]{3,2,1,0:T(8,128)(2,1)S(1)} %copy-done.2), channel_id=1, source_target_pairs={{0,1},{1,0},{2,3},{3,2},{4,5},{5,4},{6,7},{7,6},{8,9},{9,8},{10,11... | collective-permute-start | bytes 2359304 | tf_op jit(solution)/shard_map/ppermute | solution.py:221
  153.3 74.7 %copy-start = (f32[4,768,128]{2,1,0:T(8,128)S(1)}, f32[4,768,128]{2,1,0:T(8,128)}, u32[]{:S(2)}) copy-start(f32[4,768,128]{2,1,0:T(8,128)} %get-tuple-element.11) | copy-start | bytes 4718596
  222.4 20.4 %copy-start.1 = (f32[4,768,128]{2,1,0:T(8,128)S(1)}, f32[4,768,128]{2,1,0:T(8,128)}, u32[]{:S(2)}) copy-start(f32[4,768,128]{2,1,0:T(8,128)} %get-tuple-element.14) | copy-start | bytes 4718596
  224.4 8.5 %collective-permute-start.1 = (f32[4,6,64,2]{2,0,1,3:T(4,128)S(1)}, f32[4,6,64,2]{2,0,1,3:T(4,128)S(1)}, u32[]{:S(2)}, u32[]{:S(2)}) collective-permute-start(f32[4,6,64,2]{2,0,1,3:T(4,128)S(1)} %copy.78), channel_id=1, source_target_pairs={{0,1},{1,0},{2,3},{3,2},{4,5},{5,4},{6,7},{7,6},{8,9},{9,8},{10,11... | collective-permute-start | bytes 36872 | tf_op jit(solution)/shard_map/ppermute | solution.py:197
  226.4 6.6 %collective-permute-start.3 = (f32[4,6,64,2]{2,0,1,3:T(4,128)S(1)}, f32[4,6,64,2]{2,0,1,3:T(4,128)S(1)}, u32[]{:S(2)}, u32[]{:S(2)}) collective-permute-start(f32[4,6,64,2]{2,0,1,3:T(4,128)S(1)} %copy.91), channel_id=1, source_target_pairs={{0,1},{1,0},{2,3},{3,2},{4,5},{5,4},{6,7},{7,6},{8,9},{9,8},{10,11... | collective-permute-start | bytes 36872 | tf_op jit(solution)/shard_map/ppermute | solution.py:197
  229.3 21.8 %copy-start.3 = (f32[128]{0:T(128)S(1)}, f32[128]{0:T(128)}, u32[]{:S(2)}) copy-start(f32[128]{0:T(128)} %param.7) | copy-start | bytes 1540
  229.3 13.6 %collective-permute-start.4 = (bf16[4,6,64,128]{3,2,1,0:T(8,128)(2,1)S(1)}, bf16[4,6,64,128]{3,2,1,0:T(8,128)(2,1)S(1)}, u32[]{:S(2)}, u32[]{:S(2)}) collective-permute-start(bf16[4,6,64,128]{3,2,1,0:T(8,128)(2,1)S(1)} %fusion.5), channel_id=1, source_target_pairs={{0,1},{1,0},{2,3},{3,2},{4,5},{5,4},{6,7},{7,6},{8,9},{9,8},{10,11... | collective-permute-start | bytes 1179656 | tf_op jit(solution)/shard_map/ppermute | solution.py:196
  231.3 18.7 %collective-permute-start.2 = (bf16[4,6,64,128]{3,2,1,0:T(8,128)(2,1)S(1)}, bf16[4,6,64,128]{3,2,1,0:T(8,128)(2,1)S(1)}, u32[]{:S(2)}, u32[]{:S(2)}) collective-permute-start(bf16[4,6,64,128]{3,2,1,0:T(8,128)(2,1)S(1)} %fusion.4), channel_id=1, source_target_pairs={{0,1},{1,0},{2,3},{3,2},{4,5},{5,4},{6,7},{7,6},{8,9},{9,8},{10,11... | collective-permute-start | bytes 1179656 | tf_op jit(solution)/shard_map/ppermute | solution.py:196
Sparse Core Ops, SparseCore 0:
  9.0 26.5 all-gather.3
  37.2 97.9 all-gather.5

commit v13 on v12

--- a/solution.py
+++ b/solution.py
@@ -230,10 +230,10 @@
     early = attend(jnp.stack([zero, seq_index]), both_queries[0, 0], blocks, (0,))
     early_mine, early_theirs = split_halves(early, own_rows)
     early_back = send_back(early_theirs, swap)
-
-    late = attend(
-        jnp.stack([zero, top, seq_index, top]), both_queries[1, 0], blocks, (0, 1)
-    )
+    late_bounds = jnp.stack([zero, top, seq_index, top])
+    early_back, late_bounds = lax.optimization_barrier((early_back, late_bounds))
+
+    late = attend(late_bounds, both_queries[1, 0], blocks, (0, 1))
     late_mine, late_theirs = split_halves(late, own_rows)
     late_back = send_back(late_theirs, swap)
 

time: 263 us -> 267 us (1.015)
    ppermute x2, waiting for transfers between devices: 0.01 us -> 9.05 us  [send_back(): lax.ppermute(jnp.concatenate([run_max, run_sum], axis=-1), 'row', swap)]
    ppermute x2, waiting for transfers between devices: 15.9 us -> 8.81 us  [send_back(): lax.ppermute(acc.astype(jnp.bfloat16), 'row', swap).astype(jnp.float32)]
where the time goes in v13:
time: 267 us; the launch traced here: 266 us
  waiting for transfers between devices  139 us (52%)
  Pallas kernels  85.5 us (32%)
  between operations  13.7 us (5%)
  starting transfers between devices  10.8 us (4%)
  other arithmetic  10.7 us (4%)
  local copies, waits for them, and re-layouts  5.7 us (2%)
    pallas_call x2, Pallas kernels, attend(): pl.pallas_call(kernel, grid_spec=pltpu.PrefetchScalarGridSpec(num_scalar_...  85.5 us
    all_gather x1, waiting for transfers between devices, per_device(): blocks = lax.all_gather(blocks, 'inner', axis=2, tiled=False)  70.2 us
    all_gather x1, waiting for transfers between devices, per_device(): blocks = lax.all_gather(pair[:, 0], 'outer', axis=1, tiled=False)  27.2 us
    ppermute x1, waiting for transfers between devices, per_device(): partner_queries = lax.ppermute(queries, 'row', swap)  24.2 us
    ppermute x2, waiting for transfers between devices, send_back(): lax.ppermute(jnp.concatenate([run_max, run_sum], axis=-1), 'row', swap)  9.05 us
    ppermute x2, waiting for transfers between devices, send_back(): lax.ppermute(acc.astype(jnp.bfloat16), 'row', swap).astype(jnp.float32)  8.81 us
  transfers between devices with their start and end apart: 7, of which 5 were waited for; matrix products, arithmetic and copies ran while one was open for 2% of the time, Pallas kernels for 0%

profile of v13, /device:TPU:0, one launch (start us, length us, event | category | flops | bytes accessed | tf_op | source)
XLA Modules:
  0.0 265.9 jit_solution(7199930021327808012)
XLA Ops:
  6.5 0.0 copy-start.2
  6.5 0.0 all-gather.4.cloned.1.call-start
  6.5 1.8 pad_maximum_fusion
  8.3 0.0 all-gather.4.cloned.1.call-update
  8.3 0.0 all-gather.6.cloned.1.call-start
  8.4 27.2 %all-gather.4.cloned.1.call-done = bf16[2,4,64,1024]{3,2,1,0:T(8,128)(2,1)} async-done(((bf16[2,1,64,1024]{3,2,1,0:T(8,128)(2,1)}), bf16[2,4,64,1024]{3,2,1,0:T(8,128)(2,1)}) %all-gather.4.cloned.1.call-update) | async-done | bytes 1048592 | tf_op jit(solution)/shard_map/all_gather | solution.py:224
  35.6 0.0 all-gather.6.cloned.1.call-update
  35.6 0.0 copy-done.2
  35.6 3.2 %collective-permute-start = (bf16[2,1,64,3072]{3,2,1,0:T(8,128)(2,1)S(1)}, bf16[2,1,64,3072]{3,2,1,0:T(8,128)(2,1)S(1)}, u32[]{:S(2)}, u32[]{:S(2)}) collective-permute-start(bf16[2,1,64,3072]{3,2,1,0:T(8,128)(2,1)S(1)} %copy-done.2), channel_id=1, source_target_pairs={{0,1},{1,0},{2,3},{3,2},{4,5},{5,4},{6,7},{7,6},{8,9},{9,8},{10,11... | collective-permute-start | bytes 2359304 | tf_op jit(solution)/shard_map/ppermute | solution.py:221
  38.8 0.6 pad_add_fusion.bounds_ref
  39.5 0.1 constant_dynamic-update-slice_fusion.1
  39.5 24.2 %collective-permute-done = bf16[2,1,64,3072]{3,2,1,0:T(8,128)(2,1)S(1)} collective-permute-done((bf16[2,1,64,3072]{3,2,1,0:T(8,128)(2,1)S(1)}, bf16[2,1,64,3072]{3,2,1,0:T(8,128)(2,1)S(1)}, u32[]{:S(2)}, u32[]{:S(2)}) %collective-permute-start) | collective-permute-done | bytes 786464 | tf_op jit(solution)/shard_map/ppermute | solution.py:221
  63.7 0.1 constant_dynamic-update-slice_fusion
  63.8 1.2 slice_bitcast_fusion.1
  65.0 70.2 %all-gather.6.cloned.1.call-done = bf16[2,4,1024,1024]{3,2,1,0:T(8,128)(2,1)} async-done(((bf16[2,4,64,1024]{3,2,1,0:T(8,128)(2,1)}), bf16[2,4,1024,1024]{3,2,1,0:T(8,128)(2,1)}) %all-gather.6.cloned.1.call-update) | async-done | bytes 16777232 | tf_op jit(solution)/shard_map/all_gather | solution.py:225
  135.2 16.4 %shard_map.46 = (f32[4,1,768]{2,1,0:T(1,128)}, f32[4,1,768]{2,1,0:T(1,128)}, f32[4,768,128]{2,1,0:T(8,128)}) custom-call(s32[2]{0:T(128)} %pad_add_fusion.bounds_ref, bf16[128,3072]{1,0:T(8,128)(2,1)} %get-tuple-element.26.q_ref, bf16[2,64,64,1024]{3,2,1,0:T(8,128)(2,1)} %bitcast.112, bf16[2,64,64,1024]{3,2,1,0:T(8,128)(2,1)} %bitcast.113), custom_call_target="tpu_custom_call" | custom-call | flops 6442450944 | bytes 12320768 | tf_op jit(solution)/shard_map/pallas_call | solution.py:161
  151.6 0.7 reduce.1
  152.3 0.1 reshape.46
  152.4 0.7 reduce
  153.2 0.1 reshape.45
  153.3 1.2 fusion.4
  154.5 2.0 collective-permute-start.2
  156.5 1.7 collective-permute-start.1
  158.2 0.6 pad_add_fusion.1.bounds_ref
  158.9 9.1 %collective-permute-done.1 = f32[4,6,64,2]{2,0,1,3:T(4,128)S(1)} collective-permute-done((f32[4,6,64,2]{2,0,1,3:T(4,128)S(1)}, f32[4,6,64,2]{2,0,1,3:T(4,128)S(1)}, u32[]{:S(2)}, u32[]{:S(2)}) %collective-permute-start.1) | collective-permute-done | bytes 12320 | tf_op jit(solution)/shard_map/ppermute | solution.py:197
  167.9 0.0 collective-permute-done.2
  167.9 0.1 convert_element_type.21
  168.1 0.0 copy-start
  168.1 69.1 %shard_map.47 = (f32[4,1,768]{2,1,0:T(1,128)}, f32[4,1,768]{2,1,0:T(1,128)}, f32[4,768,128]{2,1,0:T(8,128)}) custom-call(s32[4]{0:T(128)} %pad_add_fusion.1.bounds_ref, bf16[128,3072]{1,0:T(8,128)(2,1)} %get-tuple-element.25.q_ref, bf16[2,64,64,1024]{3,2,1,0:T(8,128)(2,1)} %bitcast.114, bf16[2,64,64,1024]{3,2,1,0:T(8,128)(2,1)} %bitcast.115), custom_call_target="tpu_custom_call" | custom-call | flops 12884901888 | bytes 12320768 | tf_op jit(solution)/shard_map/pallas_call | solution.py:161
  237.2 0.7 reduce.3
  237.9 0.1 reshape.49
  238.1 0.7 reduce.2
  238.8 0.1 reshape.48
  238.9 0.0 copy-start.1
  239.0 2.0 collective-permute-start.3
  241.0 1.2 fusion.5
  242.2 0.0 copy-start.3
  242.2 1.9 collective-permute-start.4
  244.1 0.0 copy-done
  244.1 1.0 multiply_reduce_fusion.1
  245.2 0.0 collective-permute-done.3
  245.2 8.8 %collective-permute-done.4 = bf16[4,6,64,128]{3,2,1,0:T(8,128)(2,1)S(1)} collective-permute-done((bf16[4,6,64,128]{3,2,1,0:T(8,128)(2,1)S(1)}, bf16[4,6,64,128]{3,2,1,0:T(8,128)(2,1)S(1)}, u32[]{:S(2)}, u32[]{:S(2)}) %collective-permute-start.4) | collective-permute-done | bytes 393248 | tf_op jit(solution)/shard_map/ppermute | solution.py:196
  254.0 0.0 copy-done.1
  254.0 1.0 multiply_reduce_fusion
  255.1 0.0 copy-done.3
  255.1 1.5 fusion.6
  256.7 0.3 copy.100
  257.0 0.4 stack_reshape.7
  257.4 0.3 copy.86
  257.7 0.4 stack_reshape.6
  258.1 0.9 maximum_bitcast_fusion
  (24 shorter events, 0.2 us)
Async XLA Ops:
  6.5 29.1 %copy-start.2 = (bf16[2,1,64,3072]{3,2,1,0:T(8,128)(2,1)S(1)}, bf16[2,1,64,3072]{3,2,1,0:T(8,128)(2,1)}, u32[]{:S(2)}) copy-start(bf16[2,1,64,3072]{3,2,1,0:T(8,128)(2,1)} %param.4) | copy-start | bytes 2359300
  6.5 29.0 %all-gather.4.cloned.1.call-start = ((), (), s32[]{:S(2)}) async-start(), calls=%async_computation | async-start | bytes 1310720 | tf_op jit(solution)/shard_map/all_gather | solution.py:224
  8.3 126.9 %all-gather.6.cloned.1.call-start = ((), (), s32[]{:S(2)}) async-start(), calls=%async_computation.1 | async-start | bytes 17825792 | tf_op jit(solution)/shard_map/all_gather | solution.py:225
  35.6 28.1 %collective-permute-start = (bf16[2,1,64,3072]{3,2,1,0:T(8,128)(2,1)S(1)}, bf16[2,1,64,3072]{3,2,1,0:T(8,128)(2,1)S(1)}, u32[]{:S(2)}, u32[]{:S(2)}) collective-permute-start(bf16[2,1,64,3072]{3,2,1,0:T(8,128)(2,1)S(1)} %copy-done.2), channel_id=1, source_target_pairs={{0,1},{1,0},{2,3},{3,2},{4,5},{5,4},{6,7},{7,6},{8,9},{9,8},{10,11... | collective-permute-start | bytes 2359304 | tf_op jit(solution)/shard_map/ppermute | solution.py:221
  154.5 13.4 %collective-permute-start.2 = (bf16[4,6,64,128]{3,2,1,0:T(8,128)(2,1)S(1)}, bf16[4,6,64,128]{3,2,1,0:T(8,128)(2,1)S(1)}, u32[]{:S(2)}, u32[]{:S(2)}) collective-permute-start(bf16[4,6,64,128]{3,2,1,0:T(8,128)(2,1)S(1)} %fusion.4), channel_id=1, source_target_pairs={{0,1},{1,0},{2,3},{3,2},{4,5},{5,4},{6,7},{7,6},{8,9},{9,8},{10,11... | collective-permute-start | bytes 1179656 | tf_op jit(solution)/shard_map/ppermute | solution.py:196
  156.5 11.4 %collective-permute-start.1 = (f32[4,6,64,2]{2,0,1,3:T(4,128)S(1)}, f32[4,6,64,2]{2,0,1,3:T(4,128)S(1)}, u32[]{:S(2)}, u32[]{:S(2)}) collective-permute-start(f32[4,6,64,2]{2,0,1,3:T(4,128)S(1)} %copy.78), channel_id=1, source_target_pairs={{0,1},{1,0},{2,3},{3,2},{4,5},{5,4},{6,7},{7,6},{8,9},{9,8},{10,11... | collective-permute-start | bytes 36872 | tf_op jit(solution)/shard_map/ppermute | solution.py:197
  168.1 76.0 %copy-start = (f32[4,768,128]{2,1,0:T(8,128)S(1)}, f32[4,768,128]{2,1,0:T(8,128)}, u32[]{:S(2)}) copy-start(f32[4,768,128]{2,1,0:T(8,128)} %get-tuple-element.15) | copy-start | bytes 4718596
  238.9 15.1 %copy-start.1 = (f32[4,768,128]{2,1,0:T(8,128)S(1)}, f32[4,768,128]{2,1,0:T(8,128)}, u32[]{:S(2)}) copy-start(f32[4,768,128]{2,1,0:T(8,128)} %get-tuple-element.22) | copy-start | bytes 4718596
  239.0 6.2 %collective-permute-start.3 = (f32[4,6,64,2]{2,0,1,3:T(4,128)S(1)}, f32[4,6,64,2]{2,0,1,3:T(4,128)S(1)}, u32[]{:S(2)}, u32[]{:S(2)}) collective-permute-start(f32[4,6,64,2]{2,0,1,3:T(4,128)S(1)} %copy.91), channel_id=1, source_target_pairs={{0,1},{1,0},{2,3},{3,2},{4,5},{5,4},{6,7},{7,6},{8,9},{9,8},{10,11... | collective-permute-start | bytes 36872 | tf_op jit(solution)/shard_map/ppermute | solution.py:197
  242.2 13.0 %copy-start.3 = (f32[128]{0:T(128)S(1)}, f32[128]{0:T(128)}, u32[]{:S(2)}) copy-start(f32[128]{0:T(128)} %param.7) | copy-start | bytes 1540
  242.2 11.9 %collective-permute-start.4 = (bf16[4,6,64,128]{3,2,1,0:T(8,128)(2,1)S(1)}, bf16[4,6,64,128]{3,2,1,0:T(8,128)(2,1)S(1)}, u32[]{:S(2)}, u32[]{:S(2)}) collective-permute-start(bf16[4,6,64,128]{3,2,1,0:T(8,128)(2,1)S(1)} %fusion.5), channel_id=1, source_target_pairs={{0,1},{1,0},{2,3},{3,2},{4,5},{5,4},{6,7},{7,6},{8,9},{9,8},{10,11... | collective-permute-start | bytes 1179656 | tf_op jit(solution)/shard_map/ppermute | solution.py:196
Sparse Core Ops, SparseCore 0:
  9.0 26.5 all-gather.3
  37.2 97.9 all-gather.5

commit v14 on v12

--- a/solution.py
+++ b/solution.py
@@ -229,13 +229,14 @@
 
     early = attend(jnp.stack([zero, seq_index]), both_queries[0, 0], blocks, (0,))
     early_mine, early_theirs = split_halves(early, own_rows)
-    early_back = send_back(early_theirs, swap)
 
     late = attend(
         jnp.stack([zero, top, seq_index, top]), both_queries[1, 0], blocks, (0, 1)
     )
     late_mine, late_theirs = split_halves(late, own_rows)
-    late_back = send_back(late_theirs, swap)
+    both_back = send_back([jnp.stack(pair) for pair in zip(early_theirs, late_theirs)], swap)
+    early_back = [x[0] for x in both_back]
+    late_back = [x[1] for x in both_back]
 
     early_out = finish(early_mine, early_back, gain)
     late_out = finish(late_mine, late_back, gain)

time: 263 us -> 261 us (level)
  starting transfers between devices: 10.5 us -> 7.14 us
    ppermute x2 -> x1, waiting for transfers between devices: 0.01 us -> 18.4 us  [send_back(): lax.ppermute(jnp.concatenate([run_max, run_sum], axis=-1), 'row', swap)]
    ppermute x2 -> x1, waiting for transfers between devices: 15.9 us -> 0.01 us  [send_back(): lax.ppermute(acc.astype(jnp.bfloat16), 'row', swap).astype(jnp.float32)]
  transfers between devices with their start and end apart: 7 -> 5, of which waited for: 5 -> 4; matrix products, arithmetic and copies ran while one was open for 2% -> 1% of each run, Pallas kernels for 0% -> 0%
where the time goes in v14:
time: 261 us; the launch traced here: 260 us
  waiting for transfers between devices  139 us (53%)
  Pallas kernels  85.5 us (33%)
  between operations  13.7 us (5%)
  other arithmetic  9.48 us (4%)
  starting transfers between devices  7.14 us (3%)
  local copies, waits for them, and re-layouts  4.58 us (2%)
    pallas_call x2, Pallas kernels, attend(): pl.pallas_call(kernel, grid_spec=pltpu.PrefetchScalarGridSpec(num_scalar_...  85.5 us
    all_gather x1, waiting for transfers between devices, per_device(): blocks = lax.all_gather(blocks, 'inner', axis=2, tiled=False)  70.2 us
    all_gather x1, waiting for transfers between devices, per_device(): blocks = lax.all_gather(pair[:, 0], 'outer', axis=1, tiled=False)  27.2 us
    ppermute x1, waiting for transfers between devices, per_device(): partner_queries = lax.ppermute(queries, 'row', swap)  23.6 us
    ppermute x1, waiting for transfers between devices, send_back(): lax.ppermute(jnp.concatenate([run_max, run_sum], axis=-1), 'row', swap)  18.4 us
  transfers between devices with their start and end apart: 5, of which 4 were waited for; matrix products, arithmetic and copies ran while one was open for 1% of the time, Pallas kernels for 0%

profile of v14, /device:TPU:0, one launch (start us, length us, event | category | flops | bytes accessed | tf_op | source)
XLA Modules:
  0.0 259.8 jit_solution(17747975245903765438)
XLA Ops:
  6.5 0.0 copy-start.2
  6.5 0.0 all-gather.4.cloned.1.call-start
  6.5 1.8 pad_maximum_fusion.1
  8.3 0.0 all-gather.4.cloned.1.call-update
  8.3 0.0 all-gather.6.cloned.1.call-start
  8.4 27.2 %all-gather.4.cloned.1.call-done = bf16[2,4,64,1024]{3,2,1,0:T(8,128)(2,1)} async-done(((bf16[2,1,64,1024]{3,2,1,0:T(8,128)(2,1)}), bf16[2,4,64,1024]{3,2,1,0:T(8,128)(2,1)}) %all-gather.4.cloned.1.call-update) | async-done | bytes 1048592 | tf_op jit(solution)/shard_map/all_gather | solution.py:224
  35.6 0.0 all-gather.6.cloned.1.call-update
  35.6 0.0 copy-done.2
  35.6 3.2 %collective-permute-start = (bf16[2,1,64,3072]{3,2,1,0:T(8,128)(2,1)S(1)}, bf16[2,1,64,3072]{3,2,1,0:T(8,128)(2,1)S(1)}, u32[]{:S(2)}, u32[]{:S(2)}) collective-permute-start(bf16[2,1,64,3072]{3,2,1,0:T(8,128)(2,1)S(1)} %copy-done.2), channel_id=1, source_target_pairs={{0,1},{1,0},{2,3},{3,2},{4,5},{5,4},{6,7},{7,6},{8,9},{9,8},{10,11... | collective-permute-start | bytes 2359304 | tf_op jit(solution)/shard_map/ppermute | solution.py:221
  38.8 0.6 pad_add_fusion.bounds_ref
  39.5 0.6 pad_add_fusion.1.bounds_ref
  40.1 0.1 constant_dynamic-update-slice_fusion.1
  40.1 23.6 %collective-permute-done = bf16[2,1,64,3072]{3,2,1,0:T(8,128)(2,1)S(1)} collective-permute-done((bf16[2,1,64,3072]{3,2,1,0:T(8,128)(2,1)S(1)}, bf16[2,1,64,3072]{3,2,1,0:T(8,128)(2,1)S(1)}, u32[]{:S(2)}, u32[]{:S(2)}) %collective-permute-start) | collective-permute-done | bytes 786464 | tf_op jit(solution)/shard_map/ppermute | solution.py:221
  63.7 0.1 constant_dynamic-update-slice_fusion
  63.8 1.3 slice_bitcast_fusion.3
  65.0 70.2 %all-gather.6.cloned.1.call-done = bf16[2,4,1024,1024]{3,2,1,0:T(8,128)(2,1)} async-done(((bf16[2,4,64,1024]{3,2,1,0:T(8,128)(2,1)}), bf16[2,4,1024,1024]{3,2,1,0:T(8,128)(2,1)}) %all-gather.6.cloned.1.call-update) | async-done | bytes 16777232 | tf_op jit(solution)/shard_map/all_gather | solution.py:225
  135.2 16.4 %shard_map.46 = (f32[4,1,768]{2,1,0:T(1,128)}, f32[4,1,768]{2,1,0:T(1,128)}, f32[4,768,128]{2,1,0:T(8,128)}) custom-call(s32[2]{0:T(128)} %pad_add_fusion.bounds_ref, bf16[128,3072]{1,0:T(8,128)(2,1)} %get-tuple-element.27.q_ref, bf16[2,64,64,1024]{3,2,1,0:T(8,128)(2,1)} %bitcast.124, bf16[2,64,64,1024]{3,2,1,0:T(8,128)(2,1)} %bitcast.125), custom_call_target="tpu_custom_call" | custom-call | flops 6442450944 | bytes 12320768 | tf_op jit(solution)/shard_map/pallas_call | solution.py:161
  151.6 0.0 copy-start.4
  151.6 0.0 copy-start.3
  151.6 0.0 copy-start
  151.6 69.1 %shard_map.47 = (f32[4,1,768]{2,1,0:T(1,128)}, f32[4,1,768]{2,1,0:T(1,128)}, f32[4,768,128]{2,1,0:T(8,128)}) custom-call(s32[4]{0:T(128)} %pad_add_fusion.1.bounds_ref, bf16[128,3072]{1,0:T(8,128)(2,1)} %get-tuple-element.28.q_ref, bf16[2,64,64,1024]{3,2,1,0:T(8,128)(2,1)} %bitcast.126, bf16[2,64,64,1024]{3,2,1,0:T(8,128)(2,1)} %bitcast.127), custom_call_target="tpu_custom_call" | custom-call | flops 12884901888 | bytes 12320768 | tf_op jit(solution)/shard_map/pallas_call | solution.py:161
  220.7 0.7 reduce.1
  221.5 0.0 copy-done.4
  221.5 0.1 reshape.179
  221.6 0.0 copy-done.3
  221.7 0.7 reduce.3
  222.4 0.1 reshape.182
  222.6 0.1 reshape.181
  222.7 0.1 reshape.180
  222.8 0.0 copy-done
  222.8 1.3 fusion.6
  224.1 0.1 pad_maximum_fusion
  224.2 0.0 copy-start.1
  224.2 2.0 collective-permute-start.2
  226.2 1.9 collective-permute-start.1
  228.1 18.4 %collective-permute-done.1 = f32[2,4,6,64,2]{3,1,2,4,0:T(4,128)S(1)} collective-permute-done((f32[2,4,6,64,2]{3,1,2,4,0:T(4,128)S(1)}, f32[2,4,6,64,2]{3,1,2,4,0:T(4,128)S(1)}, u32[]{:S(2)}, u32[]{:S(2)}) %collective-permute-start.1) | collective-permute-done | bytes 24608 | tf_op jit(solution)/shard_map/ppermute | solution.py:197
  246.6 0.0 collective-permute-done.2
  246.6 0.2 convert_element_type.10
  246.8 0.0 copy-done.1
  246.8 0.0 copy-start.5
  246.8 2.1 multiply_reduce_fusion.1
  249.0 0.0 copy-done.5
  249.0 1.5 fusion.8
  250.5 0.3 copy.107
  250.8 0.4 stack_reshape.6
  251.3 0.3 copy.117
  251.5 0.4 stack_reshape.7
  252.0 0.9 maximum_bitcast_fusion
  (21 shorter events, 0.3 us)
Async XLA Ops:
  6.5 29.1 %copy-start.2 = (bf16[2,1,64,3072]{3,2,1,0:T(8,128)(2,1)S(1)}, bf16[2,1,64,3072]{3,2,1,0:T(8,128)(2,1)}, u32[]{:S(2)}) copy-start(bf16[2,1,64,3072]{3,2,1,0:T(8,128)(2,1)} %param.4) | copy-start | bytes 2359300
  6.5 29.0 %all-gather.4.cloned.1.call-start = ((), (), s32[]{:S(2)}) async-start(), calls=%async_computation | async-start | bytes 1310720 | tf_op jit(solution)/shard_map/all_gather | solution.py:224
  8.3 126.9 %all-gather.6.cloned.1.call-start = ((), (), s32[]{:S(2)}) async-start(), calls=%async_computation.1 | async-start | bytes 17825792 | tf_op jit(solution)/shard_map/all_gather | solution.py:225
  35.6 28.1 %collective-permute-start = (bf16[2,1,64,3072]{3,2,1,0:T(8,128)(2,1)S(1)}, bf16[2,1,64,3072]{3,2,1,0:T(8,128)(2,1)S(1)}, u32[]{:S(2)}, u32[]{:S(2)}) collective-permute-start(bf16[2,1,64,3072]{3,2,1,0:T(8,128)(2,1)S(1)} %copy-done.2), channel_id=1, source_target_pairs={{0,1},{1,0},{2,3},{3,2},{4,5},{5,4},{6,7},{7,6},{8,9},{9,8},{10,11... | collective-permute-start | bytes 2359304 | tf_op jit(solution)/shard_map/ppermute | solution.py:221
  151.6 69.9 %copy-start.4 = (f32[4,1,768]{2,1,0:T(1,128)S(1)}, f32[4,1,768]{2,1,0:T(1,128)}, u32[]{:S(2)}) copy-start(f32[4,1,768]{2,1,0:T(1,128)} %get-tuple-element.12) | copy-start | bytes 36868
  151.6 70.0 %copy-start.3 = (f32[4,1,768]{2,1,0:T(1,128)S(1)}, f32[4,1,768]{2,1,0:T(1,128)}, u32[]{:S(2)}) copy-start(f32[4,1,768]{2,1,0:T(1,128)} %get-tuple-element.14) | copy-start | bytes 36868
  151.6 71.2 %copy-start = (f32[4,768,128]{2,1,0:T(8,128)S(1)}, f32[4,768,128]{2,1,0:T(8,128)}, u32[]{:S(2)}) copy-start(f32[4,768,128]{2,1,0:T(8,128)} %get-tuple-element.11) | copy-start | bytes 4718596
  224.2 22.6 %copy-start.1 = (f32[4,768,128]{2,1,0:T(8,128)S(1)}, f32[4,768,128]{2,1,0:T(8,128)}, u32[]{:S(2)}) copy-start(f32[4,768,128]{2,1,0:T(8,128)} %get-tuple-element.16) | copy-start | bytes 4718596
  224.2 22.4 %collective-permute-start.2 = (bf16[2,4,6,64,128]{4,3,2,1,0:T(8,128)(2,1)S(1)}, bf16[2,4,6,64,128]{4,3,2,1,0:T(8,128)(2,1)S(1)}, u32[]{:S(2)}, u32[]{:S(2)}) collective-permute-start(bf16[2,4,6,64,128]{4,3,2,1,0:T(8,128)(2,1)S(1)} %pad_maximum_fusion), channel_id=1, source_target_pairs={{0,1},{1,0},{2,3},{3,2},{4,5},{5,4},{6,7},{7,6},{8,9},{9,8},{10,11... | collective-permute-start | bytes 2359304 | tf_op jit(solution)/shard_map/ppermute | solution.py:196
  226.2 20.3 %collective-permute-start.1 = (f32[2,4,6,64,2]{3,1,2,4,0:T(4,128)S(1)}, f32[2,4,6,64,2]{3,1,2,4,0:T(4,128)S(1)}, u32[]{:S(2)}, u32[]{:S(2)}) collective-permute-start(f32[2,4,6,64,2]{3,1,2,4,0:T(4,128)S(1)} %copy.97), channel_id=1, source_target_pairs={{0,1},{1,0},{2,3},{3,2},{4,5},{5,4},{6,7},{7,6},{8,9},{9,8},{10,11... | collective-permute-start | bytes 73736 | tf_op jit(solution)/shard_map/ppermute | solution.py:197
  246.8 2.2 copy-start.5
Sparse Core Ops, SparseCore 0:
  9.0 26.5 all-gather.3
  37.2 97.9 all-gather.5

commit v15 on v14

--- a/solution.py
+++ b/solution.py
@@ -209,8 +209,8 @@
     mixed = acc / total
     spread = jnp.sqrt(jnp.mean(mixed * mixed, axis=-1, keepdims=True) + 1e-06)
     normed = (mixed / spread * gain).astype(jnp.bfloat16)
-    rows = normed.shape[2]
-    return normed.transpose(2, 0, 1, 3).reshape(rows, KV_HEADS * GROUP * HEAD_DIM)
+    halves, rows = normed.shape[0], normed.shape[3]
+    return normed.transpose(0, 3, 1, 2, 4).reshape(halves, 1, rows, KV_HEADS * GROUP * HEAD_DIM)
 
 
 def per_device(queries, keys, values, gain, outer, inner):
@@ -235,12 +235,9 @@
     )
     late_mine, late_theirs = split_halves(late, own_rows)
     both_back = send_back([jnp.stack(pair) for pair in zip(early_theirs, late_theirs)], swap)
-    early_back = [x[0] for x in both_back]
-    late_back = [x[1] for x in both_back]
-
-    early_out = finish(early_mine, early_back, gain)
-    late_out = finish(late_mine, late_back, gain)
-    return jnp.stack([early_out, late_out]).reshape(2, 1, own_rows, KV_HEADS * GROUP * HEAD_DIM)
+
+    both_mine = [jnp.stack(pair) for pair in zip(early_mine, late_mine)]
+    return finish(both_mine, both_back, gain)
 
 
 def solution(mesh):

time: 261 us -> 263 us (level)
    ppermute x1, waiting for transfers between devices: 0.01 us -> 18.8 us  [send_back(): lax.ppermute(acc.astype(jnp.bfloat16), 'row', swap).astype(jnp.float32)]
    ppermute x1, waiting for transfers between devices: 18.4 us -> 0.11 us  [send_back(): lax.ppermute(jnp.concatenate([run_max, run_sum], axis=-1), 'row', swap)]
  transfers between devices with their start and end apart: 5 -> 5, of which waited for: 4 -> 5; matrix products, arithmetic and copies ran while one was open for 1% -> 2% of each run, Pallas kernels for 0% -> 0%
where the time goes in v15:
time: 263 us; the launch traced here: 262 us
  waiting for transfers between devices  140 us (53%)
  Pallas kernels  85.5 us (33%)
  between operations  13.6 us (5%)
  other arithmetic  9.74 us (4%)
  starting transfers between devices  7.14 us (3%)
  local copies, waits for them, and re-layouts  5.72 us (2%)
    pallas_call x2, Pallas kernels, attend(): pl.pallas_call(kernel, grid_spec=pltpu.PrefetchScalarGridSpec(num_scalar_...  85.5 us
    all_gather x1, waiting for transfers between devices, per_device(): blocks = lax.all_gather(blocks, 'inner', axis=2, tiled=False)  70.1 us
    all_gather x1, waiting for transfers between devices, per_device(): blocks = lax.all_gather(pair[:, 0], 'outer', axis=1, tiled=False)  27.2 us
    ppermute x1, waiting for transfers between devices, per_device(): partner_queries = lax.ppermute(queries, 'row', swap)  23.6 us
    ppermute x1, waiting for transfers between devices, send_back(): lax.ppermute(acc.astype(jnp.bfloat16), 'row', swap).astype(jnp.float32)  18.8 us
  transfers between devices with their start and end apart: 5, of which 5 were waited for; matrix products, arithmetic and copies ran while one was open for 2% of the time, Pallas kernels for 0%

profile of v15, /device:TPU:0, one launch (start us, length us, event | category | flops | bytes accessed | tf_op | source)
XLA Modules:
  0.0 261.6 jit_solution(8445981997856868273)
XLA Ops:
  6.5 0.0 copy-start.2
  6.5 0.0 all-gather.4.cloned.1.call-start
  6.5 1.8 pad_maximum_fusion.1
  8.3 0.0 all-gather.4.cloned.1.call-update
  8.3 0.0 all-gather.6.cloned.1.call-start
  8.4 27.2 %all-gather.4.cloned.1.call-done = bf16[2,4,64,1024]{3,2,1,0:T(8,128)(2,1)} async-done(((bf16[2,1,64,1024]{3,2,1,0:T(8,128)(2,1)}), bf16[2,4,64,1024]{3,2,1,0:T(8,128)(2,1)}) %all-gather.4.cloned.1.call-update) | async-done | bytes 1048592 | tf_op jit(solution)/shard_map/all_gather | solution.py:224
  35.6 0.0 all-gather.6.cloned.1.call-update
  35.6 0.0 copy-done.2
  35.6 3.2 %collective-permute-start = (bf16[2,1,64,3072]{3,2,1,0:T(8,128)(2,1)S(1)}, bf16[2,1,64,3072]{3,2,1,0:T(8,128)(2,1)S(1)}, u32[]{:S(2)}, u32[]{:S(2)}) collective-permute-start(bf16[2,1,64,3072]{3,2,1,0:T(8,128)(2,1)S(1)} %copy-done.2), channel_id=1, source_target_pairs={{0,1},{1,0},{2,3},{3,2},{4,5},{5,4},{6,7},{7,6},{8,9},{9,8},{10,11... | collective-permute-start | bytes 2359304 | tf_op jit(solution)/shard_map/ppermute | solution.py:221
  38.8 0.6 pad_add_fusion.bounds_ref
  39.5 0.6 pad_add_fusion.1.bounds_ref
  40.1 0.1 constant_dynamic-update-slice_fusion.1
  40.1 23.6 %collective-permute-done = bf16[2,1,64,3072]{3,2,1,0:T(8,128)(2,1)S(1)} collective-permute-done((bf16[2,1,64,3072]{3,2,1,0:T(8,128)(2,1)S(1)}, bf16[2,1,64,3072]{3,2,1,0:T(8,128)(2,1)S(1)}, u32[]{:S(2)}, u32[]{:S(2)}) %collective-permute-start) | collective-permute-done | bytes 786464 | tf_op jit(solution)/shard_map/ppermute | solution.py:221
  63.7 0.1 constant_dynamic-update-slice_fusion
  63.8 1.3 slice_bitcast_fusion.1
  65.0 70.1 %all-gather.6.cloned.1.call-done = bf16[2,4,1024,1024]{3,2,1,0:T(8,128)(2,1)} async-done(((bf16[2,4,64,1024]{3,2,1,0:T(8,128)(2,1)}), bf16[2,4,1024,1024]{3,2,1,0:T(8,128)(2,1)}) %all-gather.6.cloned.1.call-update) | async-done | bytes 16777232 | tf_op jit(solution)/shard_map/all_gather | solution.py:225
  135.2 16.4 %shard_map.46 = (f32[4,1,768]{2,1,0:T(1,128)}, f32[4,1,768]{2,1,0:T(1,128)}, f32[4,768,128]{2,1,0:T(8,128)}) custom-call(s32[2]{0:T(128)} %pad_add_fusion.bounds_ref, bf16[128,3072]{1,0:T(8,128)(2,1)} %get-tuple-element.17.q_ref, bf16[2,64,64,1024]{3,2,1,0:T(8,128)(2,1)} %bitcast.41, bf16[2,64,64,1024]{3,2,1,0:T(8,128)(2,1)} %bitcast.42), custom_call_target="tpu_custom_call" | custom-call | flops 6442450944 | bytes 12320768 | tf_op jit(solution)/shard_map/pallas_call | solution.py:161
  151.6 0.7 reduce
  152.3 0.1 reshape.36
  152.4 0.7 reduce.2
  153.2 0.1 reshape.38
  153.3 0.0 copy-start
  153.3 69.1 %shard_map.47 = (f32[4,1,768]{2,1,0:T(1,128)}, f32[4,1,768]{2,1,0:T(1,128)}, f32[4,768,128]{2,1,0:T(8,128)}) custom-call(s32[4]{0:T(128)} %pad_add_fusion.1.bounds_ref, bf16[128,3072]{1,0:T(8,128)(2,1)} %get-tuple-element.18.q_ref, bf16[2,64,64,1024]{3,2,1,0:T(8,128)(2,1)} %bitcast.43, bf16[2,64,64,1024]{3,2,1,0:T(8,128)(2,1)} %bitcast.44), custom_call_target="tpu_custom_call" | custom-call | flops 12884901888 | bytes 12320768 | tf_op jit(solution)/shard_map/pallas_call | solution.py:161
  222.4 0.7 reduce.1
  223.2 0.7 reduce.3
  223.9 0.1 reshape.39
  224.1 0.1 reshape.37
  224.2 2.0 collective-permute-start.1
  226.2 0.0 copy-done
  226.2 0.0 copy-start.1
  226.2 1.4 fusion.2
  227.6 0.1 pad_maximum_fusion
  227.7 1.9 collective-permute-start.2
  229.6 0.0 copy-done.1
  229.6 0.2 copy_bitcast_fusion
  229.8 0.0 copy-start.3
  229.8 0.1 collective-permute-done.1
  230.0 18.8 %collective-permute-done.2 = bf16[2,4,6,64,128]{4,3,2,1,0:T(8,128)(2,1)S(1)} collective-permute-done((bf16[2,4,6,64,128]{4,3,2,1,0:T(8,128)(2,1)S(1)}, bf16[2,4,6,64,128]{4,3,2,1,0:T(8,128)(2,1)S(1)}, u32[]{:S(2)}, u32[]{:S(2)}) %collective-permute-start.2) | collective-permute-done | bytes 786464 | tf_op jit(solution)/shard_map/ppermute | solution.py:196
  248.8 2.1 multiply_reduce_fusion
  251.0 0.0 copy-done.3
  251.0 1.5 fusion.1
  252.5 0.5 copy.96
  253.1 1.7 reshape.40
  (15 shorter events, 0.2 us)
Async XLA Ops:
  6.5 29.1 %copy-start.2 = (bf16[2,1,64,3072]{3,2,1,0:T(8,128)(2,1)S(1)}, bf16[2,1,64,3072]{3,2,1,0:T(8,128)(2,1)}, u32[]{:S(2)}) copy-start(bf16[2,1,64,3072]{3,2,1,0:T(8,128)(2,1)} %param.4) | copy-start | bytes 2359300
  6.5 29.0 %all-gather.4.cloned.1.call-start = ((), (), s32[]{:S(2)}) async-start(), calls=%async_computation | async-start | bytes 1310720 | tf_op jit(solution)/shard_map/all_gather | solution.py:224
  8.3 126.9 %all-gather.6.cloned.1.call-start = ((), (), s32[]{:S(2)}) async-start(), calls=%async_computation.1 | async-start | bytes 17825792 | tf_op jit(solution)/shard_map/all_gather | solution.py:225
  35.6 28.1 %collective-permute-start = (bf16[2,1,64,3072]{3,2,1,0:T(8,128)(2,1)S(1)}, bf16[2,1,64,3072]{3,2,1,0:T(8,128)(2,1)S(1)}, u32[]{:S(2)}, u32[]{:S(2)}) collective-permute-start(bf16[2,1,64,3072]{3,2,1,0:T(8,128)(2,1)S(1)} %copy-done.2), channel_id=1, source_target_pairs={{0,1},{1,0},{2,3},{3,2},{4,5},{5,4},{6,7},{7,6},{8,9},{9,8},{10,11... | collective-permute-start | bytes 2359304 | tf_op jit(solution)/shard_map/ppermute | solution.py:221
  153.3 72.9 %copy-start = (f32[4,768,128]{2,1,0:T(8,128)S(1)}, f32[4,768,128]{2,1,0:T(8,128)}, u32[]{:S(2)}) copy-start(f32[4,768,128]{2,1,0:T(8,128)} %get-tuple-element.11) | copy-start | bytes 4718596
  224.2 5.7 %collective-permute-start.1 = (f32[2,4,6,64,2]{3,1,4,2,0:T(4,128)S(1)}, f32[2,4,6,64,2]{3,1,4,2,0:T(4,128)S(1)}, u32[]{:S(2)}, u32[]{:S(2)}) collective-permute-start(f32[2,4,6,64,2]{3,1,4,2,0:T(4,128)S(1)} %maximum_maximum_fusion), channel_id=1, source_target_pairs={{0,1},{1,0},{2,3},{3,2},{4,5},{5,4},{6,7},{7,6},{8,9},{9,8},{10,11... | collective-permute-start | bytes 73736 | tf_op jit(solution)/shard_map/ppermute | solution.py:197
  226.2 3.4 %copy-start.1 = (f32[4,768,128]{2,1,0:T(8,128)S(1)}, f32[4,768,128]{2,1,0:T(8,128)}, u32[]{:S(2)}) copy-start(f32[4,768,128]{2,1,0:T(8,128)} %get-tuple-element.12) | copy-start | bytes 4718596
  227.7 21.2 %collective-permute-start.2 = (bf16[2,4,6,64,128]{4,3,2,1,0:T(8,128)(2,1)S(1)}, bf16[2,4,6,64,128]{4,3,2,1,0:T(8,128)(2,1)S(1)}, u32[]{:S(2)}, u32[]{:S(2)}) collective-permute-start(bf16[2,4,6,64,128]{4,3,2,1,0:T(8,128)(2,1)S(1)} %pad_maximum_fusion), channel_id=1, source_target_pairs={{0,1},{1,0},{2,3},{3,2},{4,5},{5,4},{6,7},{7,6},{8,9},{9,8},{10,11... | collective-permute-start | bytes 2359304 | tf_op jit(solution)/shard_map/ppermute | solution.py:196
  229.8 21.2 %copy-start.3 = (f32[128]{0:T(128)S(1)}, f32[128]{0:T(128)}, u32[]{:S(2)}) copy-start(f32[128]{0:T(128)} %param.7) | copy-start | bytes 1540
Sparse Core Ops, SparseCore 0:
  9.0 26.5 all-gather.3
  37.2 97.9 all-gather.5

commit v16 on v14

--- a/solution.py
+++ b/solution.py
@@ -29,8 +29,8 @@
     if carry_in:
         m_in, l_in, acc_in = rest[:3]
         rest = rest[3:]
-    m_out, l_out, acc_out = rest[:3]
-    q_sc, m_sc, l_sc, acc_sc, vals_sc = rest[3:]
+    m_out, l_out, acc_out, far_out = rest[:4]
+    q_sc, m_sc, l_sc, acc_sc, vals_sc = rest[4:]
 
     t = pl.program_id(1)
     last = pl.num_programs(1) - 1
@@ -105,6 +105,10 @@
         m_out[0] = to_row(m_sc[...])
         l_out[0] = to_row(l_sc[...])
         acc_out[0] = acc_sc[...]
+        rows = q_ref.shape[0]
+        own = rows // 2
+        for j in range(GROUP):
+            far_out[0, j] = acc_sc[j * rows + own:(j + 1) * rows].astype(far_out.dtype)
 
 
 def attend(bounds, q, kv, halves, state=None):
@@ -146,6 +150,12 @@
         jax.ShapeDtypeStruct((KV_HEADS, 1, qrows), jnp.float32),
         jax.ShapeDtypeStruct((KV_HEADS, qrows, HEAD_DIM), jnp.float32),
     ]
+    out_specs = state_specs + [
+        pl.BlockSpec((1, GROUP, rows // 2, HEAD_DIM), lambda g, t, b: (g, 0, 0, 0))
+    ]
+    out_shapes = state_shapes + [
+        jax.ShapeDtypeStruct((KV_HEADS, GROUP, rows // 2, HEAD_DIM), jnp.bfloat16)
+    ]
     if state is not None:
         in_specs += state_specs
         operands += list(state)
@@ -164,7 +174,7 @@
             num_scalar_prefetch=1,
             grid=(KV_HEADS, n_tiles * phases),
             in_specs=in_specs,
-            out_specs=state_specs,
+            out_specs=out_specs,
             scratch_shapes=[
                 pltpu.VMEM((qrows, HEAD_DIM), jnp.bfloat16),
                 pltpu.VMEM((qrows, 1), jnp.float32),
@@ -173,7 +183,7 @@
                 pltpu.VMEM((TILE_KEYS, 2 * HEAD_DIM), jnp.bfloat16),
             ],
         ),
-        out_shape=state_shapes,
+        out_shape=out_shapes,
         compiler_params=pltpu.CompilerParams(
             dimension_semantics=("arbitrary", "arbitrary"),
         ),
@@ -183,11 +193,13 @@
 
 def split_halves(state, own_rows):
     mine, theirs = [], []
+    *state, far_acc = state
     for part in state:
         width = part.shape[-1] if part.shape[1] != 1 else 1
         shaped = part.reshape(KV_HEADS, GROUP, 2, own_rows, width)
         mine.append(shaped[:, :, 0])
         theirs.append(shaped[:, :, 1])
+    theirs[-1] = far_acc
     return mine, theirs
 
 

time: 261 us -> 261 us (level)
  no operation moved by 1% of the time
where the time goes in v16:
time: 261 us; the launch traced here: 260 us
  waiting for transfers between devices  140 us (54%)
  Pallas kernels  85.7 us (33%)
  between operations  13.6 us (5%)
  other arithmetic  10.6 us (4%)
  starting transfers between devices  7.14 us (3%)
  local copies, waits for them, and re-layouts  3.28 us (1%)
    pallas_call x2, Pallas kernels, attend(): pl.pallas_call(kernel, grid_spec=pltpu.PrefetchScalarGridSpec(num_scalar_...  85.7 us
    all_gather x1, waiting for transfers between devices, per_device(): blocks = lax.all_gather(blocks, 'inner', axis=2, tiled=False)  70.2 us
    all_gather x1, waiting for transfers between devices, per_device(): blocks = lax.all_gather(pair[:, 0], 'outer', axis=1, tiled=False)  27.2 us
    ppermute x1, waiting for transfers between devices, per_device(): partner_queries = lax.ppermute(queries, 'row', swap)  23.6 us
    ppermute x1, waiting for transfers between devices, send_back(): lax.ppermute(jnp.concatenate([run_max, run_sum], axis=-1), 'row', swap)  18.7 us
  transfers between devices with their start and end apart: 5, of which 4 were waited for; matrix products, arithmetic and copies ran while one was open for 1% of the time, Pallas kernels for 0%

profile of v16, /device:TPU:0, one launch (start us, length us, event | category | flops | bytes accessed | tf_op | source)
XLA Modules:
  0.0 260.0 jit_solution(6385037601419441399)
XLA Ops:
  6.5 0.0 copy-start.2
  6.5 0.0 all-gather.4.cloned.1.call-start
  6.5 1.8 pad_maximum_fusion.1
  8.3 0.0 all-gather.4.cloned.1.call-update
  8.3 0.0 all-gather.6.cloned.1.call-start
  8.4 27.2 %all-gather.4.cloned.1.call-done = bf16[2,4,64,1024]{3,2,1,0:T(8,128)(2,1)} async-done(((bf16[2,1,64,1024]{3,2,1,0:T(8,128)(2,1)}), bf16[2,4,64,1024]{3,2,1,0:T(8,128)(2,1)}) %all-gather.4.cloned.1.call-update) | async-done | bytes 1048592 | tf_op jit(solution)/shard_map/all_gather | solution.py:236
  35.6 0.0 all-gather.6.cloned.1.call-update
  35.6 0.0 copy-done.2
  35.6 3.2 %collective-permute-start = (bf16[2,1,64,3072]{3,2,1,0:T(8,128)(2,1)S(1)}, bf16[2,1,64,3072]{3,2,1,0:T(8,128)(2,1)S(1)}, u32[]{:S(2)}, u32[]{:S(2)}) collective-permute-start(bf16[2,1,64,3072]{3,2,1,0:T(8,128)(2,1)S(1)} %copy-done.2), channel_id=1, source_target_pairs={{0,1},{1,0},{2,3},{3,2},{4,5},{5,4},{6,7},{7,6},{8,9},{9,8},{10,11... | collective-permute-start | bytes 2359304 | tf_op jit(solution)/shard_map/ppermute | solution.py:233
  38.8 0.6 pad_add_fusion.bounds_ref
  39.5 0.7 pad_add_fusion.1.bounds_ref
  40.1 0.1 constant_dynamic-update-slice_fusion.1
  40.2 23.6 %collective-permute-done = bf16[2,1,64,3072]{3,2,1,0:T(8,128)(2,1)S(1)} collective-permute-done((bf16[2,1,64,3072]{3,2,1,0:T(8,128)(2,1)S(1)}, bf16[2,1,64,3072]{3,2,1,0:T(8,128)(2,1)S(1)}, u32[]{:S(2)}, u32[]{:S(2)}) %collective-permute-start) | collective-permute-done | bytes 786464 | tf_op jit(solution)/shard_map/ppermute | solution.py:233
  63.7 0.1 constant_dynamic-update-slice_fusion
  63.8 1.3 slice_bitcast_fusion.5
  65.0 70.2 %all-gather.6.cloned.1.call-done = bf16[2,4,1024,1024]{3,2,1,0:T(8,128)(2,1)} async-done(((bf16[2,4,64,1024]{3,2,1,0:T(8,128)(2,1)}), bf16[2,4,1024,1024]{3,2,1,0:T(8,128)(2,1)}) %all-gather.6.cloned.1.call-update) | async-done | bytes 16777232 | tf_op jit(solution)/shard_map/all_gather | solution.py:237
  135.2 16.5 %shard_map.46 = (f32[4,1,768]{2,1,0:T(1,128)}, f32[4,1,768]{2,1,0:T(1,128)}, f32[4,768,128]{2,1,0:T(8,128)}, bf16[4,6,64,128]{3,2,1,0:T(8,128)(2,1)}) custom-call(s32[2]{0:T(128)} %pad_add_fusion.bounds_ref, bf16[128,3072]{1,0:T(8,128)(2,1)} %get-tuple-element.31.q_ref, bf16[2,64,64,1024]{3,2,1,0:T(8,128)(2,1)} %bitcast.126, bf16[2,64,64,1024]{3,2,1,0:T(8,128)(2,1)} %bitcast.127), custom_call_target="tpu_custom_call" | custom-call | flops 6442450944 | bytes 12320768 | tf_op jit(solution)/shard_map/pallas_call | solution.py:171
  151.7 0.0 copy-start.5
  151.7 0.0 copy-start.4
  151.7 0.0 copy-start.3
  151.7 69.2 %shard_map.47 = (f32[4,1,768]{2,1,0:T(1,128)}, f32[4,1,768]{2,1,0:T(1,128)}, f32[4,768,128]{2,1,0:T(8,128)}, bf16[4,6,64,128]{3,2,1,0:T(8,128)(2,1)}) custom-call(s32[4]{0:T(128)} %pad_add_fusion.1.bounds_ref, bf16[128,3072]{1,0:T(8,128)(2,1)} %get-tuple-element.32.q_ref, bf16[2,64,64,1024]{3,2,1,0:T(8,128)(2,1)} %bitcast.128, ...), custom_call_target="tpu_custom_call" | custom-call | flops 12884901888 | bytes 12320768 | tf_op jit(solution)/shard_map/pallas_call | solution.py:171
  220.9 0.7 reduce.1
  221.6 0.0 copy-done.5
  221.7 0.1 reshape.179
  221.8 0.0 copy-done.4
  221.8 0.7 reduce.3
  222.6 0.1 reshape.182
  222.7 0.1 reshape.181
  222.8 0.1 reshape.180
  222.9 0.0 copy-done.3
  222.9 0.0 copy-start.1
  223.0 1.2 pad_maximum_fusion
  224.1 0.0 copy-start
  224.2 2.0 collective-permute-start.2
  226.2 1.9 collective-permute-start.1
  228.1 18.7 %collective-permute-done.1 = f32[2,4,6,64,2]{3,2,1,4,0:T(8,128)S(1)} collective-permute-done((f32[2,4,6,64,2]{3,2,1,4,0:T(8,128)S(1)}, f32[2,4,6,64,2]{3,2,1,4,0:T(8,128)S(1)}, u32[]{:S(2)}, u32[]{:S(2)}) %collective-permute-start.1) | collective-permute-done | bytes 24608 | tf_op jit(solution)/shard_map/ppermute | solution.py:209
  246.8 0.0 collective-permute-done.2
  246.9 0.2 convert_element_type.9
  247.0 0.0 copy-done.1
  247.0 0.0 copy-done
  247.0 0.0 copy-start.6
  247.1 2.1 multiply_reduce_fusion.1
  249.2 0.0 copy-done.6
  249.2 1.5 fusion.6
  250.8 0.3 copy.20
  251.0 0.4 stack_reshape.6
  251.5 0.3 copy.24
  251.8 0.4 stack_reshape.7
  252.2 0.9 maximum_bitcast_fusion
  (12 shorter events, 0.2 us)
Async XLA Ops:
  6.5 29.1 %copy-start.2 = (bf16[2,1,64,3072]{3,2,1,0:T(8,128)(2,1)S(1)}, bf16[2,1,64,3072]{3,2,1,0:T(8,128)(2,1)}, u32[]{:S(2)}) copy-start(bf16[2,1,64,3072]{3,2,1,0:T(8,128)(2,1)} %param.4) | copy-start | bytes 2359300
  6.5 29.0 %all-gather.4.cloned.1.call-start = ((), (), s32[]{:S(2)}) async-start(), calls=%async_computation | async-start | bytes 1310720 | tf_op jit(solution)/shard_map/all_gather | solution.py:236
  8.3 126.9 %all-gather.6.cloned.1.call-start = ((), (), s32[]{:S(2)}) async-start(), calls=%async_computation.1 | async-start | bytes 17825792 | tf_op jit(solution)/shard_map/all_gather | solution.py:237
  35.6 28.1 %collective-permute-start = (bf16[2,1,64,3072]{3,2,1,0:T(8,128)(2,1)S(1)}, bf16[2,1,64,3072]{3,2,1,0:T(8,128)(2,1)S(1)}, u32[]{:S(2)}, u32[]{:S(2)}) collective-permute-start(bf16[2,1,64,3072]{3,2,1,0:T(8,128)(2,1)S(1)} %copy-done.2), channel_id=1, source_target_pairs={{0,1},{1,0},{2,3},{3,2},{4,5},{5,4},{6,7},{7,6},{8,9},{9,8},{10,11... | collective-permute-start | bytes 2359304 | tf_op jit(solution)/shard_map/ppermute | solution.py:233
  151.7 70.0 %copy-start.5 = (f32[4,1,768]{2,1,0:T(1,128)S(1)}, f32[4,1,768]{2,1,0:T(1,128)}, u32[]{:S(2)}) copy-start(f32[4,1,768]{2,1,0:T(1,128)} %get-tuple-element.14) | copy-start | bytes 36868
  151.7 70.1 %copy-start.4 = (f32[4,1,768]{2,1,0:T(1,128)S(1)}, f32[4,1,768]{2,1,0:T(1,128)}, u32[]{:S(2)}) copy-start(f32[4,1,768]{2,1,0:T(1,128)} %get-tuple-element.16) | copy-start | bytes 36868
  151.7 71.3 %copy-start.3 = (bf16[4,6,64,128]{3,2,1,0:T(8,128)(2,1)S(1)}, bf16[4,6,64,128]{3,2,1,0:T(8,128)(2,1)}, u32[]{:S(2)}) copy-start(bf16[4,6,64,128]{3,2,1,0:T(8,128)(2,1)} %get-tuple-element.18) | copy-start | bytes 1179652
  222.9 24.1 %copy-start.1 = (f32[4,768,128]{2,1,0:T(8,128)S(1)}, f32[4,768,128]{2,1,0:T(8,128)}, u32[]{:S(2)}) copy-start(f32[4,768,128]{2,1,0:T(8,128)} %get-tuple-element.20) | copy-start | bytes 4718596
  224.1 22.9 %copy-start = (f32[4,768,128]{2,1,0:T(8,128)S(1)}, f32[4,768,128]{2,1,0:T(8,128)}, u32[]{:S(2)}) copy-start(f32[4,768,128]{2,1,0:T(8,128)} %get-tuple-element.13) | copy-start | bytes 4718596
  224.2 22.7 %collective-permute-start.2 = (bf16[2,4,6,64,128]{4,3,2,1,0:T(8,128)(2,1)S(1)}, bf16[2,4,6,64,128]{4,3,2,1,0:T(8,128)(2,1)S(1)}, u32[]{:S(2)}, u32[]{:S(2)}) collective-permute-start(bf16[2,4,6,64,128]{4,3,2,1,0:T(8,128)(2,1)S(1)} %pad_maximum_fusion), channel_id=1, source_target_pairs={{0,1},{1,0},{2,3},{3,2},{4,5},{5,4},{6,7},{7,6},{8,9},{9,8},{10,11... | collective-permute-start | bytes 2359304 | tf_op jit(solution)/shard_map/ppermute | solution.py:208
  226.2 20.6 %collective-permute-start.1 = (f32[2,4,6,64,2]{3,2,1,4,0:T(8,128)S(1)}, f32[2,4,6,64,2]{3,2,1,4,0:T(8,128)S(1)}, u32[]{:S(2)}, u32[]{:S(2)}) collective-permute-start(f32[2,4,6,64,2]{3,2,1,4,0:T(8,128)S(1)} %maximum_maximum_fusion), channel_id=1, source_target_pairs={{0,1},{1,0},{2,3},{3,2},{4,5},{5,4},{6,7},{7,6},{8,9},{9,8},{10,11... | collective-permute-start | bytes 73736 | tf_op jit(solution)/shard_map/ppermute | solution.py:209
  247.0 2.1 copy-start.6
Sparse Core Ops, SparseCore 0:
  9.0 26.5 all-gather.3
  37.2 97.9 all-gather.5
